TPU v7x, 32 devices: a whole 2x2x4 slice. The times are simulated.
32 devices in a mesh: seq: 16 (over z, y, x), head: 2 (over core).
Axes of the slice: x: 2, y: 2, z: 4, core: 2. Of those that a mesh axis runs over, the one named last changes fastest.
Arguments:
- query_raw: bfloat16 [4096, 8, 128], P('seq', 'head'), may hold values from -6 to 6
- key_raw: bfloat16 [4096, 8, 128], P('seq', 'head'), may hold values from -6 to 6
- value_raw: bfloat16 [4096, 8, 128], P('seq', 'head'), may hold values from -6 to 6
- out_gain: float32 [8, 128], P('head'), may hold values from 0.5 to 1.5
- out_grad: bfloat16 [4096, 8, 128], P('seq', 'head'), may hold values from -6 to 6
Outputs:
- normed_out: bfloat16 [4096, 8, 128], P('seq', 'head')
- query_grad: bfloat16 [4096, 8, 128], P('seq', 'head')
- key_grad: bfloat16 [4096, 8, 128], P('seq', 'head')
- value_grad: bfloat16 [4096, 8, 128], P('seq', 'head')
All inputs are finite; a program needn't handle non-finite values.
Results may differ from a plain program's by a relative error of at most 0.0065.
Values sent between devices are 32-bit elements; how exact they have to be, the bound alone decides.
No kernel may reach another device: no remote copies, remote signals or barrier semaphores. Data moves between devices by JAX's collectives and lax.ppermute only.
A program may use at most 64 MiB of HBM per device.

v0:
```python
import jax
import jax.numpy as jnp
from jax import lax
from jax.sharding import PartitionSpec as P

GROUP = 256


def from_behind(shard, axis, by):
    count = lax.axis_size(axis)
    pairs = [(i, i + by) for i in range(count) if 0 <= i + by < count]
    return lax.ppermute(shard, axis, pairs)


def silu_grad(raw):
    sigma = jax.nn.sigmoid(raw)
    return sigma * (1.0 + raw * (1.0 - sigma))


def causal_mask(length):
    rows = lax.broadcasted_iota(jnp.int32, (length, length), 0)
    cols = lax.broadcasted_iota(jnp.int32, (length, length), 1)
    return cols <= rows


def lower_sum(own_total):
    inclusive = own_total
    stride = 1
    while stride < lax.axis_size("seq"):
        inclusive = inclusive + from_behind(inclusive, "seq", stride)
        stride = stride * 2
    return inclusive - own_total


def upper_sum(own_total):
    inclusive = own_total
    stride = 1
    while stride < lax.axis_size("seq"):
        inclusive = inclusive + from_behind(inclusive, "seq", -stride)
        stride = stride * 2
    return inclusive - own_total


def body(query_raw, key_raw, value_raw, out_gain, out_grad):
    tok_rows, head_count, width = query_raw.shape
    blocks = tok_rows // GROUP
    blocked = (blocks, GROUP, head_count, width)
    query_act = jax.nn.silu(query_raw.astype(jnp.float32)).astype(jnp.bfloat16).reshape(blocked)
    key_act = jax.nn.silu(key_raw.astype(jnp.float32)).astype(jnp.bfloat16).reshape(blocked)
    value_blk = value_raw.reshape(blocked)
    mask = causal_mask(GROUP)[None, None]
    block_kv = jnp.einsum("cshd,cshe->chde", key_act, value_blk, preferred_element_type=jnp.float32)
    own_total = jnp.sum(block_kv, axis=0)
    before = lower_sum(own_total)
    state_b = (before[None] + (jnp.cumsum(block_kv, axis=0) - block_kv)).astype(jnp.bfloat16)
    scores = jnp.einsum("cthd,cshd->chts", query_act, key_act, preferred_element_type=jnp.float32)
    attn = jnp.where(mask, scores, 0.0).astype(jnp.bfloat16)
    mixed = jnp.einsum("chts,cshe->cthe", attn, value_blk, preferred_element_type=jnp.float32)
    mixed = mixed + jnp.einsum(
        "cthd,chde->cthe", query_act, state_b, preferred_element_type=jnp.float32
    )
    mixed = mixed.reshape(tok_rows, head_count, width)
    grad_in = out_grad.astype(jnp.float32) * out_gain
    sq_part = jnp.sum(mixed * mixed, axis=(1, 2))
    cross_part = jnp.sum(grad_in * mixed, axis=(1, 2))
    sq_total, cross_total = lax.psum((sq_part, cross_part), "head")
    features = head_count * width * lax.axis_size("head")
    inv_rms = lax.rsqrt(sq_total / features + 1e-06)
    normed_out = (mixed * inv_rms[:, None, None] * out_gain).astype(jnp.bfloat16)
    delta = (
        grad_in * inv_rms[:, None, None]
        - mixed * (cross_total * inv_rms**3 / features)[:, None, None]
    ).astype(jnp.bfloat16)
    delta_blk = delta.reshape(blocked)
    block_grad = jnp.einsum(
        "cthd,cthe->chde", query_act, delta_blk, preferred_element_type=jnp.float32
    )
    own_grad = jnp.sum(block_grad, axis=0)
    after = upper_sum(own_grad)
    local_after = jnp.flip(jnp.cumsum(jnp.flip(block_grad, 0), axis=0), 0) - block_grad
    grad_state = (after[None] + local_after).astype(jnp.bfloat16)
    bscore = jnp.einsum("cthe,cshe->chts", delta_blk, value_blk, preferred_element_type=jnp.float32)
    bscore = jnp.where(mask, bscore, 0.0).astype(jnp.bfloat16)
    dquery = jnp.einsum("chts,cshd->cthd", bscore, key_act, preferred_element_type=jnp.float32)
    dquery = dquery + jnp.einsum(
        "cthe,chde->cthd", delta_blk, state_b, preferred_element_type=jnp.float32
    )
    dkey = jnp.einsum("chts,cthd->cshd", bscore, query_act, preferred_element_type=jnp.float32)
    dkey = dkey + jnp.einsum(
        "cshe,chde->cshd", value_blk, grad_state, preferred_element_type=jnp.float32
    )
    dvalue = jnp.einsum("chts,cthe->cshe", attn, delta_blk, preferred_element_type=jnp.float32)
    dvalue = dvalue + jnp.einsum(
        "cshd,chde->cshe", key_act, grad_state, preferred_element_type=jnp.float32
    )
    whole = (tok_rows, head_count, width)
    query_grad = (dquery.reshape(whole) * silu_grad(query_raw.astype(jnp.float32))).astype(
        jnp.bfloat16
    )
    key_grad = (dkey.reshape(whole) * silu_grad(key_raw.astype(jnp.float32))).astype(jnp.bfloat16)
    value_grad = dvalue.reshape(whole).astype(jnp.bfloat16)
    return (normed_out, query_grad, key_grad, value_grad)


def solution(mesh):
    in_specs = (
        P("seq", "head", None),
        P("seq", "head", None),
        P("seq", "head", None),
        P("head", None),
        P("seq", "head", None),
    )
    out_specs = (
        P("seq", "head", None),
        P("seq", "head", None),
        P("seq", "head", None),
        P("seq", "head", None),
    )
    return jax.shard_map(body, mesh=mesh, in_specs=in_specs, out_specs=out_specs, check_vma=False)
```

profile of v0, /device:TPU:0, one launch (start us, length us, event | category | flops | bytes accessed | tf_op | source)
XLA Modules:
  0.0 94.8 jit_solution(10915825543777581510)
XLA Ops:
  0.6 1.1 %copy.10 = bf16[256,4,128]{0,2,1:T(8,128)(2,1)S(1)} copy(bf16[256,4,128]{2,1,0:T(4,128)(2,1)} %param.6) | data formatting | bytes 524288 | tf_op args[1]
  2.1 4.9 %collective-permute-start = (f32[4,128,128]{2,1,0:T(8,128)S(1)}, f32[4,128,128]{2,1,0:T(8,128)S(1)}, u32[]{:S(2)}, u32[]{:S(2)}) collective-permute-start(f32[4,128,128]{2,1,0:T(8,128)S(1)} %fusion.26), channel_id=1, source_target_pairs={{0,2},{2,4},{4,6},{6,8},{8,10},{10,12},{12,14},{14,16},{16,18},{18... | collective-permute-start | bytes 786440 | tf_op jit(solution)/shard_map/ppermute | solution.py:12
  7.0 5.5 %collective-permute-done = f32[4,128,128]{2,1,0:T(8,128)S(1)} collective-permute-done((f32[4,128,128]{2,1,0:T(8,128)S(1)}, f32[4,128,128]{2,1,0:T(8,128)S(1)}, u32[]{:S(2)}, u32[]{:S(2)}) %collective-permute-start) | collective-permute-done | bytes 262176 | tf_op jit(solution)/shard_map/ppermute | solution.py:12
  12.5 5.5 %collective-permute-start.1 = (f32[4,128,128]{2,1,0:T(8,128)S(1)}, f32[4,128,128]{2,1,0:T(8,128)S(1)}, u32[]{:S(2)}, u32[]{:S(2)}) collective-permute-start(f32[4,128,128]{2,1,0:T(8,128)S(1)} %add.95), channel_id=1, source_target_pairs={{0,4},{2,6},{4,8},{6,10},{8,12},{10,14},{12,16},{14,18},{16,20},{1... | collective-permute-start | bytes 786440 | tf_op jit(solution)/shard_map/ppermute | solution.py:12
  18.0 4.7 %collective-permute-done.1 = f32[4,128,128]{2,1,0:T(8,128)S(1)} collective-permute-done((f32[4,128,128]{2,1,0:T(8,128)S(1)}, f32[4,128,128]{2,1,0:T(8,128)S(1)}, u32[]{:S(2)}, u32[]{:S(2)}) %collective-permute-start.1) | collective-permute-done | bytes 262176 | tf_op jit(solution)/shard_map/ppermute | solution.py:12
  22.7 6.3 %collective-permute-start.2 = (f32[4,128,128]{2,1,0:T(8,128)S(1)}, f32[4,128,128]{2,1,0:T(8,128)S(1)}, u32[]{:S(2)}, u32[]{:S(2)}) collective-permute-start(f32[4,128,128]{2,1,0:T(8,128)S(1)} %add.96), channel_id=1, source_target_pairs={{0,8},{2,10},{4,12},{6,14},{8,16},{10,18},{12,20},{14,22},{16,24},... | collective-permute-start | bytes 786440 | tf_op jit(solution)/shard_map/ppermute | solution.py:12
  29.2 3.6 %collective-permute-done.2 = f32[4,128,128]{2,1,0:T(8,128)S(1)} collective-permute-done((f32[4,128,128]{2,1,0:T(8,128)S(1)}, f32[4,128,128]{2,1,0:T(8,128)S(1)}, u32[]{:S(2)}, u32[]{:S(2)}) %collective-permute-start.2) | collective-permute-done | bytes 262176 | tf_op jit(solution)/shard_map/ppermute | solution.py:12
  32.9 5.5 %collective-permute-start.3 = (f32[4,128,128]{2,1,0:T(8,128)S(1)}, f32[4,128,128]{2,1,0:T(8,128)S(1)}, u32[]{:S(2)}, u32[]{:S(2)}) collective-permute-start(f32[4,128,128]{2,1,0:T(8,128)S(1)} %add.97), channel_id=1, source_target_pairs={{0,16},{2,18},{4,20},{6,22},{8,24},{10,26},{12,28},{14,30},{1,17},... | collective-permute-start | bytes 786440 | tf_op jit(solution)/shard_map/ppermute | solution.py:12
  38.4 0.5 fusion
  39.4 2.9 %collective-permute-done.3 = f32[4,128,128]{2,1,0:T(8,128)S(1)} collective-permute-done((f32[4,128,128]{2,1,0:T(8,128)S(1)}, f32[4,128,128]{2,1,0:T(8,128)S(1)}, u32[]{:S(2)}, u32[]{:S(2)}) %collective-permute-start.3) | collective-permute-done | bytes 262176 | tf_op jit(solution)/shard_map/ppermute | solution.py:12
  42.7 2.5 %all-reduce = (f32[256]{0:T(256)S(1)}, f32[256]{0:T(256)S(1)}) all-reduce(f32[256]{0:T(256)S(1)} %get-tuple-element.9, f32[256]{0:T(256)S(1)} %get-tuple-element.8), channel_id=1, replica_groups=mesh['seq'=16,'head'=2] {'head'}, use_global_device_ids=true, to_apply=%region_1.2 | all-reduce | flops 512 | bytes 4096 | tf_op jit(solution)/shard_map/psum | solution.py:66
  45.6 1.3 %collective-permute-start.4 = (f32[4,128,128]{2,1,0:T(8,128)S(1)}, f32[4,128,128]{2,1,0:T(8,128)S(1)}, u32[]{:S(2)}, u32[]{:S(2)}) collective-permute-start(f32[4,128,128]{2,1,0:T(8,128)S(1)} %fusion.35), channel_id=1, source_target_pairs={{2,0},{4,2},{6,4},{8,6},{10,8},{12,10},{14,12},{16,14},{18,16},{20... | collective-permute-start | bytes 786440 | tf_op jit(solution)/shard_map/ppermute | solution.py:12
  46.9 9.0 %collective-permute-done.4 = f32[4,128,128]{2,1,0:T(8,128)S(1)} collective-permute-done((f32[4,128,128]{2,1,0:T(8,128)S(1)}, f32[4,128,128]{2,1,0:T(8,128)S(1)}, u32[]{:S(2)}, u32[]{:S(2)}) %collective-permute-start.4) | collective-permute-done | bytes 262176 | tf_op jit(solution)/shard_map/ppermute | solution.py:12
  56.0 1.3 %collective-permute-start.5 = (f32[4,128,128]{2,1,0:T(8,128)S(1)}, f32[4,128,128]{2,1,0:T(8,128)S(1)}, u32[]{:S(2)}, u32[]{:S(2)}) collective-permute-start(f32[4,128,128]{2,1,0:T(8,128)S(1)} %add.109), channel_id=1, source_target_pairs={{4,0},{6,2},{8,4},{10,6},{12,8},{14,10},{16,12},{18,14},{20,16},{2... | collective-permute-start | bytes 786440 | tf_op jit(solution)/shard_map/ppermute | solution.py:12
  57.3 0.3 fusion.1
  57.6 7.8 %collective-permute-done.5 = f32[4,128,128]{2,1,0:T(8,128)S(1)} collective-permute-done((f32[4,128,128]{2,1,0:T(8,128)S(1)}, f32[4,128,128]{2,1,0:T(8,128)S(1)}, u32[]{:S(2)}, u32[]{:S(2)}) %collective-permute-start.5) | collective-permute-done | bytes 262176 | tf_op jit(solution)/shard_map/ppermute | solution.py:12
  65.4 1.3 %collective-permute-start.6 = (f32[4,128,128]{2,1,0:T(8,128)S(1)}, f32[4,128,128]{2,1,0:T(8,128)S(1)}, u32[]{:S(2)}, u32[]{:S(2)}) collective-permute-start(f32[4,128,128]{2,1,0:T(8,128)S(1)} %add.110), channel_id=1, source_target_pairs={{8,0},{10,2},{12,4},{14,6},{16,8},{18,10},{20,12},{22,14},{24,16},... | collective-permute-start | bytes 786440 | tf_op jit(solution)/shard_map/ppermute | solution.py:12
  67.4 10.6 %collective-permute-done.6 = f32[4,128,128]{2,1,0:T(8,128)S(1)} collective-permute-done((f32[4,128,128]{2,1,0:T(8,128)S(1)}, f32[4,128,128]{2,1,0:T(8,128)S(1)}, u32[]{:S(2)}, u32[]{:S(2)}) %collective-permute-start.6) | collective-permute-done | bytes 262176 | tf_op jit(solution)/shard_map/ppermute | solution.py:12
  78.0 1.3 %collective-permute-start.7 = (f32[4,128,128]{2,1,0:T(8,128)S(1)}, f32[4,128,128]{2,1,0:T(8,128)S(1)}, u32[]{:S(2)}, u32[]{:S(2)}) collective-permute-start(f32[4,128,128]{2,1,0:T(8,128)S(1)} %add.111), channel_id=1, source_target_pairs={{16,0},{18,2},{20,4},{22,6},{24,8},{26,10},{28,12},{30,14},{17,1},... | collective-permute-start | bytes 786440 | tf_op jit(solution)/shard_map/ppermute | solution.py:12
  79.6 0.9 copy.25
  80.4 0.9 copy.26
  81.6 10.8 %collective-permute-done.7 = f32[4,128,128]{2,1,0:T(8,128)S(1)} collective-permute-done((f32[4,128,128]{2,1,0:T(8,128)S(1)}, f32[4,128,128]{2,1,0:T(8,128)S(1)}, u32[]{:S(2)}, u32[]{:S(2)}) %collective-permute-start.7) | collective-permute-done | bytes 262176 | tf_op jit(solution)/shard_map/ppermute | solution.py:12
  92.8 0.9 copy.28
  94.0 0.9 copy.27
  (35 shorter events, 3.8 us)
Async XLA Ops:
  0.6 1.2 %copy-start = (bf16[256,4,128]{2,1,0:T(4,128)(2,1)S(1)}, bf16[256,4,128]{2,1,0:T(4,128)(2,1)}, u32[]{:S(2)}) copy-start(bf16[256,4,128]{2,1,0:T(4,128)(2,1)} %param.7) | copy-start | bytes 786436
  2.1 10.4 %collective-permute-start = (f32[4,128,128]{2,1,0:T(8,128)S(1)}, f32[4,128,128]{2,1,0:T(8,128)S(1)}, u32[]{:S(2)}, u32[]{:S(2)}) collective-permute-start(f32[4,128,128]{2,1,0:T(8,128)S(1)} %fusion.26), channel_id=1, source_target_pairs={{0,2},{2,4},{4,6},{6,8},{8,10},{10,12},{12,14},{14,16},{16,18},{18... | collective-permute-start | bytes 786440 | tf_op jit(solution)/shard_map/ppermute | solution.py:12
  12.5 16.4 %copy-start.1 = (bf16[256,4,128]{2,1,0:T(4,128)(2,1)S(1)}, bf16[256,4,128]{2,1,0:T(4,128)(2,1)}, u32[]{:S(2)}) copy-start(bf16[256,4,128]{2,1,0:T(4,128)(2,1)} %param.5) | copy-start | bytes 786436
  12.5 10.1 %collective-permute-start.1 = (f32[4,128,128]{2,1,0:T(8,128)S(1)}, f32[4,128,128]{2,1,0:T(8,128)S(1)}, u32[]{:S(2)}, u32[]{:S(2)}) collective-permute-start(f32[4,128,128]{2,1,0:T(8,128)S(1)} %add.95), channel_id=1, source_target_pairs={{0,4},{2,6},{4,8},{6,10},{8,12},{10,14},{12,16},{14,18},{16,20},{1... | collective-permute-start | bytes 786440 | tf_op jit(solution)/shard_map/ppermute | solution.py:12
  22.7 10.1 %collective-permute-start.2 = (f32[4,128,128]{2,1,0:T(8,128)S(1)}, f32[4,128,128]{2,1,0:T(8,128)S(1)}, u32[]{:S(2)}, u32[]{:S(2)}) collective-permute-start(f32[4,128,128]{2,1,0:T(8,128)S(1)} %add.96), channel_id=1, source_target_pairs={{0,8},{2,10},{4,12},{6,14},{8,16},{10,18},{12,20},{14,22},{16,24},... | collective-permute-start | bytes 786440 | tf_op jit(solution)/shard_map/ppermute | solution.py:12
  32.9 6.1 %copy-start.2 = (bf16[256,4,128]{2,1,0:T(4,128)(2,1)S(1)}, bf16[256,4,128]{2,1,0:T(4,128)(2,1)}, u32[]{:S(2)}) copy-start(bf16[256,4,128]{2,1,0:T(4,128)(2,1)} %param.9) | copy-start | bytes 786436
  32.9 9.5 %collective-permute-start.3 = (f32[4,128,128]{2,1,0:T(8,128)S(1)}, f32[4,128,128]{2,1,0:T(8,128)S(1)}, u32[]{:S(2)}, u32[]{:S(2)}) collective-permute-start(f32[4,128,128]{2,1,0:T(8,128)S(1)} %add.97), channel_id=1, source_target_pairs={{0,16},{2,18},{4,20},{6,22},{8,24},{10,26},{12,28},{14,30},{1,17},... | collective-permute-start | bytes 786440 | tf_op jit(solution)/shard_map/ppermute | solution.py:12
  39.4 2.9 %copy-start.3 = (f32[4,128]{1,0:T(4,128)S(1)}, f32[4,128]{1,0:T(4,128)}, u32[]{:S(2)}) copy-start(f32[4,128]{1,0:T(4,128)} %param.8) | copy-start | bytes 6148
  45.6 10.3 %collective-permute-start.4 = (f32[4,128,128]{2,1,0:T(8,128)S(1)}, f32[4,128,128]{2,1,0:T(8,128)S(1)}, u32[]{:S(2)}, u32[]{:S(2)}) collective-permute-start(f32[4,128,128]{2,1,0:T(8,128)S(1)} %fusion.35), channel_id=1, source_target_pairs={{2,0},{4,2},{6,4},{8,6},{10,8},{12,10},{14,12},{16,14},{18,16},{20... | collective-permute-start | bytes 786440 | tf_op jit(solution)/shard_map/ppermute | solution.py:12
  56.0 9.4 %collective-permute-start.5 = (f32[4,128,128]{2,1,0:T(8,128)S(1)}, f32[4,128,128]{2,1,0:T(8,128)S(1)}, u32[]{:S(2)}, u32[]{:S(2)}) collective-permute-start(f32[4,128,128]{2,1,0:T(8,128)S(1)} %add.109), channel_id=1, source_target_pairs={{4,0},{6,2},{8,4},{10,6},{12,8},{14,10},{16,12},{18,14},{20,16},{2... | collective-permute-start | bytes 786440 | tf_op jit(solution)/shard_map/ppermute | solution.py:12
  57.6 9.4 %copy-start.4 = (bf16[4,256,256]{2,1,0:T(8,128)(2,1)}, bf16[4,256,256]{2,1,0:T(8,128)(2,1)S(1)}, u32[]{:S(2)}) copy-start(bf16[4,256,256]{2,1,0:T(8,128)(2,1)S(1)} %fusion.1) | copy-start | bytes 1572868
  65.4 12.5 %collective-permute-start.6 = (f32[4,128,128]{2,1,0:T(8,128)S(1)}, f32[4,128,128]{2,1,0:T(8,128)S(1)}, u32[]{:S(2)}, u32[]{:S(2)}) collective-permute-start(f32[4,128,128]{2,1,0:T(8,128)S(1)} %add.110), channel_id=1, source_target_pairs={{8,0},{10,2},{12,4},{14,6},{16,8},{18,10},{20,12},{22,14},{24,16},... | collective-permute-start | bytes 786440 | tf_op jit(solution)/shard_map/ppermute | solution.py:12
  78.0 14.4 %collective-permute-start.7 = (f32[4,128,128]{2,1,0:T(8,128)S(1)}, f32[4,128,128]{2,1,0:T(8,128)S(1)}, u32[]{:S(2)}, u32[]{:S(2)}) collective-permute-start(f32[4,128,128]{2,1,0:T(8,128)S(1)} %add.111), channel_id=1, source_target_pairs={{16,0},{18,2},{20,4},{22,6},{24,8},{26,10},{28,12},{30,14},{17,1},... | collective-permute-start | bytes 786440 | tf_op jit(solution)/shard_map/ppermute | solution.py:12
  79.5 1.7 %copy-start.5 = (bf16[4,256,256]{2,1,0:T(8,128)(2,1)S(1)}, bf16[4,256,256]{2,1,0:T(8,128)(2,1)}, u32[]{:S(2)}) copy-start(bf16[4,256,256]{2,1,0:T(8,128)(2,1)} %copy-done.4) | copy-start | bytes 1572868
where the time goes:
time: 95.4 us; the launch traced here: 94.8 us
  waiting for transfers between devices  54.9 us (58%)
  starting transfers between devices  27.3 us (29%)
  local copies, waits for them, and re-layouts  5 us (5%)
  matrix products  3.8 us (4%)
  blocking collectives  2.47 us (3%)
    ppermute x8, waiting for transfers between devices, from_behind(): return lax.ppermute(shard, axis, pairs)  54.9 us
    ppermute x8, starting transfers between devices, from_behind(): return lax.ppermute(shard, axis, pairs)  27.3 us
    unnamed x19, local copies, waits for them, and re-layouts  5 us
    psum x1, blocking collectives, body(): sq_total, cross_total = lax.psum((sq_part, cross_part), 'head')  2.47 us
  transfers between devices with their start and end apart: 8, of which 8 were waited for; matrix products, arithmetic and copies ran while one was open for 5% of the time, Pallas kernels for 0%

commit v1 on v0

--- a/solution.py
+++ b/solution.py
@@ -23,22 +23,29 @@
     return cols <= rows
 
 
+def exclusive_scan(own_total, reverse):
+    count = lax.axis_size("seq")
+    flat = own_total.reshape(-1)
+    size = flat.shape[0]
+    chunk = -(-size // count)
+    flat = jnp.pad(flat, (0, chunk * count - size))
+    gathered = lax.all_to_all(flat.reshape(count, chunk), "seq", 0, 0, tiled=True)
+    zero = jnp.zeros((1, chunk), gathered.dtype)
+    if reverse:
+        later = jnp.flip(jnp.cumsum(jnp.flip(gathered[1:], 0), axis=0), 0)
+        prefix = jnp.concatenate([later, zero], axis=0)
+    else:
+        prefix = jnp.concatenate([zero, jnp.cumsum(gathered[:-1], axis=0)], axis=0)
+    spread = lax.all_to_all(prefix, "seq", 0, 0, tiled=True)
+    return spread.reshape(-1)[:size].reshape(own_total.shape)
+
+
 def lower_sum(own_total):
-    inclusive = own_total
-    stride = 1
-    while stride < lax.axis_size("seq"):
-        inclusive = inclusive + from_behind(inclusive, "seq", stride)
-        stride = stride * 2
-    return inclusive - own_total
+    return exclusive_scan(own_total, False)
 
 
 def upper_sum(own_total):
-    inclusive = own_total
-    stride = 1
-    while stride < lax.axis_size("seq"):
-        inclusive = inclusive + from_behind(inclusive, "seq", -stride)
-        stride = stride * 2
-    return inclusive - own_total
+    return exclusive_scan(own_total, True)
 
 
 def body(query_raw, key_raw, value_raw, out_gain, out_grad):

time: 95.4 us -> 75.6 us (0.79)
  waiting for transfers between devices: 54.9 us -> 34.1 us
  starting transfers between devices: 27.3 us -> 19.1 us
  local copies, waits for them, and re-layouts: 5 us -> 9.75 us
  matrix products: 3.8 us -> 6.02 us
  other arithmetic: 0.52 us -> 2.65 us
    ppermute x8 -> x0, waiting for transfers between devices: 54.9 us -> none  [from_behind(): return lax.ppermute(shard, axis, pairs)]
    all_to_all x0 -> x4, waiting for transfers between devices: none -> 34.1 us  [the longest x2 17.6 us: exclusive_scan(): lax.all_to_all(flat.reshape(count, chunk), 'seq', 0, 0, tiled=True)]
    ppermute x8 -> x0, starting transfers between devices: 27.3 us -> none  [from_behind(): return lax.ppermute(shard, axis, pairs)]
    all_to_all x0 -> x4, starting transfers between devices: none -> 19.1 us  [the longest x2 12 us: exclusive_scan(): lax.all_to_all(flat.reshape(count, chunk), 'seq', 0, 0, tiled=True)]
    all_to_all x0 -> x4, local copies, waits for them, and re-layouts: none -> 1.99 us  [exclusive_scan(): spread = lax.all_to_all(prefix, 'seq', 0, 0, tiled=True)]
    rev x0 -> x2, local copies, waits for them, and re-layouts: none -> 1.52 us  [exclusive_scan(): later = jnp.flip(jnp.cumsum(jnp.flip(gathered[1:], 0), axis=0), 0)]
    unnamed x19, local copies, waits for them, and re-layouts: 5 us -> 6.21 us
  transfers between devices with their start and end apart: 8 -> 4, of which waited for: 8 -> 4; matrix products, arithmetic and copies ran while one was open for 5% -> 5% of each run, Pallas kernels for 0% -> 0%
where the time goes in v1:
time: 75.6 us; the launch traced here: 74.9 us
  waiting for transfers between devices  34.1 us (45%)
  starting transfers between devices  19.1 us (25%)
  local copies, waits for them, and re-layouts  9.75 us (13%)
  matrix products  6.02 us (8%)
  other arithmetic  2.65 us (4%)
  blocking collectives  2.47 us (3%)
  between operations  0.87 us (1%)
    all_to_all x2, waiting for transfers between devices, exclusive_scan(): lax.all_to_all(flat.reshape(count, chunk), 'seq', 0, 0, tiled=True)  17.6 us
    all_to_all x2, waiting for transfers between devices, exclusive_scan(): spread = lax.all_to_all(prefix, 'seq', 0, 0, tiled=True)  16.5 us
    all_to_all x2, starting transfers between devices, exclusive_scan(): lax.all_to_all(flat.reshape(count, chunk), 'seq', 0, 0, tiled=True)  12 us
    all_to_all x2, starting transfers between devices, exclusive_scan(): spread = lax.all_to_all(prefix, 'seq', 0, 0, tiled=True)  7.08 us
    unnamed x19, local copies, waits for them, and re-layouts  6.21 us
    psum x1, blocking collectives, body(): sq_total, cross_total = lax.psum((sq_part, cross_part), 'head')  2.47 us
    all_to_all x4, local copies, waits for them, and re-layouts, exclusive_scan(): spread = lax.all_to_all(prefix, 'seq', 0, 0, tiled=True)  1.99 us
    rev x2, local copies, waits for them, and re-layouts, exclusive_scan(): later = jnp.flip(jnp.cumsum(jnp.flip(gathered[1:], 0), axis=0), 0)  1.52 us
  transfers between devices with their start and end apart: 4, of which 4 were waited for; matrix products, arithmetic and copies ran while one was open for 5% of the time, Pallas kernels for 0%

profile of v1, /device:TPU:0, one launch (start us, length us, event | category | flops | bytes accessed | tf_op | source)
XLA Modules:
  0.0 74.9 jit_solution(295471247522717399)
XLA Ops:
  0.6 1.1 %copy.30 = bf16[256,4,128]{0,2,1:T(8,128)(2,1)S(1)} copy(bf16[256,4,128]{2,1,0:T(4,128)(2,1)} %param.6) | data formatting | bytes 524288 | tf_op args[1]
  1.8 1.0 %fusion.28 = f32[4,128,128]{2,1,0:T(8,128)} fusion(bf16[256,4,128]{2,1,0:T(4,128)(2,1)S(1)} %copy-done, bf16[256,4,128]{0,2,1:T(8,128)(2,1)S(1)} %copy.30), kind=kOutput, calls=%fused_computation.53 | convolution fusion | flops 34340864 | bytes 786432 | tf_op jit(solution)/shard_map/cshd,cshe->chde/dot_general | solution.py:59
  2.8 8.4 %all-to-all-start = ((f32[16,1,4096]{2,1,0:T(1,128)}), f32[16,1,4096]{2,1,0:T(1,128)S(1)}, u32[]{:S(2)}, u32[]{:S(2)}) async-start(f32[16,1,4096]{2,1,0:T(1,128)} %bitcast.1), calls=%async_computation | async-start | bytes 524288 | tf_op jit(solution)/shard_map/all_to_all | solution.py:32
  11.4 0.8 %copy-done.2 = bf16[256,4,128]{2,1,0:T(4,128)(2,1)S(1)} copy-done((bf16[256,4,128]{2,1,0:T(4,128)(2,1)S(1)}, bf16[256,4,128]{2,1,0:T(4,128)(2,1)}, u32[]{:S(2)}) %copy-start.2) | copy-done | bytes 262168
  12.4 8.7 %all-to-all-done = f32[16,1,4096]{2,1,0:T(1,128)S(1)} async-done(((f32[16,1,4096]{2,1,0:T(1,128)}), f32[16,1,4096]{2,1,0:T(1,128)S(1)}, u32[]{:S(2)}, u32[]{:S(2)}) %all-to-all-start) | async-done | bytes 262176 | tf_op jit(solution)/shard_map/all_to_all | solution.py:32
  21.5 1.0 %copy.36 = f32[16,1,4096]{2,1,0:T(1,128)} copy(f32[16,1,4096]{2,0,1:T(8,128)S(1)} %pad_bitcast_fusion.1) | data formatting | bytes 524288 | tf_op jit(solution)/shard_map/all_to_all | solution.py:39
  22.5 3.5 %all-to-all-start.1 = ((f32[16,1,4096]{2,1,0:T(1,128)}), f32[16,1,4096]{2,1,0:T(1,128)S(1)}, u32[]{:S(2)}, u32[]{:S(2)}) async-start(f32[16,1,4096]{2,1,0:T(1,128)} %copy.36), calls=%async_computation.1 | async-start | bytes 524288 | tf_op jit(solution)/shard_map/all_to_all | solution.py:39
  26.9 8.4 %all-to-all-done.1 = f32[16,1,4096]{2,1,0:T(1,128)S(1)} async-done(((f32[16,1,4096]{2,1,0:T(1,128)}), f32[16,1,4096]{2,1,0:T(1,128)S(1)}, u32[]{:S(2)}, u32[]{:S(2)}) %all-to-all-start.1) | async-done | bytes 262176 | tf_op jit(solution)/shard_map/all_to_all | solution.py:39
  35.3 1.0 %fusion.24 = bf16[4,128,128]{2,1,0:T(8,128)(2,1)S(1)} fusion(f32[4,128,128]{2,1,0:T(8,128)} %fusion.28, f32[4,128,128]{2,1,0:T(8,128)S(1)} %bitcast.70), kind=kLoop, calls=%fused_computation.46 | loop fusion | flops 196608 | bytes 655360 | tf_op jit(solution)/shard_map/convert_element_type | solution.py:62
  36.6 2.5 %all-reduce.2 = (f32[256]{0:T(256)S(1)}, f32[256]{0:T(256)S(1)}) all-reduce(f32[256]{0:T(256)S(1)} %get-tuple-element.13, f32[256]{0:T(256)S(1)} %get-tuple-element.12), channel_id=1, replica_groups=mesh['seq'=16,'head'=2] {'head'}, use_global_device_ids=true, to_apply=%region_2.3 | all-reduce | flops 512 | bytes 4096 | tf_op jit(solution)/shard_map/psum | solution.py:73
  39.3 1.0 %fusion.37 = f32[4,128,128]{2,1,0:T(8,128)} fusion(bf16[256,4,128]{0,2,1:T(8,128)(2,1)S(1)} %get-tuple-element.16, bf16[256,4,128]{0,2,1:T(8,128)(2,1)S(1)} %copy.29), kind=kOutput, calls=%fused_computation.60 | convolution fusion | flops 34340864 | bytes 786432 | tf_op jit(solution)/shard_map/cthd,cthe->chde/dot_general | solution.py:82
  40.6 0.9 %copy.49 = bf16[256,4,128]{2,1,0:T(4,128)(2,1)} copy(bf16[256,4,128]{0,2,1:T(8,128)(2,1)S(1)} %get-tuple-element.17) | data formatting | bytes 524288
  41.5 3.5 %all-to-all-start.2 = ((f32[16,1,4096]{2,1,0:T(1,128)}), f32[16,1,4096]{2,1,0:T(1,128)S(1)}, u32[]{:S(2)}, u32[]{:S(2)}) async-start(f32[16,1,4096]{2,1,0:T(1,128)} %bitcast.12), calls=%async_computation.2 | async-start | bytes 524288 | tf_op jit(solution)/shard_map/all_to_all | solution.py:32
  45.7 0.9 %copy.50 = bf16[256,4,128]{2,1,0:T(4,128)(2,1)} copy(bf16[256,4,128]{0,2,1:T(8,128)(2,1)S(1)} %fusion.7) | data formatting | bytes 524288
  46.6 8.9 %all-to-all-done.2 = f32[16,1,4096]{2,1,0:T(1,128)S(1)} async-done(((f32[16,1,4096]{2,1,0:T(1,128)}), f32[16,1,4096]{2,1,0:T(1,128)S(1)}, u32[]{:S(2)}, u32[]{:S(2)}) %all-to-all-start.2) | async-done | bytes 262176 | tf_op jit(solution)/shard_map/all_to_all | solution.py:32
  55.6 0.8 %rev.7 = f32[15,4096]{1,0:T(8,128)S(1)} reverse(f32[15,4096]{1,0:T(8,128)S(1)} %bitcast.71), dimensions={0} | reverse | bytes 491520 | tf_op jit(solution)/shard_map/jit(_flip)/rev | solution.py:35
  56.6 0.8 %rev.8 = f32[15,4096]{1,0:T(8,128)S(1)} reverse(f32[15,4096]{1,0:T(8,128)S(1)} %reduce_window_sum.25), dimensions={0} | reverse | bytes 491520 | tf_op jit(solution)/shard_map/jit(_flip)/rev | solution.py:35
  57.4 1.0 %copy.45 = f32[16,1,4096]{2,1,0:T(1,128)} copy(f32[16,1,4096]{2,0,1:T(8,128)S(1)} %pad_bitcast_fusion) | data formatting | bytes 524288 | tf_op jit(solution)/shard_map/all_to_all | solution.py:39
  58.4 3.5 %all-to-all-start.3 = ((f32[16,1,4096]{2,1,0:T(1,128)}), f32[16,1,4096]{2,1,0:T(1,128)S(1)}, u32[]{:S(2)}, u32[]{:S(2)}) async-start(f32[16,1,4096]{2,1,0:T(1,128)} %copy.45), calls=%async_computation.3 | async-start | bytes 524288 | tf_op jit(solution)/shard_map/all_to_all | solution.py:39
  62.2 1.1 %fusion.39 = f32[4,128,256]{2,1,0:T(8,128)} fusion(bf16[4,256,256]{2,1,0:T(8,128)(2,1)S(1)} %fusion.1, bf16[256,4,128]{0,2,1:T(8,128)(2,1)S(1)} %copy.29), kind=kOutput, calls=%fused_computation.61 | convolution fusion | flops 67895296 | bytes 1310720 | tf_op jit(solution)/shard_map/chts,cthd->cshd/dot_general | solution.py:95
  63.3 8.1 %all-to-all-done.3 = f32[16,1,4096]{2,1,0:T(1,128)S(1)} async-done(((f32[16,1,4096]{2,1,0:T(1,128)}), f32[16,1,4096]{2,1,0:T(1,128)S(1)}, u32[]{:S(2)}, u32[]{:S(2)}) %all-to-all-start.3) | async-done | bytes 262176 | tf_op jit(solution)/shard_map/all_to_all | solution.py:39
  71.4 1.0 %fusion.23 = bf16[4,128,128]{2,1,0:T(8,128)(2,1)S(1)} fusion(f32[4,128,128]{2,1,0:T(8,128)} %fusion.37, f32[4,128,128]{2,1,0:T(8,128)S(1)} %bitcast.69), kind=kLoop, calls=%fused_computation.44 | loop fusion | flops 196608 | bytes 655360 | tf_op jit(solution)/shard_map/convert_element_type | solution.py:88
  72.7 0.9 %copy.52 = bf16[256,4,128]{2,1,0:T(4,128)(2,1)} copy(bf16[256,4,128]{0,2,1:T(8,128)(2,1)S(1)} %fusion.10) | data formatting | bytes 524288
  74.0 0.9 %copy.51 = bf16[256,4,128]{2,1,0:T(4,128)(2,1)} copy(bf16[256,4,128]{0,2,1:T(8,128)(2,1)S(1)} %fusion.8) | data formatting | bytes 524288
  (31 shorter events, 4.6 us)
Async XLA Ops:
  0.6 1.2 %copy-start = (bf16[256,4,128]{2,1,0:T(4,128)(2,1)S(1)}, bf16[256,4,128]{2,1,0:T(4,128)(2,1)}, u32[]{:S(2)}) copy-start(bf16[256,4,128]{2,1,0:T(4,128)(2,1)} %param.7) | copy-start | bytes 786436
  2.8 8.5 %copy-start.1 = (bf16[256,4,128]{2,1,0:T(4,128)(2,1)S(1)}, bf16[256,4,128]{2,1,0:T(4,128)(2,1)}, u32[]{:S(2)}) copy-start(bf16[256,4,128]{2,1,0:T(4,128)(2,1)} %param.5) | copy-start | bytes 786436
  2.8 18.3 %all-to-all-start = ((f32[16,1,4096]{2,1,0:T(1,128)}), f32[16,1,4096]{2,1,0:T(1,128)S(1)}, u32[]{:S(2)}, u32[]{:S(2)}) async-start(f32[16,1,4096]{2,1,0:T(1,128)} %bitcast.1), calls=%async_computation | async-start | bytes 524288 | tf_op jit(solution)/shard_map/all_to_all | solution.py:32
  11.3 1.0 %copy-start.2 = (bf16[256,4,128]{2,1,0:T(4,128)(2,1)S(1)}, bf16[256,4,128]{2,1,0:T(4,128)(2,1)}, u32[]{:S(2)}) copy-start(bf16[256,4,128]{2,1,0:T(4,128)(2,1)} %param.9) | copy-start | bytes 786436
  22.5 12.8 %all-to-all-start.1 = ((f32[16,1,4096]{2,1,0:T(1,128)}), f32[16,1,4096]{2,1,0:T(1,128)S(1)}, u32[]{:S(2)}, u32[]{:S(2)}) async-start(f32[16,1,4096]{2,1,0:T(1,128)} %copy.36), calls=%async_computation.1 | async-start | bytes 524288 | tf_op jit(solution)/shard_map/all_to_all | solution.py:39
  35.3 1.0 %copy-start.3 = (f32[4,128]{1,0:T(4,128)S(1)}, f32[4,128]{1,0:T(4,128)}, u32[]{:S(2)}) copy-start(f32[4,128]{1,0:T(4,128)} %param.8) | copy-start | bytes 6148
  41.5 14.0 %all-to-all-start.2 = ((f32[16,1,4096]{2,1,0:T(1,128)}), f32[16,1,4096]{2,1,0:T(1,128)S(1)}, u32[]{:S(2)}, u32[]{:S(2)}) async-start(f32[16,1,4096]{2,1,0:T(1,128)} %bitcast.12), calls=%async_computation.2 | async-start | bytes 524288 | tf_op jit(solution)/shard_map/all_to_all | solution.py:32
  58.4 13.0 %all-to-all-start.3 = ((f32[16,1,4096]{2,1,0:T(1,128)}), f32[16,1,4096]{2,1,0:T(1,128)S(1)}, u32[]{:S(2)}, u32[]{:S(2)}) async-start(f32[16,1,4096]{2,1,0:T(1,128)} %copy.45), calls=%async_computation.3 | async-start | bytes 524288 | tf_op jit(solution)/shard_map/all_to_all | solution.py:39
  72.7 1.0 %copy-start.4 = (f32[4,128,256]{2,1,0:T(8,128)S(1)}, f32[4,128,256]{2,1,0:T(8,128)}, u32[]{:S(2)}) copy-start(f32[4,128,256]{2,1,0:T(8,128)} %fusion.39) | copy-start | bytes 1572868

commit v2 on v1

--- a/solution.py
+++ b/solution.py
@@ -25,19 +25,16 @@
 
 def exclusive_scan(own_total, reverse):
     count = lax.axis_size("seq")
-    flat = own_total.reshape(-1)
-    size = flat.shape[0]
+    width = own_total.shape[-1]
+    rows = own_total.reshape(-1, width)
+    size = rows.shape[0]
     chunk = -(-size // count)
-    flat = jnp.pad(flat, (0, chunk * count - size))
-    gathered = lax.all_to_all(flat.reshape(count, chunk), "seq", 0, 0, tiled=True)
-    zero = jnp.zeros((1, chunk), gathered.dtype)
-    if reverse:
-        later = jnp.flip(jnp.cumsum(jnp.flip(gathered[1:], 0), axis=0), 0)
-        prefix = jnp.concatenate([later, zero], axis=0)
-    else:
-        prefix = jnp.concatenate([zero, jnp.cumsum(gathered[:-1], axis=0)], axis=0)
+    rows = jnp.pad(rows, ((0, chunk * count - size), (0, 0)))
+    gathered = lax.all_to_all(rows.reshape(count, chunk, width), "seq", 0, 0, tiled=True)
+    inclusive = lax.cumsum(gathered, axis=0, reverse=reverse)
+    prefix = inclusive - gathered
     spread = lax.all_to_all(prefix, "seq", 0, 0, tiled=True)
-    return spread.reshape(-1)[:size].reshape(own_total.shape)
+    return spread.reshape(-1, width)[:size].reshape(own_total.shape)
 
 
 def lower_sum(own_total):
@@ -70,7 +67,9 @@
     grad_in = out_grad.astype(jnp.float32) * out_gain
     sq_part = jnp.sum(mixed * mixed, axis=(1, 2))
     cross_part = jnp.sum(grad_in * mixed, axis=(1, 2))
-    sq_total, cross_total = lax.psum((sq_part, cross_part), "head")
+    both = jnp.stack([sq_part, cross_part])
+    both = both + lax.ppermute(both, "head", [(0, 1), (1, 0)])
+    sq_total, cross_total = both[0], both[1]
     features = head_count * width * lax.axis_size("head")
     inv_rms = lax.rsqrt(sq_total / features + 1e-06)
     normed_out = (mixed * inv_rms[:, None, None] * out_gain).astype(jnp.bfloat16)

time: 75.6 us -> 71.4 us (0.944)
  local copies, waits for them, and re-layouts: 9.75 us -> 5.74 us
  blocking collectives: 2.47 us -> 0 us
  waiting for transfers between devices: 34.1 us -> 36 us
  other arithmetic: 2.65 us -> 3.73 us
  matrix products: 6.02 us -> 5.22 us
    psum x1 -> x0, blocking collectives: 2.47 us -> none  [body(): sq_total, cross_total = lax.psum((sq_part, cross_part), 'head')]
    all_to_all x4 -> x0, local copies, waits for them, and re-layouts: 1.99 us -> none  [exclusive_scan(): spread = lax.all_to_all(prefix, 'seq', 0, 0, tiled=True)]
    rev x2 -> x0, local copies, waits for them, and re-layouts: 1.52 us -> none  [exclusive_scan(): later = jnp.flip(jnp.cumsum(jnp.flip(gathered[1:], 0), axis=0), 0)]
    ppermute x0 -> x1, waiting for transfers between devices: none -> 1.14 us  [body(): both = both + lax.ppermute(both, 'head', [(0, 1), (1, 0)])]
    another operation x2 -> x3, other arithmetic: 0.45 us -> 1.52 us  [the longest x2 1.51 us: exclusive_scan(): inclusive = lax.cumsum(gathered, axis=0, reverse=reverse)]
    dot_general x1, matrix products: 1.08 us -> 0.29 us  [body(): jnp.einsum('chts,cthd->cshd', bscore, query_act, preferred_element_type=j...]
    all_to_all x2, waiting for transfers between devices: 16.5 us -> 17.3 us  [exclusive_scan(): spread = lax.all_to_all(prefix, 'seq', 0, 0, tiled=True)]
    unnamed x19 -> x15, local copies, waits for them, and re-layouts: 6.21 us -> 5.74 us
  transfers between devices with their start and end apart: 4 -> 5, of which waited for: 4 -> 5; matrix products, arithmetic and copies ran while one was open for 5% -> 5% of each run, Pallas kernels for 0% -> 0%
where the time goes in v2:
time: 71.4 us; the launch traced here: 70.7 us
  waiting for transfers between devices  36 us (50%)
  starting transfers between devices  19.1 us (27%)
  local copies, waits for them, and re-layouts  5.74 us (8%)
  matrix products  5.22 us (7%)
  other arithmetic  3.73 us (5%)
  between operations  0.83 us (1%)
    all_to_all x2, waiting for transfers between devices, exclusive_scan(): lax.all_to_all(rows.reshape(count, chunk, width), 'seq', 0, 0, tiled=True)  17.6 us
    all_to_all x2, waiting for transfers between devices, exclusive_scan(): spread = lax.all_to_all(prefix, 'seq', 0, 0, tiled=True)  17.3 us
    all_to_all x2, starting transfers between devices, exclusive_scan(): lax.all_to_all(rows.reshape(count, chunk, width), 'seq', 0, 0, tiled=True)  12 us
    all_to_all x2, starting transfers between devices, exclusive_scan(): spread = lax.all_to_all(prefix, 'seq', 0, 0, tiled=True)  7.08 us
    unnamed x15, local copies, waits for them, and re-layouts  5.74 us
    another operation x2, other arithmetic, exclusive_scan(): inclusive = lax.cumsum(gathered, axis=0, reverse=reverse)  1.51 us
  transfers between devices with their start and end apart: 5, of which 5 were waited for; matrix products, arithmetic and copies ran while one was open for 5% of the time, Pallas kernels for 0%

profile of v2, /device:TPU:0, one launch (start us, length us, event | category | flops | bytes accessed | tf_op | source)
XLA Modules:
  0.0 70.7 jit_solution(7834454952633129370)
XLA Ops:
  0.6 1.1 %copy.10 = bf16[256,4,128]{0,2,1:T(8,128)(2,1)S(1)} copy(bf16[256,4,128]{2,1,0:T(4,128)(2,1)} %param.6) | data formatting | bytes 524288 | tf_op args[1]
  1.8 1.0 %fusion.28 = f32[4,128,128]{2,1,0:T(8,128)} fusion(bf16[256,4,128]{2,1,0:T(4,128)(2,1)S(1)} %copy-done, bf16[256,4,128]{0,2,1:T(8,128)(2,1)S(1)} %copy.10), kind=kOutput, calls=%fused_computation.51 | convolution fusion | flops 34340864 | bytes 786432 | tf_op jit(solution)/shard_map/cshd,cshe->chde/dot_general | solution.py:56
  2.8 8.4 %all-to-all-start = ((f32[16,32,128]{2,1,0:T(8,128)}), f32[16,32,128]{2,1,0:T(8,128)S(1)}, u32[]{:S(2)}, u32[]{:S(2)}) async-start(f32[16,32,128]{2,1,0:T(8,128)} %bitcast.1), calls=%async_computation | async-start | bytes 524288 | tf_op jit(solution)/shard_map/all_to_all | solution.py:33
  11.4 0.8 %copy-done.2 = bf16[256,4,128]{2,1,0:T(4,128)(2,1)S(1)} copy-done((bf16[256,4,128]{2,1,0:T(4,128)(2,1)S(1)}, bf16[256,4,128]{2,1,0:T(4,128)(2,1)}, u32[]{:S(2)}) %copy-start.2) | copy-done | bytes 262168
  12.4 8.7 %all-to-all-done = f32[16,32,128]{2,1,0:T(8,128)S(1)} async-done(((f32[16,32,128]{2,1,0:T(8,128)}), f32[16,32,128]{2,1,0:T(8,128)S(1)}, u32[]{:S(2)}, u32[]{:S(2)}) %all-to-all-start) | async-done | bytes 262176 | tf_op jit(solution)/shard_map/all_to_all | solution.py:33
  21.1 0.7 %reduce-window_subtract_fusion.1 = f32[16,32,128]{2,1,0:T(8,128)} fusion(f32[16,32,128]{2,1,0:T(8,128)S(1)} %all-to-all-done), kind=kOutput, calls=%fused_computation.18 | output fusion | flops 1048576 | bytes 524288 | tf_op jit(solution)/shard_map/exclusive_scan/reduce_window_sum | solution.py:34
  21.8 3.5 %all-to-all-start.1 = ((f32[16,32,128]{2,1,0:T(8,128)}), f32[16,32,128]{2,1,0:T(8,128)S(1)}, u32[]{:S(2)}, u32[]{:S(2)}) async-start(f32[16,32,128]{2,1,0:T(8,128)} %reduce-window_subtract_fusion.1), calls=%async_computation.1 | async-start | bytes 524288 | tf_op jit(solution)/shard_map/all_to_all | solution.py:36
  25.4 0.5 fusion
  26.2 8.4 %all-to-all-done.1 = f32[16,32,128]{2,1,0:T(8,128)S(1)} async-done(((f32[16,32,128]{2,1,0:T(8,128)}), f32[16,32,128]{2,1,0:T(8,128)S(1)}, u32[]{:S(2)}, u32[]{:S(2)}) %all-to-all-start.1) | async-done | bytes 262176 | tf_op jit(solution)/shard_map/all_to_all | solution.py:36
  34.6 1.0 %fusion.24 = bf16[4,128,128]{2,1,0:T(8,128)(2,1)S(1)} fusion(f32[4,128,128]{2,1,0:T(8,128)} %fusion.28, f32[4,128,128]{2,1,0:T(8,128)S(1)} %bitcast.65), kind=kLoop, calls=%fused_computation.46 | loop fusion | flops 196608 | bytes 655360 | tf_op jit(solution)/shard_map/convert_element_type | solution.py:59
  36.0 1.1 %collective-permute-done = f32[2,256]{1,0:T(2,128)S(1)} collective-permute-done((f32[2,256]{1,0:T(2,128)S(1)}, f32[2,256]{1,0:T(2,128)S(1)}, u32[]{:S(2)}, u32[]{:S(2)}) %collective-permute-start) | collective-permute-done | bytes 2080 | tf_op jit(solution)/shard_map/ppermute | solution.py:71
  37.4 1.0 %fusion.40 = f32[4,128,128]{2,1,0:T(8,128)} fusion(bf16[256,4,128]{0,2,1:T(8,128)(2,1)S(1)} %get-tuple-element.10, bf16[256,4,128]{0,2,1:T(8,128)(2,1)S(1)} %copy.9), kind=kOutput, calls=%fused_computation.62 | convolution fusion | flops 34340864 | bytes 786432 | tf_op jit(solution)/shard_map/cthd,cthe->chde/dot_general | solution.py:81
  38.4 0.3 fusion.1
  38.7 0.9 %copy.25 = bf16[256,4,128]{2,1,0:T(4,128)(2,1)} copy(bf16[256,4,128]{0,2,1:T(8,128)(2,1)S(1)} %get-tuple-element.11) | data formatting | bytes 524288
  39.6 3.5 %all-to-all-start.2 = ((f32[16,32,128]{2,1,0:T(8,128)}), f32[16,32,128]{2,1,0:T(8,128)S(1)}, u32[]{:S(2)}, u32[]{:S(2)}) async-start(f32[16,32,128]{2,1,0:T(8,128)} %bitcast.15), calls=%async_computation.2 | async-start | bytes 524288 | tf_op jit(solution)/shard_map/all_to_all | solution.py:33
  43.8 0.9 %copy.26 = bf16[256,4,128]{2,1,0:T(4,128)(2,1)} copy(bf16[256,4,128]{0,2,1:T(8,128)(2,1)S(1)} %fusion.7) | data formatting | bytes 524288
  44.7 8.9 %all-to-all-done.2 = f32[16,32,128]{2,1,0:T(8,128)S(1)} async-done(((f32[16,32,128]{2,1,0:T(8,128)}), f32[16,32,128]{2,1,0:T(8,128)S(1)}, u32[]{:S(2)}, u32[]{:S(2)}) %all-to-all-start.2) | async-done | bytes 262176 | tf_op jit(solution)/shard_map/all_to_all | solution.py:33
  53.6 0.8 %reduce-window_subtract_fusion = f32[16,32,128]{2,1,0:T(8,128)} fusion(f32[16,32,128]{2,1,0:T(8,128)S(1)} %all-to-all-done.2), kind=kOutput, calls=%fused_computation.17 | output fusion | flops 1048576 | bytes 524288 | tf_op jit(solution)/shard_map/exclusive_scan/reduce_window_sum | solution.py:34
  54.4 3.5 %all-to-all-start.3 = ((f32[16,32,128]{2,1,0:T(8,128)}), f32[16,32,128]{2,1,0:T(8,128)S(1)}, u32[]{:S(2)}, u32[]{:S(2)}) async-start(f32[16,32,128]{2,1,0:T(8,128)} %reduce-window_subtract_fusion), calls=%async_computation.3 | async-start | bytes 524288 | tf_op jit(solution)/shard_map/all_to_all | solution.py:36
  58.4 8.9 %all-to-all-done.3 = f32[16,32,128]{2,1,0:T(8,128)S(1)} async-done(((f32[16,32,128]{2,1,0:T(8,128)}), f32[16,32,128]{2,1,0:T(8,128)S(1)}, u32[]{:S(2)}, u32[]{:S(2)}) %all-to-all-start.3) | async-done | bytes 262176 | tf_op jit(solution)/shard_map/all_to_all | solution.py:36
  67.3 1.0 %fusion.23 = bf16[4,128,128]{2,1,0:T(8,128)(2,1)S(1)} fusion(f32[4,128,128]{2,1,0:T(8,128)} %fusion.40, f32[4,128,128]{2,1,0:T(8,128)S(1)} %bitcast.64), kind=kLoop, calls=%fused_computation.44 | loop fusion | flops 196608 | bytes 655360 | tf_op jit(solution)/shard_map/convert_element_type | solution.py:87
  68.3 0.3 fusion.10
  68.6 0.9 %copy.28 = bf16[256,4,128]{2,1,0:T(4,128)(2,1)} copy(bf16[256,4,128]{0,2,1:T(8,128)(2,1)S(1)} %fusion.10) | data formatting | bytes 524288
  69.8 0.9 %copy.27 = bf16[256,4,128]{2,1,0:T(4,128)(2,1)} copy(bf16[256,4,128]{0,2,1:T(8,128)(2,1)S(1)} %fusion.8) | data formatting | bytes 524288
  (23 shorter events, 2.8 us)
Async XLA Ops:
  0.6 1.2 %copy-start = (bf16[256,4,128]{2,1,0:T(4,128)(2,1)S(1)}, bf16[256,4,128]{2,1,0:T(4,128)(2,1)}, u32[]{:S(2)}) copy-start(bf16[256,4,128]{2,1,0:T(4,128)(2,1)} %param.7) | copy-start | bytes 786436
  2.8 8.5 %copy-start.1 = (bf16[256,4,128]{2,1,0:T(4,128)(2,1)S(1)}, bf16[256,4,128]{2,1,0:T(4,128)(2,1)}, u32[]{:S(2)}) copy-start(bf16[256,4,128]{2,1,0:T(4,128)(2,1)} %param.5) | copy-start | bytes 786436
  2.8 18.3 %all-to-all-start = ((f32[16,32,128]{2,1,0:T(8,128)}), f32[16,32,128]{2,1,0:T(8,128)S(1)}, u32[]{:S(2)}, u32[]{:S(2)}) async-start(f32[16,32,128]{2,1,0:T(8,128)} %bitcast.1), calls=%async_computation | async-start | bytes 524288 | tf_op jit(solution)/shard_map/all_to_all | solution.py:33
  11.3 1.0 %copy-start.2 = (bf16[256,4,128]{2,1,0:T(4,128)(2,1)S(1)}, bf16[256,4,128]{2,1,0:T(4,128)(2,1)}, u32[]{:S(2)}) copy-start(bf16[256,4,128]{2,1,0:T(4,128)(2,1)} %param.9) | copy-start | bytes 786436
  21.8 12.8 %all-to-all-start.1 = ((f32[16,32,128]{2,1,0:T(8,128)}), f32[16,32,128]{2,1,0:T(8,128)S(1)}, u32[]{:S(2)}, u32[]{:S(2)}) async-start(f32[16,32,128]{2,1,0:T(8,128)} %reduce-window_subtract_fusion.1), calls=%async_computation.1 | async-start | bytes 524288 | tf_op jit(solution)/shard_map/all_to_all | solution.py:36
  34.6 1.0 %copy-start.3 = (f32[4,128]{1,0:T(4,128)S(1)}, f32[4,128]{1,0:T(4,128)}, u32[]{:S(2)}) copy-start(f32[4,128]{1,0:T(4,128)} %param.8) | copy-start | bytes 6148
  36.0 1.2 %collective-permute-start = (f32[2,256]{1,0:T(2,128)S(1)}, f32[2,256]{1,0:T(2,128)S(1)}, u32[]{:S(2)}, u32[]{:S(2)}) collective-permute-start(f32[2,256]{1,0:T(2,128)S(1)} %pad_maximum_fusion), channel_id=1, source_target_pairs={{0,1},{1,0},{2,3},{3,2},{4,5},{5,4},{6,7},{7,6},{8,9},{9,8},{10,11... | collective-permute-start | bytes 6152 | tf_op jit(solution)/shard_map/ppermute | solution.py:71
  39.6 14.0 %all-to-all-start.2 = ((f32[16,32,128]{2,1,0:T(8,128)}), f32[16,32,128]{2,1,0:T(8,128)S(1)}, u32[]{:S(2)}, u32[]{:S(2)}) async-start(f32[16,32,128]{2,1,0:T(8,128)} %bitcast.15), calls=%async_computation.2 | async-start | bytes 524288 | tf_op jit(solution)/shard_map/all_to_all | solution.py:33
  54.4 13.0 %all-to-all-start.3 = ((f32[16,32,128]{2,1,0:T(8,128)}), f32[16,32,128]{2,1,0:T(8,128)S(1)}, u32[]{:S(2)}, u32[]{:S(2)}) async-start(f32[16,32,128]{2,1,0:T(8,128)} %reduce-window_subtract_fusion), calls=%async_computation.3 | async-start | bytes 524288 | tf_op jit(solution)/shard_map/all_to_all | solution.py:36

commit v3 on v2

--- a/solution.py
+++ b/solution.py
@@ -31,8 +31,16 @@
     chunk = -(-size // count)
     rows = jnp.pad(rows, ((0, chunk * count - size), (0, 0)))
     gathered = lax.all_to_all(rows.reshape(count, chunk, width), "seq", 0, 0, tiled=True)
-    inclusive = lax.cumsum(gathered, axis=0, reverse=reverse)
-    prefix = inclusive - gathered
+    if count > 32:
+        prefix = lax.cumsum(gathered, axis=0, reverse=reverse) - gathered
+    else:
+        order = range(count - 1, -1, -1) if reverse else range(count)
+        running = jnp.zeros_like(gathered[0])
+        parts = [None] * count
+        for index in order:
+            parts[index] = running
+            running = running + gathered[index]
+        prefix = jnp.stack(parts)
     spread = lax.all_to_all(prefix, "seq", 0, 0, tiled=True)
     return spread.reshape(-1, width)[:size].reshape(own_total.shape)
 
@@ -83,7 +91,7 @@
     )
     own_grad = jnp.sum(block_grad, axis=0)
     after = upper_sum(own_grad)
-    local_after = jnp.flip(jnp.cumsum(jnp.flip(block_grad, 0), axis=0), 0) - block_grad
+    local_after = lax.cumsum(block_grad, axis=0, reverse=True) - block_grad
     grad_state = (after[None] + local_after).astype(jnp.bfloat16)
     bscore = jnp.einsum("cthe,cshe->chts", delta_blk, value_blk, preferred_element_type=jnp.float32)
     bscore = jnp.where(mask, bscore, 0.0).astype(jnp.bfloat16)

time: 71.4 us -> 88.9 us (1.25)
  other arithmetic: 3.73 us -> 16.2 us
  local copies, waits for them, and re-layouts: 5.74 us -> 11.4 us
  waiting for transfers between devices: 36 us -> 34.6 us
    unnamed x0 -> x22, other arithmetic: none -> 13.4 us
    unnamed x15 -> x25, local copies, waits for them, and re-layouts: 5.74 us -> 10.8 us
    another operation x2 -> x1, other arithmetic: 1.51 us -> 0.61 us  [exclusive_scan(): prefix = jnp.stack(parts)]
where the time goes in v3:
time: 88.9 us; the launch traced here: 88.2 us
  waiting for transfers between devices  34.6 us (39%)
  starting transfers between devices  19.1 us (21%)
  other arithmetic  16.2 us (18%)
  local copies, waits for them, and re-layouts  11.4 us (13%)
  matrix products  6.02 us (7%)
    all_to_all x2, waiting for transfers between devices, exclusive_scan(): lax.all_to_all(rows.reshape(count, chunk, width), 'seq', 0, 0, tiled=True)  17 us
    all_to_all x2, waiting for transfers between devices, exclusive_scan(): spread = lax.all_to_all(prefix, 'seq', 0, 0, tiled=True)  16.5 us
    unnamed x22, other arithmetic  13.4 us
    all_to_all x2, starting transfers between devices, exclusive_scan(): lax.all_to_all(rows.reshape(count, chunk, width), 'seq', 0, 0, tiled=True)  12 us
    unnamed x25, local copies, waits for them, and re-layouts  10.8 us
    all_to_all x2, starting transfers between devices, exclusive_scan(): spread = lax.all_to_all(prefix, 'seq', 0, 0, tiled=True)  7.08 us
  transfers between devices with their start and end apart: 5, of which 5 were waited for; matrix products, arithmetic and copies ran while one was open for 5% of the time, Pallas kernels for 0%

profile of v3, /device:TPU:0, one launch (start us, length us, event | category | flops | bytes accessed | tf_op | source)
XLA Modules:
  0.0 88.2 jit_solution(5838164292148082990)
XLA Ops:
  0.6 1.1 %copy.10 = bf16[256,4,128]{0,2,1:T(8,128)(2,1)S(1)} copy(bf16[256,4,128]{2,1,0:T(4,128)(2,1)} %param.6) | data formatting | bytes 524288 | tf_op args[1]
  1.8 1.0 %fusion.28 = f32[4,128,128]{2,1,0:T(8,128)} fusion(bf16[256,4,128]{2,1,0:T(4,128)(2,1)S(1)} %copy-done, bf16[256,4,128]{0,2,1:T(8,128)(2,1)S(1)} %copy.10), kind=kOutput, calls=%fused_computation.49 | convolution fusion | flops 34340864 | bytes 786432 | tf_op jit(solution)/shard_map/cshd,cshe->chde/dot_general | solution.py:64
  2.8 8.4 %all-to-all-start = ((f32[16,32,128]{2,1,0:T(8,128)}), f32[16,32,128]{2,1,0:T(8,128)S(1)}, u32[]{:S(2)}, u32[]{:S(2)}) async-start(f32[16,32,128]{2,1,0:T(8,128)} %bitcast.1), calls=%async_computation | async-start | bytes 524288 | tf_op jit(solution)/shard_map/all_to_all | solution.py:33
  11.4 0.8 copy-done.2
  13.0 8.1 %all-to-all-done = f32[16,32,128]{2,1,0:T(8,128)S(1)} async-done(((f32[16,32,128]{2,1,0:T(8,128)}), f32[16,32,128]{2,1,0:T(8,128)S(1)}, u32[]{:S(2)}, u32[]{:S(2)}) %all-to-all-start) | async-done | bytes 262176 | tf_op jit(solution)/shard_map/all_to_all | solution.py:33
  22.3 0.6 constant_dynamic-update-slice_fusion.12
  22.9 0.6 constant_dynamic-update-slice_fusion.11
  29.6 0.6 constant_dynamic-update-slice_fusion
  30.3 3.5 %all-to-all-start.1 = ((f32[16,32,128]{2,1,0:T(8,128)}), f32[16,32,128]{2,1,0:T(8,128)S(1)}, u32[]{:S(2)}, u32[]{:S(2)}) async-start(f32[16,32,128]{2,1,0:T(8,128)} %constant_dynamic-update-slice_fusion), calls=%async_computation.1 | async-start | bytes 524288 | tf_op jit(solution)/shard_map/all_to_all | solution.py:44
  34.6 8.4 %all-to-all-done.1 = f32[16,32,128]{2,1,0:T(8,128)S(1)} async-done(((f32[16,32,128]{2,1,0:T(8,128)}), f32[16,32,128]{2,1,0:T(8,128)S(1)}, u32[]{:S(2)}, u32[]{:S(2)}) %all-to-all-start.1) | async-done | bytes 262176 | tf_op jit(solution)/shard_map/all_to_all | solution.py:44
  43.0 1.0 %fusion.24 = bf16[4,128,128]{2,1,0:T(8,128)(2,1)S(1)} fusion(f32[4,128,128]{2,1,0:T(8,128)} %fusion.28, f32[4,128,128]{2,1,0:T(8,128)S(1)} %bitcast.63), kind=kLoop, calls=%fused_computation.44 | loop fusion | flops 196608 | bytes 655360 | tf_op jit(solution)/shard_map/convert_element_type | solution.py:67
  44.5 1.1 %collective-permute-done = f32[2,256]{1,0:T(2,128)S(1)} collective-permute-done((f32[2,256]{1,0:T(2,128)S(1)}, f32[2,256]{1,0:T(2,128)S(1)}, u32[]{:S(2)}, u32[]{:S(2)}) %collective-permute-start) | collective-permute-done | bytes 2080 | tf_op jit(solution)/shard_map/ppermute | solution.py:79
  45.8 1.0 %fusion.40 = f32[4,128,128]{2,1,0:T(8,128)} fusion(bf16[256,4,128]{0,2,1:T(8,128)(2,1)S(1)} %get-tuple-element.26, bf16[256,4,128]{0,2,1:T(8,128)(2,1)S(1)} %copy.9), kind=kOutput, calls=%fused_computation.120 | convolution fusion | flops 34340864 | bytes 786432 | tf_op jit(solution)/shard_map/cthd,cthe->chde/dot_general | solution.py:89
  47.2 0.9 copy.25
  48.0 3.5 %all-to-all-start.2 = ((f32[16,32,128]{2,1,0:T(8,128)}), f32[16,32,128]{2,1,0:T(8,128)S(1)}, u32[]{:S(2)}, u32[]{:S(2)}) async-start(f32[16,32,128]{2,1,0:T(8,128)} %bitcast.15), calls=%async_computation.2 | async-start | bytes 524288 | tf_op jit(solution)/shard_map/all_to_all | solution.py:33
  52.2 0.9 copy.26
  53.1 8.9 %all-to-all-done.2 = f32[16,32,128]{2,1,0:T(8,128)S(1)} async-done(((f32[16,32,128]{2,1,0:T(8,128)}), f32[16,32,128]{2,1,0:T(8,128)S(1)}, u32[]{:S(2)}, u32[]{:S(2)}) %all-to-all-start.2) | async-done | bytes 262176 | tf_op jit(solution)/shard_map/all_to_all | solution.py:33
  62.0 0.6 constant_dynamic-update-slice_fusion.31
  71.7 3.5 %all-to-all-start.3 = ((f32[16,32,128]{2,1,0:T(8,128)}), f32[16,32,128]{2,1,0:T(8,128)S(1)}, u32[]{:S(2)}, u32[]{:S(2)}) async-start(f32[16,32,128]{2,1,0:T(8,128)} %constant_dynamic-update-slice_fusion.16), calls=%async_computation.3 | async-start | bytes 524288 | tf_op jit(solution)/shard_map/all_to_all | solution.py:44
  75.5 1.1 %fusion.42 = f32[4,128,256]{2,1,0:T(8,128)} fusion(bf16[4,256,256]{2,1,0:T(8,128)(2,1)S(1)} %fusion.1, bf16[256,4,128]{0,2,1:T(8,128)(2,1)S(1)} %copy.9), kind=kOutput, calls=%fused_computation.121 | convolution fusion | flops 67895296 | bytes 1310720 | tf_op jit(solution)/shard_map/chts,cthd->cshd/dot_general | solution.py:102
  76.6 8.1 %all-to-all-done.3 = f32[16,32,128]{2,1,0:T(8,128)S(1)} async-done(((f32[16,32,128]{2,1,0:T(8,128)}), f32[16,32,128]{2,1,0:T(8,128)S(1)}, u32[]{:S(2)}, u32[]{:S(2)}) %all-to-all-start.3) | async-done | bytes 262176 | tf_op jit(solution)/shard_map/all_to_all | solution.py:44
  84.7 1.0 %fusion.23 = bf16[4,128,128]{2,1,0:T(8,128)(2,1)S(1)} fusion(f32[4,128,128]{2,1,0:T(8,128)} %fusion.40, f32[4,128,128]{2,1,0:T(8,128)S(1)} %bitcast.62), kind=kLoop, calls=%fused_computation.42 | loop fusion | flops 196608 | bytes 655360 | tf_op jit(solution)/shard_map/convert_element_type | solution.py:95
  86.0 0.9 copy.28
  87.4 0.9 copy.27
  (55 shorter events, 20.8 us)
Async XLA Ops:
  0.6 1.2 %copy-start = (bf16[256,4,128]{2,1,0:T(4,128)(2,1)S(1)}, bf16[256,4,128]{2,1,0:T(4,128)(2,1)}, u32[]{:S(2)}) copy-start(bf16[256,4,128]{2,1,0:T(4,128)(2,1)} %param.7) | copy-start | bytes 786436
  2.8 8.5 %copy-start.1 = (bf16[256,4,128]{2,1,0:T(4,128)(2,1)S(1)}, bf16[256,4,128]{2,1,0:T(4,128)(2,1)}, u32[]{:S(2)}) copy-start(bf16[256,4,128]{2,1,0:T(4,128)(2,1)} %param.5) | copy-start | bytes 786436
  2.8 18.3 %all-to-all-start = ((f32[16,32,128]{2,1,0:T(8,128)}), f32[16,32,128]{2,1,0:T(8,128)S(1)}, u32[]{:S(2)}, u32[]{:S(2)}) async-start(f32[16,32,128]{2,1,0:T(8,128)} %bitcast.1), calls=%async_computation | async-start | bytes 524288 | tf_op jit(solution)/shard_map/all_to_all | solution.py:33
  11.3 1.0 %copy-start.2 = (bf16[256,4,128]{2,1,0:T(4,128)(2,1)S(1)}, bf16[256,4,128]{2,1,0:T(4,128)(2,1)}, u32[]{:S(2)}) copy-start(bf16[256,4,128]{2,1,0:T(4,128)(2,1)} %param.9) | copy-start | bytes 786436
  30.3 12.8 %all-to-all-start.1 = ((f32[16,32,128]{2,1,0:T(8,128)}), f32[16,32,128]{2,1,0:T(8,128)S(1)}, u32[]{:S(2)}, u32[]{:S(2)}) async-start(f32[16,32,128]{2,1,0:T(8,128)} %constant_dynamic-update-slice_fusion), calls=%async_computation.1 | async-start | bytes 524288 | tf_op jit(solution)/shard_map/all_to_all | solution.py:44
  43.0 1.0 %copy-start.3 = (f32[4,128]{1,0:T(4,128)S(1)}, f32[4,128]{1,0:T(4,128)}, u32[]{:S(2)}) copy-start(f32[4,128]{1,0:T(4,128)} %param.8) | copy-start | bytes 6148
  44.4 1.2 %collective-permute-start = (f32[2,256]{1,0:T(2,128)S(1)}, f32[2,256]{1,0:T(2,128)S(1)}, u32[]{:S(2)}, u32[]{:S(2)}) collective-permute-start(f32[2,256]{1,0:T(2,128)S(1)} %pad_maximum_fusion), channel_id=1, source_target_pairs={{0,1},{1,0},{2,3},{3,2},{4,5},{5,4},{6,7},{7,6},{8,9},{9,8},{10,11... | collective-permute-start | bytes 6152 | tf_op jit(solution)/shard_map/ppermute | solution.py:79
  48.0 14.0 %all-to-all-start.2 = ((f32[16,32,128]{2,1,0:T(8,128)}), f32[16,32,128]{2,1,0:T(8,128)S(1)}, u32[]{:S(2)}, u32[]{:S(2)}) async-start(f32[16,32,128]{2,1,0:T(8,128)} %bitcast.15), calls=%async_computation.2 | async-start | bytes 524288 | tf_op jit(solution)/shard_map/all_to_all | solution.py:33
  71.7 13.0 %all-to-all-start.3 = ((f32[16,32,128]{2,1,0:T(8,128)}), f32[16,32,128]{2,1,0:T(8,128)S(1)}, u32[]{:S(2)}, u32[]{:S(2)}) async-start(f32[16,32,128]{2,1,0:T(8,128)} %constant_dynamic-update-slice_fusion.16), calls=%async_computation.3 | async-start | bytes 524288 | tf_op jit(solution)/shard_map/all_to_all | solution.py:44
  86.0 1.0 %copy-start.4 = (f32[4,128,256]{2,1,0:T(8,128)S(1)}, f32[4,128,256]{2,1,0:T(8,128)}, u32[]{:S(2)}) copy-start(f32[4,128,256]{2,1,0:T(8,128)} %fusion.42) | copy-start | bytes 1572868

commit v4 on v2

v4 whole, which is shorter than its diff:
```python
import jax
import jax.numpy as jnp
from jax import lax
from jax.sharding import PartitionSpec as P

GROUP = 256


def from_behind(shard, axis, by):
    count = lax.axis_size(axis)
    pairs = [(i, i + by) for i in range(count) if 0 <= i + by < count]
    return lax.ppermute(shard, axis, pairs)


def silu_grad(raw):
    sigma = jax.nn.sigmoid(raw)
    return sigma * (1.0 + raw * (1.0 - sigma))


def causal_mask(length):
    rows = lax.broadcasted_iota(jnp.int32, (length, length), 0)
    cols = lax.broadcasted_iota(jnp.int32, (length, length), 1)
    return cols <= rows


def exclusive_scan(own_total, reverse):
    count = lax.axis_size("seq")
    width = own_total.shape[-1]
    rows = own_total.reshape(-1, width)
    size = rows.shape[0]
    chunk = -(-size // count)
    rows = jnp.pad(rows, ((0, chunk * count - size), (0, 0)))
    gathered = lax.all_to_all(rows.reshape(count, chunk, width), "seq", 0, 0, tiled=True)
    inclusive = lax.cumsum(gathered, axis=0, reverse=reverse)
    prefix = inclusive - gathered
    spread = lax.all_to_all(prefix, "seq", 0, 0, tiled=True)
    return spread.reshape(-1, width)[:size].reshape(own_total.shape)


def lower_sum(own_total):
    return exclusive_scan(own_total, False)


def upper_sum(own_total):
    return exclusive_scan(own_total, True)


def mm(lhs, rhs, lhs_dim, rhs_dim):
    dims = (((lhs_dim,), (rhs_dim,)), ((), ()))
    return lax.dot_general(lhs, rhs, dims, preferred_element_type=jnp.float32)


def body(query_raw, key_raw, value_raw, out_gain, out_grad):
    tok_rows, head_count, width = query_raw.shape
    blocks = tok_rows // GROUP
    query_act = jax.nn.silu(query_raw.astype(jnp.float32)).astype(jnp.bfloat16)
    key_act = jax.nn.silu(key_raw.astype(jnp.float32)).astype(jnp.bfloat16)
    mask = causal_mask(GROUP)
    cells = [(c, h) for c in range(blocks) for h in range(head_count)]

    def cut(array, c, h):
        return array[c * GROUP:(c + 1) * GROUP, h, :]

    def join(parts):
        rows = [jnp.stack([parts[(c, h)] for h in range(head_count)], axis=1) for c in range(blocks)]
        return rows[0] if blocks == 1 else jnp.concatenate(rows, axis=0)

    block_kv = jnp.stack([
        jnp.stack([mm(cut(key_act, c, h), cut(value_raw, c, h), 0, 0) for h in range(head_count)])
        for c in range(blocks)
    ])
    own_total = jnp.sum(block_kv, axis=0)
    before = lower_sum(own_total)
    state_b = (before[None] + (jnp.cumsum(block_kv, axis=0) - block_kv)).astype(jnp.bfloat16)
    attn = {}
    mixed_parts = {}
    for c, h in cells:
        scores = mm(cut(query_act, c, h), cut(key_act, c, h), 1, 1)
        attn[c, h] = jnp.where(mask, scores, 0.0).astype(jnp.bfloat16)
        mixed_parts[c, h] = mm(attn[c, h], cut(value_raw, c, h), 1, 0) + mm(
            cut(query_act, c, h), state_b[c, h], 1, 0
        )
    mixed = join(mixed_parts)
    grad_in = out_grad.astype(jnp.float32) * out_gain
    sq_part = jnp.sum(mixed * mixed, axis=(1, 2))
    cross_part = jnp.sum(grad_in * mixed, axis=(1, 2))
    both = jnp.stack([sq_part, cross_part])
    both = both + lax.ppermute(both, "head", [(0, 1), (1, 0)])
    sq_total, cross_total = both[0], both[1]
    features = head_count * width * lax.axis_size("head")
    inv_rms = lax.rsqrt(sq_total / features + 1e-06)
    normed_out = (mixed * inv_rms[:, None, None] * out_gain).astype(jnp.bfloat16)
    delta = (
        grad_in * inv_rms[:, None, None]
        - mixed * (cross_total * inv_rms**3 / features)[:, None, None]
    ).astype(jnp.bfloat16)
    block_grad = jnp.stack([
        jnp.stack([mm(cut(query_act, c, h), cut(delta, c, h), 0, 0) for h in range(head_count)])
        for c in range(blocks)
    ])
    own_grad = jnp.sum(block_grad, axis=0)
    after = upper_sum(own_grad)
    local_after = lax.cumsum(block_grad, axis=0, reverse=True) - block_grad
    grad_state = (after[None] + local_after).astype(jnp.bfloat16)
    dq_parts, dk_parts, dv_parts = {}, {}, {}
    for c, h in cells:
        delta_c = cut(delta, c, h)
        value_c = cut(value_raw, c, h)
        bscore = jnp.where(mask, mm(delta_c, value_c, 1, 1), 0.0).astype(jnp.bfloat16)
        dq_parts[c, h] = mm(bscore, cut(key_act, c, h), 1, 0) + mm(delta_c, state_b[c, h], 1, 1)
        dk_parts[c, h] = mm(bscore, cut(query_act, c, h), 0, 0) + mm(value_c, grad_state[c, h], 1, 1)
        dv_parts[c, h] = mm(attn[c, h], delta_c, 0, 0) + mm(cut(key_act, c, h), grad_state[c, h], 1, 0)
    query_grad = (join(dq_parts) * silu_grad(query_raw.astype(jnp.float32))).astype(jnp.bfloat16)
    key_grad = (join(dk_parts) * silu_grad(key_raw.astype(jnp.float32))).astype(jnp.bfloat16)
    value_grad = join(dv_parts).astype(jnp.bfloat16)
    return (normed_out, query_grad, key_grad, value_grad)


def solution(mesh):
    in_specs = (
        P("seq", "head", None),
        P("seq", "head", None),
        P("seq", "head", None),
        P("head", None),
        P("seq", "head", None),
    )
    out_specs = (
        P("seq", "head", None),
        P("seq", "head", None),
        P("seq", "head", None),
        P("seq", "head", None),
    )
    return jax.shard_map(body, mesh=mesh, in_specs=in_specs, out_specs=out_specs, check_vma=False)
```

time: 71.4 us -> 76.5 us (1.071)
  matrix products: 5.22 us -> 9.92 us
  waiting for transfers between devices: 36 us -> 33.7 us
  other arithmetic: 3.73 us -> 5.15 us
  local copies, waits for them, and re-layouts: 5.74 us -> 6.83 us
    dot_general x12 -> x48, matrix products: 5.22 us -> 9.92 us  [mm(): return lax.dot_general(lhs, rhs, dims, preferred_element_type=jnp.float32)]
    all_to_all x2, waiting for transfers between devices: 17.3 us -> 13.9 us  [exclusive_scan(): spread = lax.all_to_all(prefix, 'seq', 0, 0, tiled=True)]
    convert_element_type x0 -> x4, other arithmetic: none -> 1.7 us  [the longest x1 1.14 us: body(): key_act = jax.nn.silu(key_raw.astype(jnp.float32)).astype(jnp.bfloat16)]
    another operation x0 -> x3, other arithmetic: none -> 1.5 us  [the longest x1 0.73 us: body(): jnp.stack([mm(cut(query_act, c, h), cut(delta, c, h), 0, 0) for h in rang...]
    all_to_all x2, waiting for transfers between devices: 17.6 us -> 18.7 us  [exclusive_scan(): lax.all_to_all(rows.reshape(count, chunk, width), 'seq', 0, 0, tiled=True)]
    convert_element_type x1, other arithmetic: 0.99 us -> 0.03 us  [body(): (before[None] + (jnp.cumsum(block_kv, axis=0) - block_kv)).astype(jnp.bfl...]
    convert_element_type x1, other arithmetic: 0.98 us -> 0.03 us  [body(): grad_state = (after[None] + local_after).astype(jnp.bfloat16)]
    unnamed x15 -> x17, local copies, waits for them, and re-layouts: 5.74 us -> 6.41 us
  transfers between devices with their start and end apart: 5 -> 5, of which waited for: 5 -> 5; matrix products, arithmetic and copies ran while one was open for 5% -> 6% of each run, Pallas kernels for 0% -> 0%
where the time goes in v4:
time: 76.5 us; the launch traced here: 75.9 us
  waiting for transfers between devices  33.7 us (44%)
  starting transfers between devices  19.1 us (25%)
  matrix products  9.92 us (13%)
  local copies, waits for them, and re-layouts  6.83 us (9%)
  other arithmetic  5.15 us (7%)
  between operations  1.15 us (2%)
    all_to_all x2, waiting for transfers between devices, exclusive_scan(): lax.all_to_all(rows.reshape(count, chunk, width), 'seq', 0, 0, tiled=True)  18.7 us
    all_to_all x2, waiting for transfers between devices, exclusive_scan(): spread = lax.all_to_all(prefix, 'seq', 0, 0, tiled=True)  13.9 us
    all_to_all x2, starting transfers between devices, exclusive_scan(): lax.all_to_all(rows.reshape(count, chunk, width), 'seq', 0, 0, tiled=True)  12 us
    dot_general x48, matrix products, mm(): return lax.dot_general(lhs, rhs, dims, preferred_element_type=jnp.float32)  9.92 us
    all_to_all x2, starting transfers between devices, exclusive_scan(): spread = lax.all_to_all(prefix, 'seq', 0, 0, tiled=True)  7.08 us
    unnamed x17, local copies, waits for them, and re-layouts  6.41 us
  transfers between devices with their start and end apart: 5, of which 5 were waited for; matrix products, arithmetic and copies ran while one was open for 6% of the time, Pallas kernels for 0%

profile of v4, /device:TPU:0, one launch (start us, length us, event | category | flops | bytes accessed | tf_op | source)
XLA Modules:
  0.0 75.9 jit_solution(16460641725027071231)
XLA Ops:
  0.6 1.1 %fusion.39 = bf16[256,4,128]{2,0,1:T(8,128)(2,1)S(1)} fusion(bf16[256,4,128]{2,1,0:T(4,128)(2,1)} %param.6), kind=kLoop, calls=%fused_computation.75 | loop fusion | flops 786432 | bytes 524288 | tf_op jit(solution)/shard_map/convert_element_type | solution.py:57
  1.8 0.4 fusion.73
  3.0 0.7 pad_maximum_fusion.1
  3.8 8.4 %all-to-all-start = ((f32[16,32,128]{2,1,0:T(8,128)}), f32[16,32,128]{2,1,0:T(8,128)S(1)}, u32[]{:S(2)}, u32[]{:S(2)}) async-start(f32[16,32,128]{2,1,0:T(8,128)} %bitcast.13), calls=%async_computation | async-start | bytes 524288 | tf_op jit(solution)/shard_map/all_to_all | solution.py:33
  12.6 9.5 %all-to-all-done = f32[16,32,128]{2,1,0:T(8,128)S(1)} async-done(((f32[16,32,128]{2,1,0:T(8,128)}), f32[16,32,128]{2,1,0:T(8,128)S(1)}, u32[]{:S(2)}, u32[]{:S(2)}) %all-to-all-start) | async-done | bytes 262176 | tf_op jit(solution)/shard_map/all_to_all | solution.py:33
  22.1 0.7 reduce-window_subtract_fusion.1
  22.8 3.5 %all-to-all-start.1 = ((f32[16,32,128]{2,1,0:T(8,128)}), f32[16,32,128]{2,1,0:T(8,128)S(1)}, u32[]{:S(2)}, u32[]{:S(2)}) async-start(f32[16,32,128]{2,1,0:T(8,128)} %reduce-window_subtract_fusion.1), calls=%async_computation.1 | async-start | bytes 524288 | tf_op jit(solution)/shard_map/all_to_all | solution.py:36
  26.6 0.7 copy-done.4
  27.9 7.7 %all-to-all-done.1 = f32[16,32,128]{2,1,0:T(8,128)S(1)} async-done(((f32[16,32,128]{2,1,0:T(8,128)}), f32[16,32,128]{2,1,0:T(8,128)S(1)}, u32[]{:S(2)}, u32[]{:S(2)}) %all-to-all-start.1) | async-done | bytes 262176 | tf_op jit(solution)/shard_map/all_to_all | solution.py:36
  37.4 0.4 copy-done.5
  38.1 1.1 %collective-permute-done = f32[2,256]{1,0:T(2,128)S(1)} collective-permute-done((f32[2,256]{1,0:T(2,128)S(1)}, f32[2,256]{1,0:T(2,128)S(1)}, u32[]{:S(2)}, u32[]{:S(2)}) %collective-permute-start) | collective-permute-done | bytes 2080 | tf_op jit(solution)/shard_map/ppermute | solution.py:88
  41.5 0.7 pad_maximum_fusion.2
  42.2 3.6 %all-to-all-start.2 = ((f32[16,32,128]{2,1,0:T(8,128)}), f32[16,32,128]{2,1,0:T(8,128)S(1)}, u32[]{:S(2)}, u32[]{:S(2)}) async-start(f32[16,32,128]{2,1,0:T(8,128)} %bitcast.46), calls=%async_computation.2 | async-start | bytes 524288 | tf_op jit(solution)/shard_map/all_to_all | solution.py:33
  45.8 0.8 %fusion.15 = f32[256,1,128]{2,0,1:T(8,128)} fusion(f32[256,128]{1,0:T(8,128)S(1)} %fusion.64, bf16[256,256]{1,0:T(8,128)(2,1)S(1)} %fusion.4, bf16[256,4,128]{2,0,1:T(8,128)(2,1)S(1)} %fusion.39), kind=kOutput, calls=%fused_computation.37 | convolution fusion | flops 16809984 | bytes 458752 | tf_op jit(solution)/shard_map/dot_general | solution.py:50
  47.0 9.1 %all-to-all-done.2 = f32[16,32,128]{2,1,0:T(8,128)S(1)} async-done(((f32[16,32,128]{2,1,0:T(8,128)}), f32[16,32,128]{2,1,0:T(8,128)S(1)}, u32[]{:S(2)}, u32[]{:S(2)}) %all-to-all-start.2) | async-done | bytes 262176 | tf_op jit(solution)/shard_map/all_to_all | solution.py:33
  56.2 0.8 %reduce-window_subtract_fusion = f32[16,32,128]{2,1,0:T(8,128)} fusion(f32[16,32,128]{2,1,0:T(8,128)S(1)} %all-to-all-done.2), kind=kOutput, calls=%fused_computation | output fusion | flops 1048576 | bytes 524288 | tf_op jit(solution)/shard_map/exclusive_scan/reduce_window_sum | solution.py:34
  57.0 3.5 %all-to-all-start.3 = ((f32[16,32,128]{2,1,0:T(8,128)}), f32[16,32,128]{2,1,0:T(8,128)S(1)}, u32[]{:S(2)}, u32[]{:S(2)}) async-start(f32[16,32,128]{2,1,0:T(8,128)} %reduce-window_subtract_fusion), calls=%async_computation.3 | async-start | bytes 524288 | tf_op jit(solution)/shard_map/all_to_all | solution.py:36
  61.0 0.7 copy-done.3
  62.0 0.9 %copy.32 = bf16[256,4,128]{2,1,0:T(4,128)(2,1)} copy(bf16[256,4,128]{2,0,1:T(8,128)(2,1)S(1)} %fusion.35) | data formatting | bytes 524288
  62.9 0.9 %copy.31 = bf16[256,4,128]{2,1,0:T(4,128)(2,1)} copy(bf16[256,4,128]{0,2,1:T(8,128)(2,1)S(1)} %get-tuple-element.15) | data formatting | bytes 524288
  63.7 6.2 %all-to-all-done.3 = f32[16,32,128]{2,1,0:T(8,128)S(1)} async-done(((f32[16,32,128]{2,1,0:T(8,128)}), f32[16,32,128]{2,1,0:T(8,128)S(1)}, u32[]{:S(2)}, u32[]{:S(2)}) %all-to-all-start.3) | async-done | bytes 262176 | tf_op jit(solution)/shard_map/all_to_all | solution.py:36
  72.2 0.9 %copy.34 = bf16[256,4,128]{2,1,0:T(4,128)(2,1)} copy(bf16[256,4,128]{2,0,1:T(8,128)(2,1)S(1)} %pad_maximum_fusion.3) | data formatting | bytes 524288
  74.0 0.7 copy-done.2
  75.0 0.9 %copy.33 = bf16[256,4,128]{2,1,0:T(4,128)(2,1)} copy(bf16[256,4,128]{2,0,1:T(8,128)(2,1)S(1)} %fusion.43) | data formatting | bytes 524288
  (71 shorter events, 10.4 us)
Async XLA Ops:
  0.6 1.2 %copy-start = (bf16[256,4,128]{2,1,0:T(4,128)(2,1)S(1)}, bf16[256,4,128]{2,1,0:T(4,128)(2,1)}, u32[]{:S(2)}) copy-start(bf16[256,4,128]{2,1,0:T(4,128)(2,1)} %param.7) | copy-start | bytes 786436
  3.8 8.5 %copy-start.1 = (bf16[256,4,128]{2,1,0:T(4,128)(2,1)S(1)}, bf16[256,4,128]{2,1,0:T(4,128)(2,1)}, u32[]{:S(2)}) copy-start(bf16[256,4,128]{2,1,0:T(4,128)(2,1)} %param.5) | copy-start | bytes 786436
  3.8 18.3 %all-to-all-start = ((f32[16,32,128]{2,1,0:T(8,128)}), f32[16,32,128]{2,1,0:T(8,128)S(1)}, u32[]{:S(2)}, u32[]{:S(2)}) async-start(f32[16,32,128]{2,1,0:T(8,128)} %bitcast.13), calls=%async_computation | async-start | bytes 524288 | tf_op jit(solution)/shard_map/all_to_all | solution.py:33
  22.8 12.8 %all-to-all-start.1 = ((f32[16,32,128]{2,1,0:T(8,128)}), f32[16,32,128]{2,1,0:T(8,128)S(1)}, u32[]{:S(2)}, u32[]{:S(2)}) async-start(f32[16,32,128]{2,1,0:T(8,128)} %reduce-window_subtract_fusion.1), calls=%async_computation.1 | async-start | bytes 524288 | tf_op jit(solution)/shard_map/all_to_all | solution.py:36
  26.4 1.0 %copy-start.4 = (bf16[256,4,128]{2,1,0:T(4,128)(2,1)S(1)}, bf16[256,4,128]{2,1,0:T(4,128)(2,1)}, u32[]{:S(2)}) copy-start(bf16[256,4,128]{2,1,0:T(4,128)(2,1)} %param.9) | copy-start | bytes 786436
  37.2 0.7 copy-start.5
  38.0 1.2 %collective-permute-start = (f32[2,256]{1,0:T(2,128)S(1)}, f32[2,256]{1,0:T(2,128)S(1)}, u32[]{:S(2)}, u32[]{:S(2)}) collective-permute-start(f32[2,256]{1,0:T(2,128)S(1)} %pad_maximum_fusion.4), channel_id=1, source_target_pairs={{0,1},{1,0},{2,3},{3,2},{4,5},{5,4},{6,7},{7,6},{8,9},{9,8},{10,11... | collective-permute-start | bytes 6152 | tf_op jit(solution)/shard_map/ppermute | solution.py:88
  42.2 14.0 %all-to-all-start.2 = ((f32[16,32,128]{2,1,0:T(8,128)}), f32[16,32,128]{2,1,0:T(8,128)S(1)}, u32[]{:S(2)}, u32[]{:S(2)}) async-start(f32[16,32,128]{2,1,0:T(8,128)} %bitcast.46), calls=%async_computation.2 | async-start | bytes 524288 | tf_op jit(solution)/shard_map/all_to_all | solution.py:33
  57.0 13.0 %all-to-all-start.3 = ((f32[16,32,128]{2,1,0:T(8,128)}), f32[16,32,128]{2,1,0:T(8,128)S(1)}, u32[]{:S(2)}, u32[]{:S(2)}) async-start(f32[16,32,128]{2,1,0:T(8,128)} %reduce-window_subtract_fusion), calls=%async_computation.3 | async-start | bytes 524288 | tf_op jit(solution)/shard_map/all_to_all | solution.py:36
  60.8 0.9 %copy-start.3 = (f32[256,1,128]{2,0,1:T(8,128)S(1)}, f32[256,1,128]{2,0,1:T(8,128)}, u32[]{:S(2)}) copy-start(f32[256,1,128]{2,0,1:T(8,128)} %fusion.15) | copy-start | bytes 393220
  73.8 1.0 %copy-start.2 = (bf16[256,4,128]{2,1,0:T(4,128)(2,1)S(1)}, bf16[256,4,128]{2,1,0:T(4,128)(2,1)}, u32[]{:S(2)}) copy-start(bf16[256,4,128]{2,1,0:T(4,128)(2,1)} %param.6) | copy-start | bytes 786436

commit v5 on v4

--- a/solution.py
+++ b/solution.py
@@ -53,34 +53,42 @@
 def body(query_raw, key_raw, value_raw, out_gain, out_grad):
     tok_rows, head_count, width = query_raw.shape
     blocks = tok_rows // GROUP
-    query_act = jax.nn.silu(query_raw.astype(jnp.float32)).astype(jnp.bfloat16)
-    key_act = jax.nn.silu(key_raw.astype(jnp.float32)).astype(jnp.bfloat16)
-    mask = causal_mask(GROUP)
-    cells = [(c, h) for c in range(blocks) for h in range(head_count)]
+    span = GROUP * head_count
+    flat = (tok_rows * head_count, width)
+    whole = (tok_rows, head_count, width)
+    query_act = jax.nn.silu(query_raw.astype(jnp.float32)).astype(jnp.bfloat16).reshape(flat)
+    key_act = jax.nn.silu(key_raw.astype(jnp.float32)).astype(jnp.bfloat16).reshape(flat)
+    value_2d = value_raw.reshape(flat)
+    row_head = lax.broadcasted_iota(jnp.int32, (span, 1), 0) % head_count
+    rows = lax.broadcasted_iota(jnp.int32, (span, span), 0)
+    cols = lax.broadcasted_iota(jnp.int32, (span, span), 1)
+    mask = (rows % head_count == cols % head_count) & (cols // head_count <= rows // head_count)
 
-    def cut(array, c, h):
-        return array[c * GROUP:(c + 1) * GROUP, h, :]
+    def cut(array, c):
+        return array[c * span:(c + 1) * span]
 
-    def join(parts):
-        rows = [jnp.stack([parts[(c, h)] for h in range(head_count)], axis=1) for c in range(blocks)]
-        return rows[0] if blocks == 1 else jnp.concatenate(rows, axis=0)
+    def per_head(pieces):
+        total = jnp.where(row_head == 0, pieces[0], 0.0)
+        for h in range(1, head_count):
+            total = total + jnp.where(row_head == h, pieces[h], 0.0)
+        return total
 
-    block_kv = jnp.stack([
-        jnp.stack([mm(cut(key_act, c, h), cut(value_raw, c, h), 0, 0) for h in range(head_count)])
-        for c in range(blocks)
-    ])
+    def head_outer(lhs, rhs):
+        return jnp.stack([mm(jnp.where(row_head == h, lhs, 0), rhs, 0, 0) for h in range(head_count)])
+
+    block_kv = jnp.stack([head_outer(cut(key_act, c), cut(value_2d, c)) for c in range(blocks)])
     own_total = jnp.sum(block_kv, axis=0)
     before = lower_sum(own_total)
     state_b = (before[None] + (jnp.cumsum(block_kv, axis=0) - block_kv)).astype(jnp.bfloat16)
-    attn = {}
-    mixed_parts = {}
-    for c, h in cells:
-        scores = mm(cut(query_act, c, h), cut(key_act, c, h), 1, 1)
-        attn[c, h] = jnp.where(mask, scores, 0.0).astype(jnp.bfloat16)
-        mixed_parts[c, h] = mm(attn[c, h], cut(value_raw, c, h), 1, 0) + mm(
-            cut(query_act, c, h), state_b[c, h], 1, 0
-        )
-    mixed = join(mixed_parts)
+    attn = []
+    mixed_rows = []
+    for c in range(blocks):
+        query_c = cut(query_act, c)
+        scores = mm(query_c, cut(key_act, c), 1, 1)
+        attn.append(jnp.where(mask, scores, 0.0).astype(jnp.bfloat16))
+        local = mm(attn[c], cut(value_2d, c), 1, 0)
+        mixed_rows.append(local + per_head([mm(query_c, state_b[c, h], 1, 0) for h in range(head_count)]))
+    mixed = jnp.concatenate(mixed_rows, axis=0).reshape(whole)
     grad_in = out_grad.astype(jnp.float32) * out_gain
     sq_part = jnp.sum(mixed * mixed, axis=(1, 2))
     cross_part = jnp.sum(grad_in * mixed, axis=(1, 2))
@@ -94,25 +102,25 @@
         grad_in * inv_rms[:, None, None]
         - mixed * (cross_total * inv_rms**3 / features)[:, None, None]
     ).astype(jnp.bfloat16)
-    block_grad = jnp.stack([
-        jnp.stack([mm(cut(query_act, c, h), cut(delta, c, h), 0, 0) for h in range(head_count)])
-        for c in range(blocks)
-    ])
+    delta_2d = delta.reshape(flat)
+    block_grad = jnp.stack([head_outer(cut(query_act, c), cut(delta_2d, c)) for c in range(blocks)])
     own_grad = jnp.sum(block_grad, axis=0)
     after = upper_sum(own_grad)
     local_after = lax.cumsum(block_grad, axis=0, reverse=True) - block_grad
     grad_state = (after[None] + local_after).astype(jnp.bfloat16)
-    dq_parts, dk_parts, dv_parts = {}, {}, {}
-    for c, h in cells:
-        delta_c = cut(delta, c, h)
-        value_c = cut(value_raw, c, h)
+    dq_rows, dk_rows, dv_rows = [], [], []
+    for c in range(blocks):
+        query_c, key_c, value_c, delta_c = (cut(a, c) for a in (query_act, key_act, value_2d, delta_2d))
         bscore = jnp.where(mask, mm(delta_c, value_c, 1, 1), 0.0).astype(jnp.bfloat16)
-        dq_parts[c, h] = mm(bscore, cut(key_act, c, h), 1, 0) + mm(delta_c, state_b[c, h], 1, 1)
-        dk_parts[c, h] = mm(bscore, cut(query_act, c, h), 0, 0) + mm(value_c, grad_state[c, h], 1, 1)
-        dv_parts[c, h] = mm(attn[c, h], delta_c, 0, 0) + mm(cut(key_act, c, h), grad_state[c, h], 1, 0)
-    query_grad = (join(dq_parts) * silu_grad(query_raw.astype(jnp.float32))).astype(jnp.bfloat16)
-    key_grad = (join(dk_parts) * silu_grad(key_raw.astype(jnp.float32))).astype(jnp.bfloat16)
-    value_grad = join(dv_parts).astype(jnp.bfloat16)
+        dq_rows.append(mm(bscore, key_c, 1, 0) + per_head([mm(delta_c, state_b[c, h], 1, 1) for h in range(head_count)]))
+        dk_rows.append(mm(bscore, query_c, 0, 0) + per_head([mm(value_c, grad_state[c, h], 1, 1) for h in range(head_count)]))
+        dv_rows.append(mm(attn[c], delta_c, 0, 0) + per_head([mm(key_c, grad_state[c, h], 1, 0) for h in range(head_count)]))
+    dquery = jnp.concatenate(dq_rows, axis=0).reshape(whole)
+    dkey = jnp.concatenate(dk_rows, axis=0).reshape(whole)
+    dvalue = jnp.concatenate(dv_rows, axis=0).reshape(whole)
+    query_grad = (dquery * silu_grad(query_raw.astype(jnp.float32))).astype(jnp.bfloat16)
+    key_grad = (dkey * silu_grad(key_raw.astype(jnp.float32))).astype(jnp.bfloat16)
+    value_grad = dvalue.astype(jnp.bfloat16)
     return (normed_out, query_grad, key_grad, value_grad)
 
 

time: 76.5 us -> 92.2 us (1.21)
  other arithmetic: 5.15 us -> 19.8 us
  matrix products: 9.92 us -> 17.5 us
  local copies, waits for them, and re-layouts: 6.83 us -> 2.85 us
  waiting for transfers between devices: 33.7 us -> 30.4 us
    dot_general x48 -> x30, matrix products: 9.92 us -> 17.5 us  [mm(): return lax.dot_general(lhs, rhs, dims, preferred_element_type=jnp.float32)]
    unnamed x17 -> x58, local copies, waits for them, and re-layouts: 6.41 us -> 1.38 us
    select_n x0 -> x2, other arithmetic: none -> 4.57 us  [head_outer(): jnp.where(row_head == h, lhs, 0)]
    all_to_all x2, waiting for transfers between devices: 18.7 us -> 15.8 us  [exclusive_scan(): lax.all_to_all(rows.reshape(count, chunk, width), 'seq', 0, 0, tiled=True)]
    convert_element_type x1, other arithmetic: 0.18 us -> 2.66 us  [body(): delta = (grad_in * inv_rms[:, None, None] - mixed * (cross_total * inv_rm...]
    reduce_sum x0 -> x1, other arithmetic: none -> 1.98 us  [body(): cross_part = jnp.sum(grad_in * mixed, axis=(1, 2))]
    convert_element_type x4 -> x2, other arithmetic: 1.7 us -> 3.31 us  [the longest x1 2.21 us: body(): (dquery * silu_grad(query_raw.astype(jnp.float32))).astype(jnp.bfloat16)]
    reduce_sum x0 -> x1, local copies, waits for them, and re-layouts: none -> 1.47 us  [body(): sq_part = jnp.sum(mixed * mixed, axis=(1, 2))]
  transfers between devices with their start and end apart: 5 -> 5, of which waited for: 5 -> 5; matrix products, arithmetic and copies ran while one was open for 6% -> 9% of each run, Pallas kernels for 0% -> 0%
where the time goes in v5:
time: 92.2 us; the launch traced here: 91.4 us
  waiting for transfers between devices  30.4 us (33%)
  other arithmetic  19.8 us (21%)
  starting transfers between devices  19.8 us (21%)
  matrix products  17.5 us (19%)
  local copies, waits for them, and re-layouts  2.85 us (3%)
  between operations  1.16 us (1%)
    dot_general x30, matrix products, mm(): return lax.dot_general(lhs, rhs, dims, preferred_element_type=jnp.float32)  17.5 us
    all_to_all x2, waiting for transfers between devices, exclusive_scan(): lax.all_to_all(rows.reshape(count, chunk, width), 'seq', 0, 0, tiled=True)  15.8 us
    all_to_all x2, waiting for transfers between devices, exclusive_scan(): spread = lax.all_to_all(prefix, 'seq', 0, 0, tiled=True)  13.4 us
    all_to_all x2, starting transfers between devices, exclusive_scan(): lax.all_to_all(rows.reshape(count, chunk, width), 'seq', 0, 0, tiled=True)  11.9 us
    all_to_all x2, starting transfers between devices, exclusive_scan(): spread = lax.all_to_all(prefix, 'seq', 0, 0, tiled=True)  7.92 us
    select_n x2, other arithmetic, head_outer(): jnp.where(row_head == h, lhs, 0)  4.57 us
    convert_element_type x1, other arithmetic, body(): delta = (grad_in * inv_rms[:, None, None] - mixed * (cross_total * inv_rm...  2.66 us
    convert_element_type x1, other arithmetic, body(): (dquery * silu_grad(query_raw.astype(jnp.float32))).astype(jnp.bfloat16)  2.21 us
  transfers between devices with their start and end apart: 5, of which 5 were waited for; matrix products, arithmetic and copies ran while one was open for 9% of the time, Pallas kernels for 0%

profile of v5, /device:TPU:0, one launch (start us, length us, event | category | flops | bytes accessed | tf_op | source)
XLA Modules:
  0.0 91.4 jit_solution(15631214147215304411)
XLA Ops:
  0.9 2.4 %broadcast_select_fusion.7 = (bf16[256,4,128]{2,1,0:T(4,128)(2,1)S(1)}, bf16[256,4,128]{2,1,0:T(4,128)(2,1)S(1)}, bf16[256,4,128]{2,1,0:T(4,128)(2,1)}, bf16[256,4,128]{2,1,0:T(4,128)(2,1)S(1)}) fusion(pred[256,4]{1,0:T(8,128)(4,1)S(1)} %fusion.68, bf16[256,4,128]{2,1,0:T(4,128)(2,1)} %param.6, bf16[256,4,128]{2,1,0:T(4,128)(2,1)} %param.5), kind=kLoop, calls=%fused_computation.99 | loop fusion | flops 1835008 | bytes 1573888 | tf_op jit(solution)/shard_map/jit(_where)/select_n | solution.py:77
  3.3 2.2 %broadcast_select_fusion.5 = (bf16[256,4,128]{2,1,0:T(4,128)(2,1)S(1)}, bf16[256,4,128]{2,1,0:T(4,128)(2,1)S(1)}, bf16[256,4,128]{2,1,0:T(4,128)(2,1)S(1)}, bf16...) fusion(bf16[256,4,128]{2,1,0:T(4,128)(2,1)S(1)} %get-tuple-element.7, ...), kind=kLoop, calls=%fused_computation.97 | loop fusion | flops 786432 | bytes 2100224 | tf_op jit(solution)/shard_map/jit(_where)/select_n | solution.py:77
  7.3 8.3 %all-to-all-start = ((f32[16,32,128]{2,1,0:T(8,128)}), f32[16,32,128]{2,1,0:T(8,128)S(1)}, u32[]{:S(2)}, u32[]{:S(2)}) async-start(f32[16,32,128]{2,1,0:T(8,128)} %bitcast.11), calls=%async_computation | async-start | bytes 524288 | tf_op jit(solution)/shard_map/all_to_all | solution.py:33
  16.3 1.5 %select_convert_fusion.1 = bf16[1024,1024]{1,0:T(8,128)(2,1)S(1)} fusion(bf16[1024,128]{1,0:T(8,128)(2,1)S(1)} %bitcast.128, bf16[1024,128]{1,0:T(8,128)(2,1)S(1)} %bitcast.122, s32[1024]{0:T(1024)S(1)} %get-tuple-element.25, s32[1024]{0:T(1024)S(1)} %get-tuple-element.28, pred[1024]{0:T(1024)(128)(4,1)S(1)} %get-tuple-element.29, ...), kind=kOutput, calls=%fused_computation.1 | convolution fusion | flops 277872640 | bytes 2639872 | tf_op jit(solution)/shard_map/dot_general | solution.py:50
  17.8 7.6 %all-to-all-done = f32[16,32,128]{2,1,0:T(8,128)S(1)} async-done(((f32[16,32,128]{2,1,0:T(8,128)}), f32[16,32,128]{2,1,0:T(8,128)S(1)}, u32[]{:S(2)}, u32[]{:S(2)}) %all-to-all-start) | async-done | bytes 262176 | tf_op jit(solution)/shard_map/all_to_all | solution.py:33
  26.2 3.5 %all-to-all-start.1 = ((f32[16,32,128]{2,1,0:T(8,128)}), f32[16,32,128]{2,1,0:T(8,128)S(1)}, u32[]{:S(2)}, u32[]{:S(2)}) async-start(f32[16,32,128]{2,1,0:T(8,128)} %reduce-window_subtract_fusion.1), calls=%async_computation.1 | async-start | bytes 524288 | tf_op jit(solution)/shard_map/all_to_all | solution.py:36
  29.8 1.5 %fusion.85 = f32[1024,128]{1,0:T(8,128)} fusion(bf16[1024,1024]{1,0:T(8,128)(2,1)S(1)} %select_convert_fusion.1, bf16[1024,128]{1,0:T(8,128)(2,1)S(1)} %bitcast.116), kind=kOutput, calls=%fused_computation.149 | convolution fusion | flops 268435456 | bytes 2883584 | tf_op jit(solution)/shard_map/dot_general | solution.py:50
  31.3 7.7 %all-to-all-done.1 = f32[16,32,128]{2,1,0:T(8,128)S(1)} async-done(((f32[16,32,128]{2,1,0:T(8,128)}), f32[16,32,128]{2,1,0:T(8,128)S(1)}, u32[]{:S(2)}, u32[]{:S(2)}) %all-to-all-start.1) | async-done | bytes 262176 | tf_op jit(solution)/shard_map/all_to_all | solution.py:36
  41.0 1.5 %reduce_sum.34 = f32[256,4]{1,0:T(8,128)} reshape(f32[1024]{0:T(1024)} %get-tuple-element.23) | data formatting | bytes 8192 | tf_op jit(solution)/shard_map/reduce_sum | solution.py:93
  42.5 1.6 %reduce_sum.35 = f32[256]{0:T(256)} reduce(f32[256,4]{1,0:T(8,128)} %reduce_sum.34, f32[]{:T(128)} %constant.81.clone.1), dimensions={1}, to_apply=%region_2.3 | reduce | flops 768 | bytes 5124 | tf_op jit(solution)/shard_map/reduce_sum | solution.py:93
  44.1 2.0 %multiply_reduce_fusion = f32[256]{0:T(256)S(1)} fusion(f32[256,4,128]{2,1,0:T(4,128)S(1)} %bitcast.140, bf16[256,4,128]{2,1,0:T(4,128)(2,1)} %param.9, f32[4,128]{1,0:T(4,128)} %param.8), kind=kLoop, calls=%fused_computation.65 | loop fusion | flops 524032 | bytes 789504 | tf_op jit(solution)/shard_map/reduce_sum | solution.py:94
  46.8 1.2 %collective-permute-done = f32[2,256]{1,0:T(2,128)S(1)} collective-permute-done((f32[2,256]{1,0:T(2,128)S(1)}, f32[2,256]{1,0:T(2,128)S(1)}, u32[]{:S(2)}, u32[]{:S(2)}) %collective-permute-start) | collective-permute-done | bytes 2080 | tf_op jit(solution)/shard_map/ppermute | solution.py:96
  48.6 2.7 %subtract_convert_fusion = (bf16[256,4,128]{2,1,0:T(4,128)(2,1)S(1)}, bf16[256,4,128]{2,1,0:T(4,128)(2,1)}) fusion(f32[256,4,128]{2,1,0:T(4,128)} %bitcast.141, bf16[256,4,128]{2,1,0:T(4,128)(2,1)} %param.9, f32[256]{0:T(256)S(1)} %fusion.78, f32[256]{0:T(256)S(1)} %bitcast.164, f32[4,128]{1,0:T(4,128)} %param.8), kind=kLoop, calls=%fused_computation.63 | loop fusion | flops 1179648 | bytes 1314816 | tf_op jit(solution)/shard_map/convert_element_type | solution.py:104
  51.3 1.5 %fusion.88 = f32[1024,128]{1,0:T(8,128)} fusion(bf16[1024,1024]{1,0:T(8,128)(2,1)S(1)} %select_convert_fusion.1, bf16[1024,128]{1,0:T(8,128)(2,1)S(1)} %bitcast.134), kind=kOutput, calls=%fused_computation.152 | convolution fusion | flops 268435456 | bytes 2883584 | tf_op jit(solution)/shard_map/dot_general | solution.py:50
  52.9 1.5 %select_convert_fusion = bf16[1024,1024]{1,0:T(8,128)(2,1)S(1)} fusion(bf16[1024,128]{1,0:T(8,128)(2,1)S(1)} %bitcast.135, bf16[1024,128]{1,0:T(8,128)(2,1)S(1)} %bitcast.117, s32[1024]{0:T(1024)S(1)} %copy-done.18, s32[1024]{0:T(1024)S(1)} %copy-done.24, pred[1024]{0:T(1024)(128)(4,1)S(1)} %copy-done.26, s32[1024]{0:T(1024)S(1)} %copy-done.20, ...), kind=kOutput, calls=%fused_computation | convolution fusion | flops 277872640 | bytes 2639872 | tf_op jit(solution)/shard_map/dot_general | solution.py:50
  54.5 1.0 %convolution_select_fusion.10 = f32[1024,128]{1,0:T(8,128)} fusion(bf16[1024,128]{1,0:T(8,128)(2,1)S(1)} %bitcast.136, pred[1024]{0:T(1024)(128)(4,1)S(1)} %broadcast_compare_fusion.1, bf16[1,4,128,128]{3,2,1,0:T(8,128)(2,1)S(1)} %fusion.36), kind=kOutput, calls=%fused_computation.15 | convolution fusion | flops 33685504 | bytes 820224 | tf_op jit(solution)/shard_map/dot_general | solution.py:50
  55.6 1.1 %convolution_select_fusion.9 = f32[1024,128]{1,0:T(8,128)} fusion(bf16[1024,128]{1,0:T(8,128)(2,1)S(1)} %bitcast.137, pred[1024]{0:T(1024)(128)(4,1)S(1)} %broadcast_compare_fusion, bf16[1,4,128,128]{3,2,1,0:T(8,128)(2,1)S(1)} %fusion.36), kind=kOutput, calls=%fused_computation.14 | convolution fusion | flops 33685504 | bytes 820224 | tf_op jit(solution)/shard_map/dot_general | solution.py:50
  58.5 3.6 %all-to-all-start.2 = ((f32[16,32,128]{2,1,0:T(8,128)}), f32[16,32,128]{2,1,0:T(8,128)S(1)}, u32[]{:S(2)}, u32[]{:S(2)}) async-start(f32[16,32,128]{2,1,0:T(8,128)} %bitcast.145), calls=%async_computation.2 | async-start | bytes 524288 | tf_op jit(solution)/shard_map/all_to_all | solution.py:33
  63.3 1.1 %fusion.16 = f32[1024,128]{1,0:T(8,128)} fusion(f32[1024,128]{1,0:T(8,128)S(1)} %fusion.86, f32[1024,128]{1,0:T(8,128)S(1)} %convolution_select_fusion.8, f32[1024,128]{1,0:T(8,128)S(1)} %copy-done.4, f32[1024,128]{1,0:T(8,128)S(1)} %copy-done.3, bf16[1024,128]{1,0:T(8,128)(2,1)S(1)} %bitcast.139, pred[1024]{0:T(1024)(128)(4,1)S(1)} %broadcast_compare_fusion.2, ...), kind=kOutput, calls=%fused_computation.36 | convolution fusion | flops 34209792 | bytes 2917376 | tf_op jit(solution)/shard_map/dot_general | solution.py:50
  64.4 8.1 %all-to-all-done.2 = f32[16,32,128]{2,1,0:T(8,128)S(1)} async-done(((f32[16,32,128]{2,1,0:T(8,128)}), f32[16,32,128]{2,1,0:T(8,128)S(1)}, u32[]{:S(2)}, u32[]{:S(2)}) %all-to-all-start.2) | async-done | bytes 262176 | tf_op jit(solution)/shard_map/all_to_all | solution.py:33
  73.3 4.4 %all-to-all-start.3 = ((f32[16,32,128]{2,1,0:T(8,128)}), f32[16,32,128]{2,1,0:T(8,128)}, u32[]{:S(2)}, u32[]{:S(2)}) async-start(f32[16,32,128]{2,1,0:T(8,128)} %reduce-window_subtract_fusion), calls=%async_computation.3 | async-start | bytes 524288 | tf_op jit(solution)/shard_map/all_to_all | solution.py:36
  77.7 2.2 %fusion.26 = bf16[256,4,128]{2,1,0:T(4,128)(2,1)} fusion(f32[256,4,128]{2,1,0:T(4,128)} %bitcast.142, bf16[256,4,128]{2,1,0:T(4,128)(2,1)} %param.5), kind=kLoop, calls=%fused_computation.54 | loop fusion | flops 1310720 | bytes 1048576 | tf_op jit(solution)/shard_map/convert_element_type | solution.py:121
  80.6 5.8 %all-to-all-done.3 = f32[16,32,128]{2,1,0:T(8,128)} async-done(((f32[16,32,128]{2,1,0:T(8,128)}), f32[16,32,128]{2,1,0:T(8,128)}, u32[]{:S(2)}, u32[]{:S(2)}) %all-to-all-start.3) | async-done | bytes 262176 | tf_op jit(solution)/shard_map/all_to_all | solution.py:36
  89.3 1.1 %fusion.34 = bf16[256,4,128]{2,1,0:T(4,128)(2,1)} fusion(f32[256,4,128]{2,1,0:T(4,128)S(1)} %bitcast.143, bf16[256,4,128]{2,1,0:T(4,128)(2,1)S(1)} %copy-done.6), kind=kLoop, calls=%fused_computation.62 | loop fusion | flops 1310720 | bytes 1048576 | tf_op jit(solution)/shard_map/convert_element_type | solution.py:122
  (102 shorter events, 15.2 us)
Async XLA Ops:
  0.6 4.8 %copy-start = (bf16[256,4,128]{2,1,0:T(4,128)(2,1)S(1)}, bf16[256,4,128]{2,1,0:T(4,128)(2,1)}, u32[]{:S(2)}) copy-start(bf16[256,4,128]{2,1,0:T(4,128)(2,1)} %param.7) | copy-start | bytes 786436
  7.3 18.2 %all-to-all-start = ((f32[16,32,128]{2,1,0:T(8,128)}), f32[16,32,128]{2,1,0:T(8,128)S(1)}, u32[]{:S(2)}, u32[]{:S(2)}) async-start(f32[16,32,128]{2,1,0:T(8,128)} %bitcast.11), calls=%async_computation | async-start | bytes 524288 | tf_op jit(solution)/shard_map/all_to_all | solution.py:33
  15.6 2.2 %copy-start.17 = (s32[1024]{0:T(1024)}, s32[1024]{0:T(1024)S(1)}, u32[]{:S(2)}) copy-start(s32[1024]{0:T(1024)S(1)} %get-tuple-element.25) | copy-start | bytes 12292
  26.2 12.8 %all-to-all-start.1 = ((f32[16,32,128]{2,1,0:T(8,128)}), f32[16,32,128]{2,1,0:T(8,128)S(1)}, u32[]{:S(2)}, u32[]{:S(2)}) async-start(f32[16,32,128]{2,1,0:T(8,128)} %reduce-window_subtract_fusion.1), calls=%async_computation.1 | async-start | bytes 524288 | tf_op jit(solution)/shard_map/all_to_all | solution.py:36
  41.0 7.6 %copy-start.1 = (f32[1024,128]{1,0:T(8,128)}, f32[1024,128]{1,0:T(8,128)S(1)}, u32[]{:S(2)}) copy-start(f32[1024,128]{1,0:T(8,128)S(1)} %get-tuple-element.24) | copy-start | bytes 1572868
  46.8 1.2 %collective-permute-start = (f32[2,256]{1,0:T(2,128)S(1)}, f32[2,256]{1,0:T(2,128)S(1)}, u32[]{:S(2)}, u32[]{:S(2)}) collective-permute-start(f32[2,256]{1,0:T(2,128)S(1)} %pad_maximum_fusion.2), channel_id=1, source_target_pairs={{0,1},{1,0},{2,3},{3,2},{4,5},{5,4},{6,7},{7,6},{8,9},{9,8},{10,11... | collective-permute-start | bytes 6152 | tf_op jit(solution)/shard_map/ppermute | solution.py:96
  51.3 1.6 %copy-start.18 = (s32[1024]{0:T(1024)S(1)}, s32[1024]{0:T(1024)}, u32[]{:S(2)}) copy-start(s32[1024]{0:T(1024)} %copy-done.17) | copy-start | bytes 12292
  51.3 1.6 %copy-start.20 = (s32[1024]{0:T(1024)S(1)}, s32[1024]{0:T(1024)}, u32[]{:S(2)}) copy-start(s32[1024]{0:T(1024)} %copy-done.19) | copy-start | bytes 12292
  51.3 1.6 %copy-start.22 = (s32[1024]{0:T(1024)S(1)}, s32[1024]{0:T(1024)}, u32[]{:S(2)}) copy-start(s32[1024]{0:T(1024)} %copy-done.21) | copy-start | bytes 12292
  51.3 1.6 %copy-start.24 = (s32[1024]{0:T(1024)S(1)}, s32[1024]{0:T(1024)}, u32[]{:S(2)}) copy-start(s32[1024]{0:T(1024)} %copy-done.23) | copy-start | bytes 12292
  51.3 1.6 %copy-start.26 = (pred[1024]{0:T(1024)(128)(4,1)S(1)}, pred[1024]{0:T(1024)(128)(4,1)}, u32[]{:S(2)}) copy-start(pred[1024]{0:T(1024)(128)(4,1)} %copy-done.25) | copy-start | bytes 3076
  51.3 1.6 %copy-start.28 = (pred[1024]{0:T(1024)(128)(4,1)S(1)}, pred[1024]{0:T(1024)(128)(4,1)}, u32[]{:S(2)}) copy-start(pred[1024]{0:T(1024)(128)(4,1)} %copy-done.27) | copy-start | bytes 3076
  52.9 3.7 %copy-start.10 = (bf16[256,4,128]{2,1,0:T(4,128)(2,1)S(1)}, bf16[256,4,128]{2,1,0:T(4,128)(2,1)}, u32[]{:S(2)}) copy-start(bf16[256,4,128]{2,1,0:T(4,128)(2,1)} %get-tuple-element.18) | copy-start | bytes 786436
  54.5 2.4 %copy-start.9 = (bf16[256,4,128]{2,1,0:T(4,128)(2,1)S(1)}, bf16[256,4,128]{2,1,0:T(4,128)(2,1)}, u32[]{:S(2)}) copy-start(bf16[256,4,128]{2,1,0:T(4,128)(2,1)} %get-tuple-element.17) | copy-start | bytes 786436
  54.5 2.7 %copy-start.8 = (bf16[256,4,128]{2,1,0:T(4,128)(2,1)S(1)}, bf16[256,4,128]{2,1,0:T(4,128)(2,1)}, u32[]{:S(2)}) copy-start(bf16[256,4,128]{2,1,0:T(4,128)(2,1)} %get-tuple-element.16) | copy-start | bytes 786436
  54.5 3.0 %copy-start.7 = (bf16[256,4,128]{2,1,0:T(4,128)(2,1)S(1)}, bf16[256,4,128]{2,1,0:T(4,128)(2,1)}, u32[]{:S(2)}) copy-start(bf16[256,4,128]{2,1,0:T(4,128)(2,1)} %get-tuple-element.19) | copy-start | bytes 786436
  57.2 1.3 %copy-start.13 = (f32[128,128,1]{1,0,2:T(8,128)}, f32[128,128,1]{1,0,2:T(8,128)S(1)}, u32[]{:S(2)}) copy-start(f32[128,128,1]{1,0,2:T(8,128)S(1)} %fusion.41) | copy-start | bytes 196612
  57.5 1.0 %copy-start.15 = (f32[128,128,1]{1,0,2:T(8,128)}, f32[128,128,1]{1,0,2:T(8,128)S(1)}, u32[]{:S(2)}) copy-start(f32[128,128,1]{1,0,2:T(8,128)S(1)} %fusion.39) | copy-start | bytes 196612
  58.5 14.0 %all-to-all-start.2 = ((f32[16,32,128]{2,1,0:T(8,128)}), f32[16,32,128]{2,1,0:T(8,128)S(1)}, u32[]{:S(2)}, u32[]{:S(2)}) async-start(f32[16,32,128]{2,1,0:T(8,128)} %bitcast.145), calls=%async_computation.2 | async-start | bytes 524288 | tf_op jit(solution)/shard_map/all_to_all | solution.py:33
  62.1 1.2 %copy-start.4 = (f32[1024,128]{1,0:T(8,128)S(1)}, f32[1024,128]{1,0:T(8,128)}, u32[]{:S(2)}) copy-start(f32[1024,128]{1,0:T(8,128)} %convolution_select_fusion.9) | copy-start | bytes 1572868
  73.3 13.1 %all-to-all-start.3 = ((f32[16,32,128]{2,1,0:T(8,128)}), f32[16,32,128]{2,1,0:T(8,128)}, u32[]{:S(2)}, u32[]{:S(2)}) async-start(f32[16,32,128]{2,1,0:T(8,128)} %reduce-window_subtract_fusion), calls=%async_computation.3 | async-start | bytes 524288 | tf_op jit(solution)/shard_map/all_to_all | solution.py:36
  79.9 6.5 %copy-start.12 = (f32[128,128,1]{1,0,2:T(8,128)S(1)}, f32[128,128,1]{1,0,2:T(8,128)}, u32[]{:S(2)}) copy-start(f32[128,128,1]{1,0,2:T(8,128)} %copy-done.11) | copy-start | bytes 196612
  79.9 6.5 %copy-start.14 = (f32[128,128,1]{1,0,2:T(8,128)S(1)}, f32[128,128,1]{1,0,2:T(8,128)}, u32[]{:S(2)}) copy-start(f32[128,128,1]{1,0,2:T(8,128)} %copy-done.13) | copy-start | bytes 196612
  88.9 1.6 %copy-start.2 = (f32[1024,128]{1,0:T(8,128)S(1)}, f32[1024,128]{1,0:T(8,128)}, u32[]{:S(2)}) copy-start(f32[1024,128]{1,0:T(8,128)} %fusion.88) | copy-start | bytes 1572868
  (10 other events, 7.6 us)

commit v6 on v2

--- a/solution.py
+++ b/solution.py
@@ -56,12 +56,15 @@
     block_kv = jnp.einsum("cshd,cshe->chde", key_act, value_blk, preferred_element_type=jnp.float32)
     own_total = jnp.sum(block_kv, axis=0)
     before = lower_sum(own_total)
-    state_b = (before[None] + (jnp.cumsum(block_kv, axis=0) - block_kv)).astype(jnp.bfloat16)
+    if blocks == 1:
+        state_b = before[None]
+    else:
+        state_b = before[None] + (jnp.cumsum(block_kv, axis=0) - block_kv)
     scores = jnp.einsum("cthd,cshd->chts", query_act, key_act, preferred_element_type=jnp.float32)
     attn = jnp.where(mask, scores, 0.0).astype(jnp.bfloat16)
     mixed = jnp.einsum("chts,cshe->cthe", attn, value_blk, preferred_element_type=jnp.float32)
     mixed = mixed + jnp.einsum(
-        "cthd,chde->cthe", query_act, state_b, preferred_element_type=jnp.float32
+        "cthd,chde->cthe", query_act, state_b, preferred_element_type=jnp.float32, precision=lax.Precision.HIGHEST
     )
     mixed = mixed.reshape(tok_rows, head_count, width)
     grad_in = out_grad.astype(jnp.float32) * out_gain
@@ -83,21 +86,23 @@
     )
     own_grad = jnp.sum(block_grad, axis=0)
     after = upper_sum(own_grad)
-    local_after = jnp.flip(jnp.cumsum(jnp.flip(block_grad, 0), axis=0), 0) - block_grad
-    grad_state = (after[None] + local_after).astype(jnp.bfloat16)
+    if blocks == 1:
+        grad_state = after[None]
+    else:
+        grad_state = after[None] + (lax.cumsum(block_grad, axis=0, reverse=True) - block_grad)
     bscore = jnp.einsum("cthe,cshe->chts", delta_blk, value_blk, preferred_element_type=jnp.float32)
     bscore = jnp.where(mask, bscore, 0.0).astype(jnp.bfloat16)
     dquery = jnp.einsum("chts,cshd->cthd", bscore, key_act, preferred_element_type=jnp.float32)
     dquery = dquery + jnp.einsum(
-        "cthe,chde->cthd", delta_blk, state_b, preferred_element_type=jnp.float32
+        "cthe,chde->cthd", delta_blk, state_b, preferred_element_type=jnp.float32, precision=lax.Precision.HIGHEST
     )
     dkey = jnp.einsum("chts,cthd->cshd", bscore, query_act, preferred_element_type=jnp.float32)
     dkey = dkey + jnp.einsum(
-        "cshe,chde->cshd", value_blk, grad_state, preferred_element_type=jnp.float32
+        "cshe,chde->cshd", value_blk, grad_state, preferred_element_type=jnp.float32, precision=lax.Precision.HIGHEST
     )
     dvalue = jnp.einsum("chts,cthe->cshe", attn, delta_blk, preferred_element_type=jnp.float32)
     dvalue = dvalue + jnp.einsum(
-        "cshd,chde->cshe", key_act, grad_state, preferred_element_type=jnp.float32
+        "cshd,chde->cshe", key_act, grad_state, preferred_element_type=jnp.float32, precision=lax.Precision.HIGHEST
     )
     whole = (tok_rows, head_count, width)
     query_grad = (dquery.reshape(whole) * silu_grad(query_raw.astype(jnp.float32))).astype(

time: 71.4 us -> 70 us (0.980)
  other arithmetic: 3.73 us -> 1.76 us
  matrix products: 5.22 us -> 6.03 us
    convert_element_type x2 -> x0, other arithmetic: 1.98 us -> none  [the longest x1 0.99 us: body(): (before[None] + (jnp.cumsum(block_kv, axis=0) - block_kv)).astype(jnp.bfl...]
where the time goes in v6:
time: 70 us; the launch traced here: 69.3 us
  waiting for transfers between devices  35.8 us (51%)
  starting transfers between devices  19.1 us (27%)
  matrix products  6.03 us (9%)
  local copies, waits for them, and re-layouts  5.75 us (8%)
  other arithmetic  1.76 us (3%)
  between operations  0.82 us (1%)
    all_to_all x2, waiting for transfers between devices, exclusive_scan(): lax.all_to_all(rows.reshape(count, chunk, width), 'seq', 0, 0, tiled=True)  17.4 us
    all_to_all x2, waiting for transfers between devices, exclusive_scan(): spread = lax.all_to_all(prefix, 'seq', 0, 0, tiled=True)  17.3 us
    all_to_all x2, starting transfers between devices, exclusive_scan(): lax.all_to_all(rows.reshape(count, chunk, width), 'seq', 0, 0, tiled=True)  12 us
    all_to_all x2, starting transfers between devices, exclusive_scan(): spread = lax.all_to_all(prefix, 'seq', 0, 0, tiled=True)  7.08 us
    unnamed x15, local copies, waits for them, and re-layouts  5.75 us
    another operation x2, other arithmetic, exclusive_scan(): inclusive = lax.cumsum(gathered, axis=0, reverse=reverse)  1.51 us
  transfers between devices with their start and end apart: 5, of which 5 were waited for; matrix products, arithmetic and copies ran while one was open for 5% of the time, Pallas kernels for 0%

profile of v6, /device:TPU:0, one launch (start us, length us, event | category | flops | bytes accessed | tf_op | source)
XLA Modules:
  0.0 69.3 jit_solution(14713788080288490868)
XLA Ops:
  0.6 1.1 %copy.30 = bf16[256,4,128]{0,2,1:T(8,128)(2,1)S(1)} copy(bf16[256,4,128]{2,1,0:T(4,128)(2,1)} %param.6) | data formatting | bytes 524288 | tf_op args[1]
  1.8 1.0 %fusion.26 = f32[4,128,128]{2,1,0:T(8,128)} fusion(bf16[256,4,128]{2,1,0:T(4,128)(2,1)S(1)} %copy-done, bf16[256,4,128]{0,2,1:T(8,128)(2,1)S(1)} %copy.30), kind=kOutput, calls=%fused_computation.47 | convolution fusion | flops 34340864 | bytes 786432 | tf_op jit(solution)/shard_map/cshd,cshe->chde/dot_general | solution.py:56
  2.8 8.4 %all-to-all-start = ((f32[16,32,128]{2,1,0:T(8,128)}), f32[16,32,128]{2,1,0:T(8,128)S(1)}, u32[]{:S(2)}, u32[]{:S(2)}) async-start(f32[16,32,128]{2,1,0:T(8,128)} %bitcast.1), calls=%async_computation | async-start | bytes 524288 | tf_op jit(solution)/shard_map/all_to_all | solution.py:33
  11.4 0.8 %copy-done.2 = bf16[256,4,128]{2,1,0:T(4,128)(2,1)S(1)} copy-done((bf16[256,4,128]{2,1,0:T(4,128)(2,1)S(1)}, bf16[256,4,128]{2,1,0:T(4,128)(2,1)}, u32[]{:S(2)}) %copy-start.2) | copy-done | bytes 262168
  12.4 8.7 %all-to-all-done = f32[16,32,128]{2,1,0:T(8,128)S(1)} async-done(((f32[16,32,128]{2,1,0:T(8,128)}), f32[16,32,128]{2,1,0:T(8,128)S(1)}, u32[]{:S(2)}, u32[]{:S(2)}) %all-to-all-start) | async-done | bytes 262176 | tf_op jit(solution)/shard_map/all_to_all | solution.py:33
  21.1 0.7 %reduce-window_subtract_fusion.1 = f32[16,32,128]{2,1,0:T(8,128)} fusion(f32[16,32,128]{2,1,0:T(8,128)S(1)} %all-to-all-done), kind=kOutput, calls=%fused_computation.18 | output fusion | flops 1048576 | bytes 524288 | tf_op jit(solution)/shard_map/exclusive_scan/reduce_window_sum | solution.py:34
  21.8 3.5 %all-to-all-start.1 = ((f32[16,32,128]{2,1,0:T(8,128)}), f32[16,32,128]{2,1,0:T(8,128)S(1)}, u32[]{:S(2)}, u32[]{:S(2)}) async-start(f32[16,32,128]{2,1,0:T(8,128)} %reduce-window_subtract_fusion.1), calls=%async_computation.1 | async-start | bytes 524288 | tf_op jit(solution)/shard_map/all_to_all | solution.py:36
  25.4 0.5 fusion
  26.2 8.4 %all-to-all-done.1 = f32[16,32,128]{2,1,0:T(8,128)S(1)} async-done(((f32[16,32,128]{2,1,0:T(8,128)}), f32[16,32,128]{2,1,0:T(8,128)S(1)}, u32[]{:S(2)}, u32[]{:S(2)}) %all-to-all-start.1) | async-done | bytes 262176 | tf_op jit(solution)/shard_map/all_to_all | solution.py:36
  34.6 0.6 multiply_reduce_fusion.1
  35.3 1.1 %collective-permute-done = f32[2,256]{1,0:T(2,128)S(1)} collective-permute-done((f32[2,256]{1,0:T(2,128)S(1)}, f32[2,256]{1,0:T(2,128)S(1)}, u32[]{:S(2)}, u32[]{:S(2)}) %collective-permute-start) | collective-permute-done | bytes 2080 | tf_op jit(solution)/shard_map/ppermute | solution.py:74
  36.7 1.0 %fusion.38 = f32[4,128,128]{2,1,0:T(8,128)} fusion(bf16[256,4,128]{0,2,1:T(8,128)(2,1)S(1)} %get-tuple-element.14, bf16[256,4,128]{0,2,1:T(8,128)(2,1)S(1)} %copy.29), kind=kOutput, calls=%fused_computation.58 | convolution fusion | flops 34340864 | bytes 786432 | tf_op jit(solution)/shard_map/cthd,cthe->chde/dot_general | solution.py:84
  38.0 0.9 %copy.45 = bf16[256,4,128]{2,1,0:T(4,128)(2,1)} copy(bf16[256,4,128]{0,2,1:T(8,128)(2,1)S(1)} %get-tuple-element.15) | data formatting | bytes 524288
  38.9 3.5 %all-to-all-start.2 = ((f32[16,32,128]{2,1,0:T(8,128)}), f32[16,32,128]{2,1,0:T(8,128)S(1)}, u32[]{:S(2)}, u32[]{:S(2)}) async-start(f32[16,32,128]{2,1,0:T(8,128)} %bitcast.15), calls=%async_computation.2 | async-start | bytes 524288 | tf_op jit(solution)/shard_map/all_to_all | solution.py:33
  42.7 0.5 fusion.7
  43.2 0.9 %copy.46 = bf16[256,4,128]{2,1,0:T(4,128)(2,1)} copy(bf16[256,4,128]{0,2,1:T(8,128)(2,1)S(1)} %fusion.7) | data formatting | bytes 524288
  44.1 8.7 %all-to-all-done.2 = f32[16,32,128]{2,1,0:T(8,128)S(1)} async-done(((f32[16,32,128]{2,1,0:T(8,128)}), f32[16,32,128]{2,1,0:T(8,128)S(1)}, u32[]{:S(2)}, u32[]{:S(2)}) %all-to-all-start.2) | async-done | bytes 262176 | tf_op jit(solution)/shard_map/all_to_all | solution.py:33
  52.8 0.8 %reduce-window_subtract_fusion = f32[16,32,128]{2,1,0:T(8,128)} fusion(f32[16,32,128]{2,1,0:T(8,128)S(1)} %all-to-all-done.2), kind=kOutput, calls=%fused_computation.17 | output fusion | flops 1048576 | bytes 524288 | tf_op jit(solution)/shard_map/exclusive_scan/reduce_window_sum | solution.py:34
  53.6 3.5 %all-to-all-start.3 = ((f32[16,32,128]{2,1,0:T(8,128)}), f32[16,32,128]{2,1,0:T(8,128)S(1)}, u32[]{:S(2)}, u32[]{:S(2)}) async-start(f32[16,32,128]{2,1,0:T(8,128)} %reduce-window_subtract_fusion), calls=%async_computation.3 | async-start | bytes 524288 | tf_op jit(solution)/shard_map/all_to_all | solution.py:36
  57.7 8.9 %all-to-all-done.3 = f32[16,32,128]{2,1,0:T(8,128)S(1)} async-done(((f32[16,32,128]{2,1,0:T(8,128)}), f32[16,32,128]{2,1,0:T(8,128)S(1)}, u32[]{:S(2)}, u32[]{:S(2)}) %all-to-all-start.3) | async-done | bytes 262176 | tf_op jit(solution)/shard_map/all_to_all | solution.py:36
  66.6 0.5 fusion.10
  67.1 0.9 %copy.48 = bf16[256,4,128]{2,1,0:T(4,128)(2,1)} copy(bf16[256,4,128]{0,2,1:T(8,128)(2,1)S(1)} %fusion.10) | data formatting | bytes 524288
  67.9 0.5 fusion.8
  68.5 0.9 %copy.47 = bf16[256,4,128]{2,1,0:T(4,128)(2,1)} copy(bf16[256,4,128]{0,2,1:T(8,128)(2,1)S(1)} %fusion.8) | data formatting | bytes 524288
  (21 shorter events, 2.2 us)
Async XLA Ops:
  0.6 1.2 %copy-start = (bf16[256,4,128]{2,1,0:T(4,128)(2,1)S(1)}, bf16[256,4,128]{2,1,0:T(4,128)(2,1)}, u32[]{:S(2)}) copy-start(bf16[256,4,128]{2,1,0:T(4,128)(2,1)} %param.7) | copy-start | bytes 786436
  2.8 8.5 %copy-start.1 = (bf16[256,4,128]{2,1,0:T(4,128)(2,1)S(1)}, bf16[256,4,128]{2,1,0:T(4,128)(2,1)}, u32[]{:S(2)}) copy-start(bf16[256,4,128]{2,1,0:T(4,128)(2,1)} %param.5) | copy-start | bytes 786436
  2.8 18.3 %all-to-all-start = ((f32[16,32,128]{2,1,0:T(8,128)}), f32[16,32,128]{2,1,0:T(8,128)S(1)}, u32[]{:S(2)}, u32[]{:S(2)}) async-start(f32[16,32,128]{2,1,0:T(8,128)} %bitcast.1), calls=%async_computation | async-start | bytes 524288 | tf_op jit(solution)/shard_map/all_to_all | solution.py:33
  11.3 1.0 %copy-start.2 = (bf16[256,4,128]{2,1,0:T(4,128)(2,1)S(1)}, bf16[256,4,128]{2,1,0:T(4,128)(2,1)}, u32[]{:S(2)}) copy-start(bf16[256,4,128]{2,1,0:T(4,128)(2,1)} %param.9) | copy-start | bytes 786436
  21.8 12.8 %all-to-all-start.1 = ((f32[16,32,128]{2,1,0:T(8,128)}), f32[16,32,128]{2,1,0:T(8,128)S(1)}, u32[]{:S(2)}, u32[]{:S(2)}) async-start(f32[16,32,128]{2,1,0:T(8,128)} %reduce-window_subtract_fusion.1), calls=%async_computation.1 | async-start | bytes 524288 | tf_op jit(solution)/shard_map/all_to_all | solution.py:36
  25.9 8.7 %copy-start.3 = (f32[4,128]{1,0:T(4,128)S(1)}, f32[4,128]{1,0:T(4,128)}, u32[]{:S(2)}) copy-start(f32[4,128]{1,0:T(4,128)} %param.8) | copy-start | bytes 6148
  35.2 1.2 %collective-permute-start = (f32[2,256]{1,0:T(2,128)S(1)}, f32[2,256]{1,0:T(2,128)S(1)}, u32[]{:S(2)}, u32[]{:S(2)}) collective-permute-start(f32[2,256]{1,0:T(2,128)S(1)} %pad_maximum_fusion), channel_id=1, source_target_pairs={{0,1},{1,0},{2,3},{3,2},{4,5},{5,4},{6,7},{7,6},{8,9},{9,8},{10,11... | collective-permute-start | bytes 6152 | tf_op jit(solution)/shard_map/ppermute | solution.py:74
  38.9 14.0 %all-to-all-start.2 = ((f32[16,32,128]{2,1,0:T(8,128)}), f32[16,32,128]{2,1,0:T(8,128)S(1)}, u32[]{:S(2)}, u32[]{:S(2)}) async-start(f32[16,32,128]{2,1,0:T(8,128)} %bitcast.15), calls=%async_computation.2 | async-start | bytes 524288 | tf_op jit(solution)/shard_map/all_to_all | solution.py:33
  53.6 13.0 %all-to-all-start.3 = ((f32[16,32,128]{2,1,0:T(8,128)}), f32[16,32,128]{2,1,0:T(8,128)S(1)}, u32[]{:S(2)}, u32[]{:S(2)}) async-start(f32[16,32,128]{2,1,0:T(8,128)} %reduce-window_subtract_fusion), calls=%async_computation.3 | async-start | bytes 524288 | tf_op jit(solution)/shard_map/all_to_all | solution.py:36

commit v7 on v6

--- a/solution.py
+++ b/solution.py
@@ -2,6 +2,7 @@
 import jax.numpy as jnp
 from jax import lax
 from jax.sharding import PartitionSpec as P
+from jax.experimental import pallas as pl
 
 GROUP = 256
 
@@ -45,6 +46,35 @@
     return exclusive_scan(own_total, True)
 
 
+def head_outer(lhs_rows, rhs_rows, head_count, lhs_silu):
+    span = GROUP * head_count
+    width = lhs_rows.shape[-1]
+    blocks = lhs_rows.shape[0] // span
+
+    def kernel(lhs_ref, rhs_ref, out_ref):
+        lhs = lhs_ref[...]
+        if lhs_silu:
+            lhs = jax.nn.silu(lhs.astype(jnp.float32)).astype(jnp.bfloat16)
+        rhs = rhs_ref[...]
+        row_head = lax.broadcasted_iota(jnp.int32, lhs.shape, 0) % head_count
+        for h in range(head_count):
+            picked = jnp.where(row_head == h, lhs, jnp.zeros_like(lhs))
+            out_ref[h] = lax.dot_general(
+                picked, rhs, (((0,), (0,)), ((), ())), preferred_element_type=jnp.float32
+            )
+
+    return pl.pallas_call(
+        kernel,
+        grid=(blocks,),
+        in_specs=[
+            pl.BlockSpec((span, width), lambda c: (c, 0)),
+            pl.BlockSpec((span, width), lambda c: (c, 0)),
+        ],
+        out_specs=pl.BlockSpec((None, head_count, width, width), lambda c: (c, 0, 0, 0)),
+        out_shape=jax.ShapeDtypeStruct((blocks, head_count, width, width), jnp.float32),
+    )(lhs_rows, rhs_rows)
+
+
 def body(query_raw, key_raw, value_raw, out_gain, out_grad):
     tok_rows, head_count, width = query_raw.shape
     blocks = tok_rows // GROUP
@@ -53,7 +83,8 @@
     key_act = jax.nn.silu(key_raw.astype(jnp.float32)).astype(jnp.bfloat16).reshape(blocked)
     value_blk = value_raw.reshape(blocked)
     mask = causal_mask(GROUP)[None, None]
-    block_kv = jnp.einsum("cshd,cshe->chde", key_act, value_blk, preferred_element_type=jnp.float32)
+    rows = (tok_rows * head_count, width)
+    block_kv = head_outer(key_raw.reshape(rows), value_raw.reshape(rows), head_count, True)
     own_total = jnp.sum(block_kv, axis=0)
     before = lower_sum(own_total)
     if blocks == 1:
@@ -81,9 +112,7 @@
         - mixed * (cross_total * inv_rms**3 / features)[:, None, None]
     ).astype(jnp.bfloat16)
     delta_blk = delta.reshape(blocked)
-    block_grad = jnp.einsum(
-        "cthd,cthe->chde", query_act, delta_blk, preferred_element_type=jnp.float32
-    )
+    block_grad = head_outer(query_raw.reshape(rows), delta.reshape(rows), head_count, True)
     own_grad = jnp.sum(block_grad, axis=0)
     after = upper_sum(own_grad)
     if blocks == 1:

time: 70 us -> 72.5 us (1.036)
  Pallas kernels: 0 us -> 4.69 us
  matrix products: 6.03 us -> 4.17 us
    pallas_call x0 -> x2, Pallas kernels: none -> 4.69 us  [head_outer(): pl.pallas_call(kernel, grid=(blocks,), in_specs=[pl.BlockSpec((span, widt...]
    dot_general x2 -> x0, matrix products: 1.97 us -> none  [the longest x1 0.99 us: body(): jnp.einsum('cthd,cthe->chde', query_act, delta_blk, preferred_element_typ...]
    convert_element_type x0 -> x1, local copies, waits for them, and re-layouts: none -> 0.91 us  [body(): delta = (grad_in * inv_rms[:, None, None] - mixed * (cross_total * inv_rm...]
    unnamed x15 -> x16, local copies, waits for them, and re-layouts: 5.75 us -> 5.07 us
where the time goes in v7:
time: 72.5 us; the launch traced here: 71.9 us
  waiting for transfers between devices  35.3 us (49%)
  starting transfers between devices  19.1 us (26%)
  local copies, waits for them, and re-layouts  5.97 us (8%)
  Pallas kernels  4.69 us (6%)
  matrix products  4.17 us (6%)
  other arithmetic  1.8 us (2%)
  between operations  0.79 us (1%)
    all_to_all x2, waiting for transfers between devices, exclusive_scan(): lax.all_to_all(rows.reshape(count, chunk, width), 'seq', 0, 0, tiled=True)  17.4 us
    all_to_all x2, waiting for transfers between devices, exclusive_scan(): spread = lax.all_to_all(prefix, 'seq', 0, 0, tiled=True)  16.8 us
    all_to_all x2, starting transfers between devices, exclusive_scan(): lax.all_to_all(rows.reshape(count, chunk, width), 'seq', 0, 0, tiled=True)  12 us
    all_to_all x2, starting transfers between devices, exclusive_scan(): spread = lax.all_to_all(prefix, 'seq', 0, 0, tiled=True)  7.08 us
    unnamed x16, local copies, waits for them, and re-layouts  5.07 us
    pallas_call x2, Pallas kernels, head_outer(): pl.pallas_call(kernel, grid=(blocks,), in_specs=[pl.BlockSpec((span, widt...  4.69 us
    another operation x2, other arithmetic, exclusive_scan(): inclusive = lax.cumsum(gathered, axis=0, reverse=reverse)  1.51 us
  transfers between devices with their start and end apart: 5, of which 5 were waited for; matrix products, arithmetic and copies ran while one was open for 5% of the time, Pallas kernels for 0%

profile of v7, /device:TPU:0, one launch (start us, length us, event | category | flops | bytes accessed | tf_op | source)
XLA Modules:
  0.0 71.9 jit_solution(2177523812533940181)
XLA Ops:
  0.6 2.3 %shard_map.84 = f32[1,4,128,128]{3,2,1,0:T(8,128)} custom-call(bf16[1024,128]{1,0:T(8,128)(2,1)} %bitcast.60, bf16[1024,128]{1,0:T(8,128)(2,1)} %bitcast.59), custom_call_target="tpu_custom_call" | custom-call | tf_op jit(solution)/shard_map/pallas_call | solution.py:66
  3.0 8.4 %all-to-all-start = ((f32[16,32,128]{2,1,0:T(8,128)}), f32[16,32,128]{2,1,0:T(8,128)S(1)}, u32[]{:S(2)}, u32[]{:S(2)}) async-start(f32[16,32,128]{2,1,0:T(8,128)} %bitcast.63), calls=%async_computation | async-start | bytes 524288 | tf_op jit(solution)/shard_map/all_to_all | solution.py:34
  11.6 0.8 %copy-done.2 = bf16[256,4,128]{2,1,0:T(4,128)(2,1)S(1)} copy-done((bf16[256,4,128]{2,1,0:T(4,128)(2,1)S(1)}, bf16[256,4,128]{2,1,0:T(4,128)(2,1)}, u32[]{:S(2)}) %copy-start.2) | copy-done | bytes 262168
  12.6 8.7 %all-to-all-done = f32[16,32,128]{2,1,0:T(8,128)S(1)} async-done(((f32[16,32,128]{2,1,0:T(8,128)}), f32[16,32,128]{2,1,0:T(8,128)S(1)}, u32[]{:S(2)}, u32[]{:S(2)}) %all-to-all-start) | async-done | bytes 262176 | tf_op jit(solution)/shard_map/all_to_all | solution.py:34
  21.3 0.7 %reduce-window_subtract_fusion.1 = f32[16,32,128]{2,1,0:T(8,128)} fusion(f32[16,32,128]{2,1,0:T(8,128)S(1)} %all-to-all-done), kind=kOutput, calls=%fused_computation.18 | output fusion | flops 1048576 | bytes 524288 | tf_op jit(solution)/shard_map/exclusive_scan/reduce_window_sum | solution.py:35
  22.0 3.5 %all-to-all-start.1 = ((f32[16,32,128]{2,1,0:T(8,128)}), f32[16,32,128]{2,1,0:T(8,128)S(1)}, u32[]{:S(2)}, u32[]{:S(2)}) async-start(f32[16,32,128]{2,1,0:T(8,128)} %reduce-window_subtract_fusion.1), calls=%async_computation.1 | async-start | bytes 524288 | tf_op jit(solution)/shard_map/all_to_all | solution.py:37
  25.6 0.5 fusion
  26.8 8.0 %all-to-all-done.1 = f32[16,32,128]{2,1,0:T(8,128)S(1)} async-done(((f32[16,32,128]{2,1,0:T(8,128)}), f32[16,32,128]{2,1,0:T(8,128)S(1)}, u32[]{:S(2)}, u32[]{:S(2)}) %all-to-all-start.1) | async-done | bytes 262176 | tf_op jit(solution)/shard_map/all_to_all | solution.py:37
  34.8 0.7 multiply_reduce_fusion.1
  35.6 1.1 %collective-permute-done = f32[2,256]{1,0:T(2,128)S(1)} collective-permute-done((f32[2,256]{1,0:T(2,128)S(1)}, f32[2,256]{1,0:T(2,128)S(1)}, u32[]{:S(2)}, u32[]{:S(2)}) %collective-permute-start) | collective-permute-done | bytes 2080 | tf_op jit(solution)/shard_map/ppermute | solution.py:105
  37.0 0.9 %copy.38 = bf16[256,4,128]{2,1,0:T(4,128)(2,1)} copy(bf16[256,4,128]{2,0,1:T(8,128)(2,1)S(1)} %get-tuple-element.14) | data formatting | bytes 524288 | tf_op jit(solution)/shard_map/convert_element_type | solution.py:113
  38.2 0.9 %copy.43 = bf16[256,4,128]{2,1,0:T(4,128)(2,1)} copy(bf16[256,4,128]{2,0,1:T(8,128)(2,1)S(1)} %get-tuple-element.15) | data formatting | bytes 524288
  39.1 2.3 %shard_map.85 = f32[1,4,128,128]{3,2,1,0:T(8,128)} custom-call(bf16[1024,128]{1,0:T(8,128)(2,1)} %bitcast.61, bf16[1024,128]{1,0:T(8,128)(2,1)} %bitcast.64), custom_call_target="tpu_custom_call" | custom-call | tf_op jit(solution)/shard_map/pallas_call | solution.py:66
  41.5 3.5 %all-to-all-start.2 = ((f32[16,32,128]{2,1,0:T(8,128)}), f32[16,32,128]{2,1,0:T(8,128)S(1)}, u32[]{:S(2)}, u32[]{:S(2)}) async-start(f32[16,32,128]{2,1,0:T(8,128)} %bitcast.62), calls=%async_computation.2 | async-start | bytes 524288 | tf_op jit(solution)/shard_map/all_to_all | solution.py:34
  45.3 0.5 fusion.7
  45.9 0.9 %copy.44 = bf16[256,4,128]{2,1,0:T(4,128)(2,1)} copy(bf16[256,4,128]{0,2,1:T(8,128)(2,1)S(1)} %fusion.7) | data formatting | bytes 524288
  46.7 8.7 %all-to-all-done.2 = f32[16,32,128]{2,1,0:T(8,128)S(1)} async-done(((f32[16,32,128]{2,1,0:T(8,128)}), f32[16,32,128]{2,1,0:T(8,128)S(1)}, u32[]{:S(2)}, u32[]{:S(2)}) %all-to-all-start.2) | async-done | bytes 262176 | tf_op jit(solution)/shard_map/all_to_all | solution.py:34
  55.4 0.8 %reduce-window_subtract_fusion = f32[16,32,128]{2,1,0:T(8,128)} fusion(f32[16,32,128]{2,1,0:T(8,128)S(1)} %all-to-all-done.2), kind=kOutput, calls=%fused_computation.17 | output fusion | flops 1048576 | bytes 524288 | tf_op jit(solution)/shard_map/exclusive_scan/reduce_window_sum | solution.py:35
  56.2 3.5 %all-to-all-start.3 = ((f32[16,32,128]{2,1,0:T(8,128)}), f32[16,32,128]{2,1,0:T(8,128)S(1)}, u32[]{:S(2)}, u32[]{:S(2)}) async-start(f32[16,32,128]{2,1,0:T(8,128)} %reduce-window_subtract_fusion), calls=%async_computation.3 | async-start | bytes 524288 | tf_op jit(solution)/shard_map/all_to_all | solution.py:37
  60.3 8.8 %all-to-all-done.3 = f32[16,32,128]{2,1,0:T(8,128)S(1)} async-done(((f32[16,32,128]{2,1,0:T(8,128)}), f32[16,32,128]{2,1,0:T(8,128)S(1)}, u32[]{:S(2)}, u32[]{:S(2)}) %all-to-all-start.3) | async-done | bytes 262176 | tf_op jit(solution)/shard_map/all_to_all | solution.py:37
  69.2 0.5 fusion.10
  69.6 0.9 %copy.46 = bf16[256,4,128]{2,1,0:T(4,128)(2,1)} copy(bf16[256,4,128]{0,2,1:T(8,128)(2,1)S(1)} %fusion.10) | data formatting | bytes 524288
  70.5 0.5 fusion.8
  71.0 0.9 %copy.45 = bf16[256,4,128]{2,1,0:T(4,128)(2,1)} copy(bf16[256,4,128]{0,2,1:T(8,128)(2,1)S(1)} %fusion.8) | data formatting | bytes 524288
  (23 shorter events, 2.6 us)
Async XLA Ops:
  3.0 8.5 %copy-start.1 = (bf16[256,4,128]{2,1,0:T(4,128)(2,1)S(1)}, bf16[256,4,128]{2,1,0:T(4,128)(2,1)}, u32[]{:S(2)}) copy-start(bf16[256,4,128]{2,1,0:T(4,128)(2,1)} %param.6) | copy-start | bytes 786436
  3.0 18.3 %all-to-all-start = ((f32[16,32,128]{2,1,0:T(8,128)}), f32[16,32,128]{2,1,0:T(8,128)S(1)}, u32[]{:S(2)}, u32[]{:S(2)}) async-start(f32[16,32,128]{2,1,0:T(8,128)} %bitcast.63), calls=%async_computation | async-start | bytes 524288 | tf_op jit(solution)/shard_map/all_to_all | solution.py:34
  11.4 1.0 %copy-start.2 = (bf16[256,4,128]{2,1,0:T(4,128)(2,1)S(1)}, bf16[256,4,128]{2,1,0:T(4,128)(2,1)}, u32[]{:S(2)}) copy-start(bf16[256,4,128]{2,1,0:T(4,128)(2,1)} %param.5) | copy-start | bytes 786436
  22.0 12.8 %all-to-all-start.1 = ((f32[16,32,128]{2,1,0:T(8,128)}), f32[16,32,128]{2,1,0:T(8,128)S(1)}, u32[]{:S(2)}, u32[]{:S(2)}) async-start(f32[16,32,128]{2,1,0:T(8,128)} %reduce-window_subtract_fusion.1), calls=%async_computation.1 | async-start | bytes 524288 | tf_op jit(solution)/shard_map/all_to_all | solution.py:37
  25.6 1.0 %copy-start = (bf16[256,4,128]{2,1,0:T(4,128)(2,1)S(1)}, bf16[256,4,128]{2,1,0:T(4,128)(2,1)}, u32[]{:S(2)}) copy-start(bf16[256,4,128]{2,1,0:T(4,128)(2,1)} %param.7) | copy-start | bytes 786436
  26.5 8.3 %copy-start.3 = (bf16[256,4,128]{2,1,0:T(4,128)(2,1)S(1)}, bf16[256,4,128]{2,1,0:T(4,128)(2,1)}, u32[]{:S(2)}) copy-start(bf16[256,4,128]{2,1,0:T(4,128)(2,1)} %param.9) | copy-start | bytes 786436
  26.5 8.3 %copy-start.4 = (f32[4,128]{1,0:T(4,128)S(1)}, f32[4,128]{1,0:T(4,128)}, u32[]{:S(2)}) copy-start(f32[4,128]{1,0:T(4,128)} %param.8) | copy-start | bytes 6148
  35.5 1.2 %collective-permute-start = (f32[2,256]{1,0:T(2,128)S(1)}, f32[2,256]{1,0:T(2,128)S(1)}, u32[]{:S(2)}, u32[]{:S(2)}) collective-permute-start(f32[2,256]{1,0:T(2,128)S(1)} %pad_maximum_fusion), channel_id=1, source_target_pairs={{0,1},{1,0},{2,3},{3,2},{4,5},{5,4},{6,7},{7,6},{8,9},{9,8},{10,11... | collective-permute-start | bytes 6152 | tf_op jit(solution)/shard_map/ppermute | solution.py:105
  41.5 14.0 %all-to-all-start.2 = ((f32[16,32,128]{2,1,0:T(8,128)}), f32[16,32,128]{2,1,0:T(8,128)S(1)}, u32[]{:S(2)}, u32[]{:S(2)}) async-start(f32[16,32,128]{2,1,0:T(8,128)} %bitcast.62), calls=%async_computation.2 | async-start | bytes 524288 | tf_op jit(solution)/shard_map/all_to_all | solution.py:34
  56.2 13.0 %all-to-all-start.3 = ((f32[16,32,128]{2,1,0:T(8,128)}), f32[16,32,128]{2,1,0:T(8,128)S(1)}, u32[]{:S(2)}, u32[]{:S(2)}) async-start(f32[16,32,128]{2,1,0:T(8,128)} %reduce-window_subtract_fusion), calls=%async_computation.3 | async-start | bytes 524288 | tf_op jit(solution)/shard_map/all_to_all | solution.py:37

commit v8 on v7

--- a/solution.py
+++ b/solution.py
@@ -56,12 +56,11 @@
         if lhs_silu:
             lhs = jax.nn.silu(lhs.astype(jnp.float32)).astype(jnp.bfloat16)
         rhs = rhs_ref[...]
-        row_head = lax.broadcasted_iota(jnp.int32, lhs.shape, 0) % head_count
+        lhs_t = lhs.T
+        col_head = lax.broadcasted_iota(jnp.int32, lhs_t.shape, 1) % head_count
         for h in range(head_count):
-            picked = jnp.where(row_head == h, lhs, jnp.zeros_like(lhs))
-            out_ref[h] = lax.dot_general(
-                picked, rhs, (((0,), (0,)), ((), ())), preferred_element_type=jnp.float32
-            )
+            picked = jnp.where(col_head == h, lhs_t, jnp.zeros_like(lhs_t))
+            out_ref[h] = jnp.dot(picked, rhs, preferred_element_type=jnp.float32)
 
     return pl.pallas_call(
         kernel,
@@ -112,7 +111,9 @@
         - mixed * (cross_total * inv_rms**3 / features)[:, None, None]
     ).astype(jnp.bfloat16)
     delta_blk = delta.reshape(blocked)
-    block_grad = head_outer(query_raw.reshape(rows), delta.reshape(rows), head_count, True)
+    block_grad = jnp.einsum(
+        "cthd,cthe->chde", query_act, delta_blk, preferred_element_type=jnp.float32
+    )
     own_grad = jnp.sum(block_grad, axis=0)
     after = upper_sum(own_grad)
     if blocks == 1:

time: 72.5 us -> 70 us (0.966)
  Pallas kernels: 4.69 us -> 2.22 us
  waiting for transfers between devices: 35.3 us -> 34.4 us
  matrix products: 4.17 us -> 5.06 us
    pallas_call x2 -> x1, Pallas kernels: 4.69 us -> 2.22 us  [head_outer(): pl.pallas_call(kernel, grid=(blocks,), in_specs=[pl.BlockSpec((span, widt...]
    dot_general x0 -> x1, matrix products: none -> 0.99 us  [body(): jnp.einsum('cthd,cthe->chde', query_act, delta_blk, preferred_element_typ...]
    all_to_all x2, waiting for transfers between devices: 17.4 us -> 16.5 us  [exclusive_scan(): lax.all_to_all(rows.reshape(count, chunk, width), 'seq', 0, 0, tiled=True)]
    convert_element_type x1 -> x0, local copies, waits for them, and re-layouts: 0.91 us -> none  [body(): delta = (grad_in * inv_rms[:, None, None] - mixed * (cross_total * inv_rm...]
    unnamed x16 -> x17, local copies, waits for them, and re-layouts: 5.07 us -> 5.96 us
where the time goes in v8:
time: 70 us; the launch traced here: 69.4 us
  waiting for transfers between devices  34.4 us (49%)
  starting transfers between devices  19.1 us (27%)
  local copies, waits for them, and re-layouts  5.96 us (9%)
  matrix products  5.06 us (7%)
  Pallas kernels  2.22 us (3%)
  other arithmetic  1.76 us (3%)
  between operations  0.81 us (1%)
    all_to_all x2, waiting for transfers between devices, exclusive_scan(): spread = lax.all_to_all(prefix, 'seq', 0, 0, tiled=True)  16.8 us
    all_to_all x2, waiting for transfers between devices, exclusive_scan(): lax.all_to_all(rows.reshape(count, chunk, width), 'seq', 0, 0, tiled=True)  16.5 us
    all_to_all x2, starting transfers between devices, exclusive_scan(): lax.all_to_all(rows.reshape(count, chunk, width), 'seq', 0, 0, tiled=True)  12 us
    all_to_all x2, starting transfers between devices, exclusive_scan(): spread = lax.all_to_all(prefix, 'seq', 0, 0, tiled=True)  7.08 us
    unnamed x17, local copies, waits for them, and re-layouts  5.96 us
    pallas_call x1, Pallas kernels, head_outer(): pl.pallas_call(kernel, grid=(blocks,), in_specs=[pl.BlockSpec((span, widt...  2.22 us
    another operation x2, other arithmetic, exclusive_scan(): inclusive = lax.cumsum(gathered, axis=0, reverse=reverse)  1.51 us
  transfers between devices with their start and end apart: 5, of which 5 were waited for; matrix products, arithmetic and copies ran while one was open for 5% of the time, Pallas kernels for 0%

profile of v8, /device:TPU:0, one launch (start us, length us, event | category | flops | bytes accessed | tf_op | source)
XLA Modules:
  0.0 69.4 jit_solution(13322450694230355385)
XLA Ops:
  0.6 2.2 %shard_map.84 = f32[1,4,128,128]{3,2,1,0:T(8,128)} custom-call(bf16[1024,128]{1,0:T(8,128)(2,1)} %bitcast.59, bf16[1024,128]{1,0:T(8,128)(2,1)} %bitcast.58), custom_call_target="tpu_custom_call" | custom-call | tf_op jit(solution)/shard_map/pallas_call | solution.py:65
  2.9 8.4 %all-to-all-start = ((f32[16,32,128]{2,1,0:T(8,128)}), f32[16,32,128]{2,1,0:T(8,128)S(1)}, u32[]{:S(2)}, u32[]{:S(2)}) async-start(f32[16,32,128]{2,1,0:T(8,128)} %bitcast.60), calls=%async_computation | async-start | bytes 524288 | tf_op jit(solution)/shard_map/all_to_all | solution.py:34
  11.5 0.8 %copy-done.2 = bf16[256,4,128]{2,1,0:T(4,128)(2,1)S(1)} copy-done((bf16[256,4,128]{2,1,0:T(4,128)(2,1)S(1)}, bf16[256,4,128]{2,1,0:T(4,128)(2,1)}, u32[]{:S(2)}) %copy-start.2) | copy-done | bytes 262168
  12.5 0.8 %copy-done.3 = bf16[256,4,128]{2,1,0:T(4,128)(2,1)S(1)} copy-done((bf16[256,4,128]{2,1,0:T(4,128)(2,1)S(1)}, bf16[256,4,128]{2,1,0:T(4,128)(2,1)}, u32[]{:S(2)}) %copy-start.3) | copy-done | bytes 262168
  13.4 7.7 %all-to-all-done = f32[16,32,128]{2,1,0:T(8,128)S(1)} async-done(((f32[16,32,128]{2,1,0:T(8,128)}), f32[16,32,128]{2,1,0:T(8,128)S(1)}, u32[]{:S(2)}, u32[]{:S(2)}) %all-to-all-start) | async-done | bytes 262176 | tf_op jit(solution)/shard_map/all_to_all | solution.py:34
  21.2 0.7 %reduce-window_subtract_fusion.1 = f32[16,32,128]{2,1,0:T(8,128)} fusion(f32[16,32,128]{2,1,0:T(8,128)S(1)} %all-to-all-done), kind=kOutput, calls=%fused_computation.18 | output fusion | flops 1048576 | bytes 524288 | tf_op jit(solution)/shard_map/exclusive_scan/reduce_window_sum | solution.py:35
  21.9 3.5 %all-to-all-start.1 = ((f32[16,32,128]{2,1,0:T(8,128)}), f32[16,32,128]{2,1,0:T(8,128)S(1)}, u32[]{:S(2)}, u32[]{:S(2)}) async-start(f32[16,32,128]{2,1,0:T(8,128)} %reduce-window_subtract_fusion.1), calls=%async_computation.1 | async-start | bytes 524288 | tf_op jit(solution)/shard_map/all_to_all | solution.py:37
  25.5 0.5 fusion
  26.7 7.9 %all-to-all-done.1 = f32[16,32,128]{2,1,0:T(8,128)S(1)} async-done(((f32[16,32,128]{2,1,0:T(8,128)}), f32[16,32,128]{2,1,0:T(8,128)S(1)}, u32[]{:S(2)}, u32[]{:S(2)}) %all-to-all-start.1) | async-done | bytes 262176 | tf_op jit(solution)/shard_map/all_to_all | solution.py:37
  34.7 0.6 multiply_reduce_fusion.1
  35.4 1.1 %collective-permute-done = f32[2,256]{1,0:T(2,128)S(1)} collective-permute-done((f32[2,256]{1,0:T(2,128)S(1)}, f32[2,256]{1,0:T(2,128)S(1)}, u32[]{:S(2)}, u32[]{:S(2)}) %collective-permute-start) | collective-permute-done | bytes 2080 | tf_op jit(solution)/shard_map/ppermute | solution.py:104
  36.7 1.0 %fusion.35 = f32[4,128,128]{2,1,0:T(8,128)} fusion(bf16[256,4,128]{0,2,1:T(8,128)(2,1)S(1)} %get-tuple-element.14, bf16[256,4,128]{0,2,1:T(8,128)(2,1)S(1)} %copy.28), kind=kOutput, calls=%fused_computation.56 | convolution fusion | flops 34340864 | bytes 786432 | tf_op jit(solution)/shard_map/cthd,cthe->chde/dot_general | solution.py:114
  38.1 0.9 %copy.43 = bf16[256,4,128]{2,1,0:T(4,128)(2,1)} copy(bf16[256,4,128]{0,2,1:T(8,128)(2,1)S(1)} %get-tuple-element.15) | data formatting | bytes 524288
  38.9 3.5 %all-to-all-start.2 = ((f32[16,32,128]{2,1,0:T(8,128)}), f32[16,32,128]{2,1,0:T(8,128)S(1)}, u32[]{:S(2)}, u32[]{:S(2)}) async-start(f32[16,32,128]{2,1,0:T(8,128)} %bitcast.17), calls=%async_computation.2 | async-start | bytes 524288 | tf_op jit(solution)/shard_map/all_to_all | solution.py:34
  42.8 0.5 fusion.7
  43.3 0.9 %copy.44 = bf16[256,4,128]{2,1,0:T(4,128)(2,1)} copy(bf16[256,4,128]{0,2,1:T(8,128)(2,1)S(1)} %fusion.7) | data formatting | bytes 524288
  44.2 8.7 %all-to-all-done.2 = f32[16,32,128]{2,1,0:T(8,128)S(1)} async-done(((f32[16,32,128]{2,1,0:T(8,128)}), f32[16,32,128]{2,1,0:T(8,128)S(1)}, u32[]{:S(2)}, u32[]{:S(2)}) %all-to-all-start.2) | async-done | bytes 262176 | tf_op jit(solution)/shard_map/all_to_all | solution.py:34
  52.9 0.8 %reduce-window_subtract_fusion = f32[16,32,128]{2,1,0:T(8,128)} fusion(f32[16,32,128]{2,1,0:T(8,128)S(1)} %all-to-all-done.2), kind=kOutput, calls=%fused_computation.17 | output fusion | flops 1048576 | bytes 524288 | tf_op jit(solution)/shard_map/exclusive_scan/reduce_window_sum | solution.py:35
  53.7 3.5 %all-to-all-start.3 = ((f32[16,32,128]{2,1,0:T(8,128)}), f32[16,32,128]{2,1,0:T(8,128)S(1)}, u32[]{:S(2)}, u32[]{:S(2)}) async-start(f32[16,32,128]{2,1,0:T(8,128)} %reduce-window_subtract_fusion), calls=%async_computation.3 | async-start | bytes 524288 | tf_op jit(solution)/shard_map/all_to_all | solution.py:37
  57.7 8.9 %all-to-all-done.3 = f32[16,32,128]{2,1,0:T(8,128)S(1)} async-done(((f32[16,32,128]{2,1,0:T(8,128)}), f32[16,32,128]{2,1,0:T(8,128)S(1)}, u32[]{:S(2)}, u32[]{:S(2)}) %all-to-all-start.3) | async-done | bytes 262176 | tf_op jit(solution)/shard_map/all_to_all | solution.py:37
  66.6 0.5 fusion.10
  67.1 0.9 %copy.46 = bf16[256,4,128]{2,1,0:T(4,128)(2,1)} copy(bf16[256,4,128]{0,2,1:T(8,128)(2,1)S(1)} %fusion.10) | data formatting | bytes 524288
  68.0 0.5 fusion.8
  68.5 0.9 %copy.45 = bf16[256,4,128]{2,1,0:T(4,128)(2,1)} copy(bf16[256,4,128]{0,2,1:T(8,128)(2,1)S(1)} %fusion.8) | data formatting | bytes 524288
  (23 shorter events, 2.8 us)
Async XLA Ops:
  2.9 8.5 %copy-start.1 = (bf16[256,4,128]{2,1,0:T(4,128)(2,1)S(1)}, bf16[256,4,128]{2,1,0:T(4,128)(2,1)}, u32[]{:S(2)}) copy-start(bf16[256,4,128]{2,1,0:T(4,128)(2,1)} %param.6) | copy-start | bytes 786436
  2.9 18.3 %all-to-all-start = ((f32[16,32,128]{2,1,0:T(8,128)}), f32[16,32,128]{2,1,0:T(8,128)S(1)}, u32[]{:S(2)}, u32[]{:S(2)}) async-start(f32[16,32,128]{2,1,0:T(8,128)} %bitcast.60), calls=%async_computation | async-start | bytes 524288 | tf_op jit(solution)/shard_map/all_to_all | solution.py:34
  11.3 1.0 %copy-start.2 = (bf16[256,4,128]{2,1,0:T(4,128)(2,1)S(1)}, bf16[256,4,128]{2,1,0:T(4,128)(2,1)}, u32[]{:S(2)}) copy-start(bf16[256,4,128]{2,1,0:T(4,128)(2,1)} %param.5) | copy-start | bytes 786436
  12.3 0.9 %copy-start.3 = (bf16[256,4,128]{2,1,0:T(4,128)(2,1)S(1)}, bf16[256,4,128]{2,1,0:T(4,128)(2,1)}, u32[]{:S(2)}) copy-start(bf16[256,4,128]{2,1,0:T(4,128)(2,1)} %param.9) | copy-start | bytes 786436
  21.9 12.8 %all-to-all-start.1 = ((f32[16,32,128]{2,1,0:T(8,128)}), f32[16,32,128]{2,1,0:T(8,128)S(1)}, u32[]{:S(2)}, u32[]{:S(2)}) async-start(f32[16,32,128]{2,1,0:T(8,128)} %reduce-window_subtract_fusion.1), calls=%async_computation.1 | async-start | bytes 524288 | tf_op jit(solution)/shard_map/all_to_all | solution.py:37
  25.5 1.0 %copy-start = (bf16[256,4,128]{2,1,0:T(4,128)(2,1)S(1)}, bf16[256,4,128]{2,1,0:T(4,128)(2,1)}, u32[]{:S(2)}) copy-start(bf16[256,4,128]{2,1,0:T(4,128)(2,1)} %param.7) | copy-start | bytes 786436
  26.4 8.3 %copy-start.4 = (f32[4,128]{1,0:T(4,128)S(1)}, f32[4,128]{1,0:T(4,128)}, u32[]{:S(2)}) copy-start(f32[4,128]{1,0:T(4,128)} %param.8) | copy-start | bytes 6148
  35.3 1.2 %collective-permute-start = (f32[2,256]{1,0:T(2,128)S(1)}, f32[2,256]{1,0:T(2,128)S(1)}, u32[]{:S(2)}, u32[]{:S(2)}) collective-permute-start(f32[2,256]{1,0:T(2,128)S(1)} %pad_maximum_fusion), channel_id=1, source_target_pairs={{0,1},{1,0},{2,3},{3,2},{4,5},{5,4},{6,7},{7,6},{8,9},{9,8},{10,11... | collective-permute-start | bytes 6152 | tf_op jit(solution)/shard_map/ppermute | solution.py:104
  38.9 14.0 %all-to-all-start.2 = ((f32[16,32,128]{2,1,0:T(8,128)}), f32[16,32,128]{2,1,0:T(8,128)S(1)}, u32[]{:S(2)}, u32[]{:S(2)}) async-start(f32[16,32,128]{2,1,0:T(8,128)} %bitcast.17), calls=%async_computation.2 | async-start | bytes 524288 | tf_op jit(solution)/shard_map/all_to_all | solution.py:34
  53.7 13.0 %all-to-all-start.3 = ((f32[16,32,128]{2,1,0:T(8,128)}), f32[16,32,128]{2,1,0:T(8,128)S(1)}, u32[]{:S(2)}, u32[]{:S(2)}) async-start(f32[16,32,128]{2,1,0:T(8,128)} %reduce-window_subtract_fusion), calls=%async_computation.3 | async-start | bytes 524288 | tf_op jit(solution)/shard_map/all_to_all | solution.py:37

commit v9 on v6

--- a/solution.py
+++ b/solution.py
@@ -2,6 +2,7 @@
 import jax.numpy as jnp
 from jax import lax
 from jax.sharding import PartitionSpec as P
+from jax.experimental.layout import Layout, with_layout_constraint
 
 GROUP = 256
 
@@ -45,6 +46,10 @@
     return exclusive_scan(own_total, True)
 
 
+def natural(array):
+    return with_layout_constraint(array, Layout(tuple(range(array.ndim))))
+
+
 def body(query_raw, key_raw, value_raw, out_gain, out_grad):
     tok_rows, head_count, width = query_raw.shape
     blocks = tok_rows // GROUP
@@ -66,7 +71,7 @@
     mixed = mixed + jnp.einsum(
         "cthd,chde->cthe", query_act, state_b, preferred_element_type=jnp.float32, precision=lax.Precision.HIGHEST
     )
-    mixed = mixed.reshape(tok_rows, head_count, width)
+    mixed = natural(mixed.reshape(tok_rows, head_count, width))
     grad_in = out_grad.astype(jnp.float32) * out_gain
     sq_part = jnp.sum(mixed * mixed, axis=(1, 2))
     cross_part = jnp.sum(grad_in * mixed, axis=(1, 2))
@@ -105,6 +110,7 @@
         "cshd,chde->cshe", key_act, grad_state, preferred_element_type=jnp.float32, precision=lax.Precision.HIGHEST
     )
     whole = (tok_rows, head_count, width)
+    dquery, dkey, dvalue = natural(dquery), natural(dkey), natural(dvalue)
     query_grad = (dquery.reshape(whole) * silu_grad(query_raw.astype(jnp.float32))).astype(
         jnp.bfloat16
     )

time: 70 us -> 77.1 us (1.10)
  other arithmetic: 1.76 us -> 9.7 us
  matrix products: 6.03 us -> 8.46 us
  local copies, waits for them, and re-layouts: 5.75 us -> 3.34 us
  waiting for transfers between devices: 35.8 us -> 34.7 us
    unnamed x15 -> x22, local copies, waits for them, and re-layouts: 5.75 us -> 0.7 us
    convert_element_type x0 -> x6, other arithmetic: none -> 3.74 us  [the longest x1 1.8 us: body(): (dkey.reshape(whole) * silu_grad(key_raw.astype(jnp.float32))).astype(jnp...]
    convert_element_type x1, other arithmetic: 0.18 us -> 2.82 us  [body(): delta = (grad_in * inv_rms[:, None, None] - mixed * (cross_total * inv_rm...]
    all_to_all x2, waiting for transfers between devices: 17.3 us -> 15.3 us  [exclusive_scan(): spread = lax.all_to_all(prefix, 'seq', 0, 0, tiled=True)]
    add x0 -> x3, local copies, waits for them, and re-layouts: none -> 1.67 us  [the longest x1 1.26 us: body(): dkey + jnp.einsum('cshe,chde->cshd', value_blk, grad_state, preferred_ele...]
    reduce_sum x0 -> x1, other arithmetic: none -> 1.56 us  [body(): sq_part = jnp.sum(mixed * mixed, axis=(1, 2))]
    convert_element_type x0 -> x2, local copies, waits for them, and re-layouts: none -> 0.97 us  [the longest x1 0.8 us: body(): value_grad = dvalue.reshape(whole).astype(jnp.bfloat16)]
    all_to_all x2, waiting for transfers between devices: 17.4 us -> 18.3 us  [exclusive_scan(): lax.all_to_all(rows.reshape(count, chunk, width), 'seq', 0, 0, tiled=True)]
  transfers between devices with their start and end apart: 5 -> 5, of which waited for: 5 -> 5; matrix products, arithmetic and copies ran while one was open for 5% -> 7% of each run, Pallas kernels for 0% -> 0%
where the time goes in v9:
time: 77.1 us; the launch traced here: 76.4 us
  waiting for transfers between devices  34.7 us (45%)
  starting transfers between devices  19.3 us (25%)
  other arithmetic  9.7 us (13%)
  matrix products  8.46 us (11%)
  local copies, waits for them, and re-layouts  3.34 us (4%)
  between operations  0.91 us (1%)
    all_to_all x2, waiting for transfers between devices, exclusive_scan(): lax.all_to_all(rows.reshape(count, chunk, width), 'seq', 0, 0, tiled=True)  18.3 us
    all_to_all x2, waiting for transfers between devices, exclusive_scan(): spread = lax.all_to_all(prefix, 'seq', 0, 0, tiled=True)  15.3 us
    all_to_all x2, starting transfers between devices, exclusive_scan(): lax.all_to_all(rows.reshape(count, chunk, width), 'seq', 0, 0, tiled=True)  12 us
    all_to_all x2, starting transfers between devices, exclusive_scan(): spread = lax.all_to_all(prefix, 'seq', 0, 0, tiled=True)  7.21 us
    convert_element_type x1, other arithmetic, body(): delta = (grad_in * inv_rms[:, None, None] - mixed * (cross_total * inv_rm...  2.82 us
    convert_element_type x1, other arithmetic, body(): (dkey.reshape(whole) * silu_grad(key_raw.astype(jnp.float32))).astype(jnp...  1.8 us
    reduce_sum x1, other arithmetic, body(): sq_part = jnp.sum(mixed * mixed, axis=(1, 2))  1.56 us
  transfers between devices with their start and end apart: 5, of which 5 were waited for; matrix products, arithmetic and copies ran while one was open for 7% of the time, Pallas kernels for 0%

profile of v9, /device:TPU:0, one launch (start us, length us, event | category | flops | bytes accessed | tf_op | source)
XLA Modules:
  0.0 76.4 jit_solution(4561020919634841709)
XLA Ops:
  0.6 1.0 %copy_convert_fusion.1 = f32[256,4,128]{2,0,1:T(8,128)S(1)} fusion(bf16[256,4,128]{2,1,0:T(4,128)(2,1)} %param.6), kind=kLoop, calls=%fused_computation.32 | loop fusion | flops 131072 | bytes 786432 | tf_op jit(solution)/shard_map/convert_element_type | solution.py:58
  2.1 1.0 %fusion.19 = f32[4,128,128]{2,1,0:T(8,128)} fusion(bf16[256,4,128]{2,1,0:T(4,128)(2,1)S(1)} %copy-done, bf16[256,4,128]{2,1,0:T(4,128)(2,1)S(1)} %multiply_convert_fusion), kind=kOutput, calls=%fused_computation.43 | convolution fusion | flops 33554432 | bytes 786432 | tf_op jit(solution)/shard_map/cshd,cshe->chde/dot_general | solution.py:61
  3.1 8.4 %all-to-all-start = ((f32[16,32,128]{2,1,0:T(8,128)}), f32[16,32,128]{2,1,0:T(8,128)S(1)}, u32[]{:S(2)}, u32[]{:S(2)}) async-start(f32[16,32,128]{2,1,0:T(8,128)} %bitcast.1), calls=%async_computation | async-start | bytes 524288 | tf_op jit(solution)/shard_map/all_to_all | solution.py:34
  12.6 8.8 %all-to-all-done = f32[16,32,128]{2,1,0:T(8,128)S(1)} async-done(((f32[16,32,128]{2,1,0:T(8,128)}), f32[16,32,128]{2,1,0:T(8,128)S(1)}, u32[]{:S(2)}, u32[]{:S(2)}) %all-to-all-start) | async-done | bytes 262176 | tf_op jit(solution)/shard_map/all_to_all | solution.py:34
  21.4 0.7 reduce-window_subtract_fusion.1
  22.2 3.7 %all-to-all-start.1 = ((f32[16,32,128]{2,1,0:T(8,128)}), f32[16,32,128]{2,1,0:T(8,128)S(1)}, u32[]{:S(2)}, u32[]{:S(2)}) async-start(f32[16,32,128]{2,1,0:T(8,128)} %reduce-window_subtract_fusion.1), calls=%async_computation.1 | async-start | bytes 524288 | tf_op jit(solution)/shard_map/all_to_all | solution.py:37
  25.9 1.1 %fusion.21 = f32[4,256,128]{2,1,0:T(8,128)} fusion(bf16[4,256,256]{2,1,0:T(8,128)(2,1)S(1)} %fusion, bf16[256,4,128]{2,1,0:T(4,128)(2,1)S(1)} %copy-done), kind=kOutput, calls=%fused_computation.45 | convolution fusion | flops 67108864 | bytes 1310720 | tf_op jit(solution)/shard_map/chts,cshe->cthe/dot_general | solution.py:70
  27.0 8.1 %all-to-all-done.1 = f32[16,32,128]{2,1,0:T(8,128)S(1)} async-done(((f32[16,32,128]{2,1,0:T(8,128)}), f32[16,32,128]{2,1,0:T(8,128)S(1)}, u32[]{:S(2)}, u32[]{:S(2)}) %all-to-all-start.1) | async-done | bytes 262176 | tf_op jit(solution)/shard_map/all_to_all | solution.py:37
  35.5 0.6 copy-done.7
  36.1 1.6 %fusion.6 = (f32[256]{0:T(256)S(1)}, f32[256]{0:T(256)S(1)}, f32[4,128,256]{1,0,2:T(4,128)S(1)}) fusion(f32[4,128]{1,0:T(4,128)S(1)} %copy-done.10, f32[256,4,128]{2,0,1:T(8,128)S(1)} %copy_convert_fusion, f32[4,128,256]{1,2,0:T(8,128)S(1)} %fusion.34, f32[4,256,128]{2,1,0:T(8,128)S(1)} %copy-done.7), kind=kLoop, calls=%fused_computation.20 | loop fusion | flops 785920 | bytes 2101248 | tf_op jit(solution)/shard_map/reduce_sum | solution.py:76
  37.7 1.1 %collective-permute-done = f32[2,256]{1,0:T(2,128)S(1)} collective-permute-done((f32[2,256]{1,0:T(2,128)S(1)}, f32[2,256]{1,0:T(2,128)S(1)}, u32[]{:S(2)}, u32[]{:S(2)}) %collective-permute-start) | collective-permute-done | bytes 2080 | tf_op jit(solution)/shard_map/ppermute | solution.py:79
  38.9 2.8 %fusion.5 = (bf16[256,4,128]{2,1,0:T(4,128)(2,1)S(1)}, bf16[256,4,128]{2,1,0:T(4,128)(2,1)}) fusion(f32[4,128,256]{1,0,2:T(4,128)S(1)} %get-tuple-element.6, f32[256,4,128]{2,0,1:T(8,128)S(1)} %copy_convert_fusion, f32[256]{0:T(256)S(1)} %fusion.29, f32[256]{0:T(256)S(1)} %bitcast.75, f32[4,128]{1,0:T(4,128)S(1)} %copy-done.10), kind=kLoop, calls=%fused_computation.19 | loop fusion | flops 1048576 | bytes 1576960 | tf_op jit(solution)/shard_map/convert_element_type | solution.py:87
  41.7 0.9 %fusion.13 = f32[4,128,128]{2,1,0:T(8,128)} fusion(bf16[256,4,128]{0,2,1:T(8,128)(2,1)S(1)} %copy.61, bf16[256,4,128]{2,1,0:T(4,128)(2,1)S(1)} %get-tuple-element.7), kind=kOutput, calls=%fused_computation.37 | convolution fusion | flops 33554432 | bytes 786432 | tf_op jit(solution)/shard_map/cthd,cthe->chde/dot_general | solution.py:89
  43.0 3.6 %all-to-all-start.2 = ((f32[16,32,128]{2,1,0:T(8,128)}), f32[16,32,128]{2,1,0:T(8,128)S(1)}, u32[]{:S(2)}, u32[]{:S(2)}) async-start(f32[16,32,128]{2,1,0:T(8,128)} %bitcast.15), calls=%async_computation.2 | async-start | bytes 524288 | tf_op jit(solution)/shard_map/all_to_all | solution.py:34
  47.5 9.5 %all-to-all-done.2 = f32[16,32,128]{2,1,0:T(8,128)S(1)} async-done(((f32[16,32,128]{2,1,0:T(8,128)}), f32[16,32,128]{2,1,0:T(8,128)S(1)}, u32[]{:S(2)}, u32[]{:S(2)}) %all-to-all-start.2) | async-done | bytes 262176 | tf_op jit(solution)/shard_map/all_to_all | solution.py:34
  57.0 0.8 %reduce-window_subtract_fusion = f32[16,32,128]{2,1,0:T(8,128)} fusion(f32[16,32,128]{2,1,0:T(8,128)S(1)} %all-to-all-done.2), kind=kOutput, calls=%fused_computation.7 | output fusion | flops 1048576 | bytes 524288 | tf_op jit(solution)/shard_map/exclusive_scan/reduce_window_sum | solution.py:35
  57.7 3.5 %all-to-all-start.3 = ((f32[16,32,128]{2,1,0:T(8,128)}), f32[16,32,128]{2,1,0:T(8,128)S(1)}, u32[]{:S(2)}, u32[]{:S(2)}) async-start(f32[16,32,128]{2,1,0:T(8,128)} %reduce-window_subtract_fusion), calls=%async_computation.3 | async-start | bytes 524288 | tf_op jit(solution)/shard_map/all_to_all | solution.py:37
  61.3 1.1 %fusion.11 = f32[4,128,256]{2,1,0:T(8,128)} fusion(bf16[4,256,256]{2,1,0:T(8,128)(2,1)S(1)} %copy-done.3, bf16[256,4,128]{2,1,0:T(4,128)(2,1)S(1)} %get-tuple-element.7), kind=kOutput, calls=%fused_computation.35 | convolution fusion | flops 67108864 | bytes 1310720 | tf_op jit(solution)/shard_map/chts,cthe->cshe/dot_general | solution.py:108
  62.4 1.0 %fusion.35 = f32[4,128,256]{2,1,0:T(8,128)} fusion(bf16[256,4,128]{0,2,1:T(8,128)(2,1)S(1)} %copy.61, bf16[4,256,256]{2,1,0:T(8,128)(2,1)S(1)} %copy-done.5), kind=kOutput, calls=%fused_computation.62 | convolution fusion | flops 67108864 | bytes 1310720 | tf_op jit(solution)/shard_map/chts,cthd->cshd/dot_general | solution.py:104
  63.4 7.3 %all-to-all-done.3 = f32[16,32,128]{2,1,0:T(8,128)S(1)} async-done(((f32[16,32,128]{2,1,0:T(8,128)}), f32[16,32,128]{2,1,0:T(8,128)S(1)}, u32[]{:S(2)}, u32[]{:S(2)}) %all-to-all-start.3) | async-done | bytes 262176 | tf_op jit(solution)/shard_map/all_to_all | solution.py:37
  71.3 0.8 %fusion.10 = bf16[256,4,128]{2,1,0:T(4,128)(2,1)} fusion(bf16[4,128,256]{1,0,2:T(4,128)(2,1)S(1)} %copy.73), kind=kLoop, calls=%fused_computation.30 | loop fusion | bytes 524288 | tf_op jit(solution)/shard_map/convert_element_type | solution.py:118
  72.2 1.2 %convolution_add_fusion.1 = f32[4,128,256]{2,1,0:T(8,128)} fusion(f32[4,128,256]{2,1,0:T(8,128)S(1)} %copy-done.1, f32[4,128,128]{2,1,0:T(8,128)S(1)} %bitcast.71, bf16[256,4,128]{2,1,0:T(4,128)(2,1)S(1)} %copy-done), kind=kOutput, calls=%fused_computation.5 | convolution fusion | flops 201457664 | bytes 1572864 | tf_op jit(solution)/shard_map/cshe,chde->cshd/dot_general | solution.py:105
  73.4 1.3 %copy.66 = f32[4,128,256]{1,0,2:T(4,128)S(1)} copy(f32[4,128,256]{2,1,0:T(8,128)} %convolution_add_fusion.1) | data formatting | bytes 1048576 | tf_op jit(solution)/shard_map/add | solution.py:105
  74.6 1.8 %fusion.2 = (bf16[256,4,128]{2,1,0:T(4,128)(2,1)}, bf16[256,4,128]{2,1,0:T(4,128)(2,1)}) fusion(f32[4,128,256]{1,0,2:T(4,128)S(1)} %copy.66, f32[256,4,128]{2,0,1:T(8,128)S(1)} %copy_convert_fusion.1, f32[256,4,128]{2,0,1:T(8,128)S(1)} %copy_convert_fusion.2, f32[4,128,256]{1,0,2:T(4,128)S(1)} %copy.57), kind=kLoop, calls=%fused_computation.11 | loop fusion | flops 2359296 | bytes 2621440 | tf_op jit(solution)/shard_map/convert_element_type | solution.py:117
  (40 shorter events, 3.9 us)
Async XLA Ops:
  0.6 1.5 %copy-start = (bf16[256,4,128]{2,1,0:T(4,128)(2,1)S(1)}, bf16[256,4,128]{2,1,0:T(4,128)(2,1)}, u32[]{:S(2)}) copy-start(bf16[256,4,128]{2,1,0:T(4,128)(2,1)} %param.7) | copy-start | bytes 786436
  3.1 8.5 %copy-start.8 = (bf16[256,4,128]{2,1,0:T(4,128)(2,1)S(1)}, bf16[256,4,128]{2,1,0:T(4,128)(2,1)}, u32[]{:S(2)}) copy-start(bf16[256,4,128]{2,1,0:T(4,128)(2,1)} %param.5) | copy-start | bytes 786436
  3.1 18.3 %all-to-all-start = ((f32[16,32,128]{2,1,0:T(8,128)}), f32[16,32,128]{2,1,0:T(8,128)S(1)}, u32[]{:S(2)}, u32[]{:S(2)}) async-start(f32[16,32,128]{2,1,0:T(8,128)} %bitcast.1), calls=%async_computation | async-start | bytes 524288 | tf_op jit(solution)/shard_map/all_to_all | solution.py:34
  12.6 13.3 %copy-start.2 = (bf16[4,256,256]{2,1,0:T(8,128)(2,1)}, bf16[4,256,256]{2,1,0:T(8,128)(2,1)S(1)}, u32[]{:S(2)}) copy-start(bf16[4,256,256]{2,1,0:T(8,128)(2,1)S(1)} %fusion) | copy-start | bytes 1572868
  22.2 3.7 %copy-start.9 = (bf16[256,4,128]{2,1,0:T(4,128)(2,1)S(1)}, bf16[256,4,128]{2,1,0:T(4,128)(2,1)}, u32[]{:S(2)}) copy-start(bf16[256,4,128]{2,1,0:T(4,128)(2,1)} %param.9) | copy-start | bytes 786436
  22.2 12.9 %all-to-all-start.1 = ((f32[16,32,128]{2,1,0:T(8,128)}), f32[16,32,128]{2,1,0:T(8,128)S(1)}, u32[]{:S(2)}, u32[]{:S(2)}) async-start(f32[16,32,128]{2,1,0:T(8,128)} %reduce-window_subtract_fusion.1), calls=%async_computation.1 | async-start | bytes 524288 | tf_op jit(solution)/shard_map/all_to_all | solution.py:37
  35.1 1.0 %copy-start.7 = (f32[4,256,128]{2,1,0:T(8,128)S(1)}, f32[4,256,128]{2,1,0:T(8,128)}, u32[]{:S(2)}) copy-start(f32[4,256,128]{2,1,0:T(8,128)} %fusion.21) | copy-start | bytes 1572868
  35.1 1.0 %copy-start.10 = (f32[4,128]{1,0:T(4,128)S(1)}, f32[4,128]{1,0:T(4,128)}, u32[]{:S(2)}) copy-start(f32[4,128]{1,0:T(4,128)} %param.8) | copy-start | bytes 6148
  37.7 1.2 %collective-permute-start = (f32[2,256]{1,0:T(2,128)S(1)}, f32[2,256]{1,0:T(2,128)S(1)}, u32[]{:S(2)}, u32[]{:S(2)}) collective-permute-start(f32[2,256]{1,0:T(2,128)S(1)} %pad_maximum_fusion), channel_id=1, source_target_pairs={{0,1},{1,0},{2,3},{3,2},{4,5},{5,4},{6,7},{7,6},{8,9},{9,8},{10,11... | collective-permute-start | bytes 6152 | tf_op jit(solution)/shard_map/ppermute | solution.py:79
  43.0 3.6 %copy-start.4 = (bf16[4,256,256]{2,1,0:T(8,128)(2,1)}, bf16[4,256,256]{2,1,0:T(8,128)(2,1)S(1)}, u32[]{:S(2)}) copy-start(bf16[4,256,256]{2,1,0:T(8,128)(2,1)S(1)} %fusion.1) | copy-start | bytes 1572868
  43.0 14.0 %all-to-all-start.2 = ((f32[16,32,128]{2,1,0:T(8,128)}), f32[16,32,128]{2,1,0:T(8,128)S(1)}, u32[]{:S(2)}, u32[]{:S(2)}) async-start(f32[16,32,128]{2,1,0:T(8,128)} %bitcast.15), calls=%async_computation.2 | async-start | bytes 524288 | tf_op jit(solution)/shard_map/all_to_all | solution.py:34
  47.5 13.8 %copy-start.3 = (bf16[4,256,256]{2,1,0:T(8,128)(2,1)S(1)}, bf16[4,256,256]{2,1,0:T(8,128)(2,1)}, u32[]{:S(2)}) copy-start(bf16[4,256,256]{2,1,0:T(8,128)(2,1)} %copy-done.2) | copy-start | bytes 1572868
  57.7 13.0 %all-to-all-start.3 = ((f32[16,32,128]{2,1,0:T(8,128)}), f32[16,32,128]{2,1,0:T(8,128)S(1)}, u32[]{:S(2)}, u32[]{:S(2)}) async-start(f32[16,32,128]{2,1,0:T(8,128)} %reduce-window_subtract_fusion), calls=%async_computation.3 | async-start | bytes 524288 | tf_op jit(solution)/shard_map/all_to_all | solution.py:37
  61.3 1.1 %copy-start.5 = (bf16[4,256,256]{2,1,0:T(8,128)(2,1)S(1)}, bf16[4,256,256]{2,1,0:T(8,128)(2,1)}, u32[]{:S(2)}) copy-start(bf16[4,256,256]{2,1,0:T(8,128)(2,1)} %copy-done.4) | copy-start | bytes 1572868
  62.4 8.3 %copy-start.6 = (f32[4,128,256]{2,1,0:T(8,128)S(1)}, f32[4,128,256]{2,1,0:T(8,128)}, u32[]{:S(2)}) copy-start(f32[4,128,256]{2,1,0:T(8,128)} %fusion.11) | copy-start | bytes 1572868
  71.1 1.0 %copy-start.1 = (f32[4,128,256]{2,1,0:T(8,128)S(1)}, f32[4,128,256]{2,1,0:T(8,128)}, u32[]{:S(2)}) copy-start(f32[4,128,256]{2,1,0:T(8,128)} %fusion.35) | copy-start | bytes 1572868

commit v10 on v6

--- a/solution.py
+++ b/solution.py
@@ -2,6 +2,7 @@
 import jax.numpy as jnp
 from jax import lax
 from jax.sharding import PartitionSpec as P
+from jax.experimental import pallas as pl
 
 GROUP = 256
 
@@ -43,6 +44,47 @@
 
 def upper_sum(own_total):
     return exclusive_scan(own_total, True)
+
+
+def mm(lhs, rhs, lhs_dim, rhs_dim):
+    dims = (((lhs_dim,), (rhs_dim,)), ((), ()))
+    return lax.dot_general(lhs, rhs, dims, preferred_element_type=jnp.float32)
+
+
+def backward_tail(query_raw, key_raw, value_raw, delta, bscore, attn, state, grad_state):
+    tok_rows, head_count, width = query_raw.shape
+    blocks = tok_rows // GROUP
+
+    def kernel(qr_ref, kr_ref, v_ref, d_ref, bs_ref, at_ref, st_ref, gs_ref, qg_ref, kg_ref, vg_ref):
+        for h in range(head_count):
+            q_raw = qr_ref[:, h, :].astype(jnp.float32)
+            k_raw = kr_ref[:, h, :].astype(jnp.float32)
+            q_act = jax.nn.silu(q_raw).astype(jnp.bfloat16)
+            k_act = jax.nn.silu(k_raw).astype(jnp.bfloat16)
+            value = v_ref[:, h, :]
+            delta_h = d_ref[:, h, :]
+            bs = bs_ref[h]
+            at = at_ref[h]
+            state_b = st_ref[h].astype(jnp.bfloat16)
+            grad_b = gs_ref[h].astype(jnp.bfloat16)
+            dq = mm(bs, k_act, 1, 0) + mm(delta_h, state_b, 1, 1)
+            dk = mm(bs, q_act, 0, 0) + mm(value, grad_b, 1, 1)
+            dv = mm(at, delta_h, 0, 0) + mm(k_act, grad_b, 1, 0)
+            qg_ref[:, h, :] = (dq * silu_grad(q_raw)).astype(jnp.bfloat16)
+            kg_ref[:, h, :] = (dk * silu_grad(k_raw)).astype(jnp.bfloat16)
+            vg_ref[:, h, :] = dv.astype(jnp.bfloat16)
+
+    rows = pl.BlockSpec((GROUP, head_count, width), lambda c: (c, 0, 0))
+    square = pl.BlockSpec((None, head_count, GROUP, GROUP), lambda c: (c, 0, 0, 0))
+    states = pl.BlockSpec((None, head_count, width, width), lambda c: (c, 0, 0, 0))
+    out = jax.ShapeDtypeStruct(query_raw.shape, jnp.bfloat16)
+    return pl.pallas_call(
+        kernel,
+        grid=(blocks,),
+        in_specs=[rows, rows, rows, rows, square, square, states, states],
+        out_specs=[rows, rows, rows],
+        out_shape=[out, out, out],
+    )(query_raw, key_raw, value_raw, delta, bscore, attn, state, grad_state)
 
 
 def body(query_raw, key_raw, value_raw, out_gain, out_grad):
@@ -92,24 +134,9 @@
         grad_state = after[None] + (lax.cumsum(block_grad, axis=0, reverse=True) - block_grad)
     bscore = jnp.einsum("cthe,cshe->chts", delta_blk, value_blk, preferred_element_type=jnp.float32)
     bscore = jnp.where(mask, bscore, 0.0).astype(jnp.bfloat16)
-    dquery = jnp.einsum("chts,cshd->cthd", bscore, key_act, preferred_element_type=jnp.float32)
-    dquery = dquery + jnp.einsum(
-        "cthe,chde->cthd", delta_blk, state_b, preferred_element_type=jnp.float32, precision=lax.Precision.HIGHEST
+    query_grad, key_grad, value_grad = backward_tail(
+        query_raw, key_raw, value_raw, delta, bscore, attn, state_b, grad_state
     )
-    dkey = jnp.einsum("chts,cthd->cshd", bscore, query_act, preferred_element_type=jnp.float32)
-    dkey = dkey + jnp.einsum(
-        "cshe,chde->cshd", value_blk, grad_state, preferred_element_type=jnp.float32, precision=lax.Precision.HIGHEST
-    )
-    dvalue = jnp.einsum("chts,cthe->cshe", attn, delta_blk, preferred_element_type=jnp.float32)
-    dvalue = dvalue + jnp.einsum(
-        "cshd,chde->cshe", key_act, grad_state, preferred_element_type=jnp.float32, precision=lax.Precision.HIGHEST
-    )
-    whole = (tok_rows, head_count, width)
-    query_grad = (dquery.reshape(whole) * silu_grad(query_raw.astype(jnp.float32))).astype(
-        jnp.bfloat16
-    )
-    key_grad = (dkey.reshape(whole) * silu_grad(key_raw.astype(jnp.float32))).astype(jnp.bfloat16)
-    value_grad = dvalue.reshape(whole).astype(jnp.bfloat16)
     return (normed_out, query_grad, key_grad, value_grad)
 
 

time: 70 us -> 80.1 us (1.14)
  blocking collectives: 0 us -> 13.5 us
  Pallas kernels: 0 us -> 9.99 us
  waiting for transfers between devices: 35.8 us -> 26.5 us
  other arithmetic: 1.76 us -> 5.93 us
  starting transfers between devices: 19.1 us -> 15.8 us
  matrix products: 6.03 us -> 3.28 us
  local copies, waits for them, and re-layouts: 5.75 us -> 3.71 us
    all_to_all x0 -> x1, blocking collectives: none -> 13.5 us  [exclusive_scan(): lax.all_to_all(rows.reshape(count, chunk, width), 'seq', 0, 0, tiled=True)]
    pallas_call x0 -> x1, Pallas kernels: none -> 9.99 us  [backward_tail(): pl.pallas_call(kernel, grid=(blocks,), in_specs=[rows, rows, rows, rows,...]
    all_to_all x2 -> x1, waiting for transfers between devices: 17.4 us -> 9.35 us  [exclusive_scan(): lax.all_to_all(rows.reshape(count, chunk, width), 'seq', 0, 0, tiled=True)]
    all_to_all x2 -> x1, starting transfers between devices: 12 us -> 8.45 us  [exclusive_scan(): lax.all_to_all(rows.reshape(count, chunk, width), 'seq', 0, 0, tiled=True)]
    unnamed x15 -> x16, local copies, waits for them, and re-layouts: 5.75 us -> 2.91 us
    dot_general x6 -> x0, matrix products: 2.33 us -> none  [the longest x1 0.51 us: body(): jnp.einsum('cshe,chde->cshd', value_blk, grad_state, preferred_element_ty...]
    convert_element_type x0 -> x2, other arithmetic: none -> 1.52 us  [the longest x1 1.23 us: body(): jax.nn.silu(key_raw.astype(jnp.float32)).astype(jnp.bfloat16)]
    convert_element_type x1, other arithmetic: 0.18 us -> 1.69 us  [body(): delta = (grad_in * inv_rms[:, None, None] - mixed * (cross_total * inv_rm...]
  transfers between devices with their start and end apart: 5 -> 4, of which waited for: 5 -> 4; matrix products, arithmetic and copies ran while one was open for 5% -> 3% of each run, Pallas kernels for 0% -> 0%
where the time goes in v10:
time: 80.1 us; the launch traced here: 79.6 us
  waiting for transfers between devices  26.5 us (33%)
  starting transfers between devices  15.8 us (20%)
  blocking collectives  13.5 us (17%)
  Pallas kernels  9.99 us (12%)
  other arithmetic  5.93 us (7%)
  local copies, waits for them, and re-layouts  3.71 us (5%)
  matrix products  3.28 us (4%)
    all_to_all x2, waiting for transfers between devices, exclusive_scan(): spread = lax.all_to_all(prefix, 'seq', 0, 0, tiled=True)  16 us
    all_to_all x1, blocking collectives, exclusive_scan(): lax.all_to_all(rows.reshape(count, chunk, width), 'seq', 0, 0, tiled=True)  13.5 us
    pallas_call x1, Pallas kernels, backward_tail(): pl.pallas_call(kernel, grid=(blocks,), in_specs=[rows, rows, rows, rows,...  9.99 us
    all_to_all x1, waiting for transfers between devices, exclusive_scan(): lax.all_to_all(rows.reshape(count, chunk, width), 'seq', 0, 0, tiled=True)  9.35 us
    all_to_all x1, starting transfers between devices, exclusive_scan(): lax.all_to_all(rows.reshape(count, chunk, width), 'seq', 0, 0, tiled=True)  8.45 us
    all_to_all x2, starting transfers between devices, exclusive_scan(): spread = lax.all_to_all(prefix, 'seq', 0, 0, tiled=True)  7.27 us
    unnamed x16, local copies, waits for them, and re-layouts  2.91 us
    convert_element_type x1, other arithmetic, body(): delta = (grad_in * inv_rms[:, None, None] - mixed * (cross_total * inv_rm...  1.69 us
  transfers between devices with their start and end apart: 4, of which 4 were waited for; matrix products, arithmetic and copies ran while one was open for 3% of the time, Pallas kernels for 0%

profile of v10, /device:TPU:0, one launch (start us, length us, event | category | flops | bytes accessed | tf_op | source)
XLA Modules:
  0.0 79.6 jit_solution(18022311685514204364)
XLA Ops:
  0.6 1.2 %fusion.8 = bf16[256,4,128]{2,1,0:T(4,128)(2,1)S(1)} fusion(bf16[256,4,128]{2,1,0:T(4,128)(2,1)} %kr_ref.1), kind=kLoop, calls=%fused_computation.16 | loop fusion | flops 786432 | bytes 524288 | tf_op jit(solution)/shard_map/convert_element_type | solution.py:95
  2.1 0.8 copy-done.1
  2.8 0.9 %fusion.21 = f32[4,128,128]{2,1,0:T(8,128)} fusion(bf16[256,4,128]{0,2,1:T(8,128)(2,1)S(1)} %copy.25, bf16[256,4,128]{2,1,0:T(4,128)(2,1)S(1)} %copy-done.1), kind=kOutput, calls=%fused_computation.36 | convolution fusion | flops 33554432 | bytes 786432 | tf_op jit(solution)/shard_map/cshd,cshe->chde/dot_general | solution.py:98
  3.7 8.4 %all-to-all-start = ((f32[16,32,128]{2,1,0:T(8,128)}), f32[16,32,128]{2,1,0:T(8,128)S(1)}, u32[]{:S(2)}, u32[]{:S(2)}) async-start(f32[16,32,128]{2,1,0:T(8,128)} %bitcast.1), calls=%async_computation | async-start | bytes 524288 | tf_op jit(solution)/shard_map/all_to_all | solution.py:34
  12.2 0.3 fusion.5
  12.7 9.4 %all-to-all-done = f32[16,32,128]{2,1,0:T(8,128)S(1)} async-done(((f32[16,32,128]{2,1,0:T(8,128)}), f32[16,32,128]{2,1,0:T(8,128)S(1)}, u32[]{:S(2)}, u32[]{:S(2)}) %all-to-all-start) | async-done | bytes 262176 | tf_op jit(solution)/shard_map/all_to_all | solution.py:34
  22.1 0.7 reduce-window_subtract_fusion.1
  22.8 3.5 %all-to-all-start.1 = ((f32[16,32,128]{2,1,0:T(8,128)}), f32[16,32,128]{2,1,0:T(8,128)S(1)}, u32[]{:S(2)}, u32[]{:S(2)}) async-start(f32[16,32,128]{2,1,0:T(8,128)} %reduce-window_subtract_fusion.1), calls=%async_computation.1 | async-start | bytes 524288 | tf_op jit(solution)/shard_map/all_to_all | solution.py:37
  26.3 0.3 fusion
  26.7 0.3 fusion.18
  27.0 0.5 copy-done
  27.7 7.8 %all-to-all-done.1 = f32[16,32,128]{2,1,0:T(8,128)S(1)} async-done(((f32[16,32,128]{2,1,0:T(8,128)}), f32[16,32,128]{2,1,0:T(8,128)S(1)}, u32[]{:S(2)}, u32[]{:S(2)}) %all-to-all-start.1) | async-done | bytes 262176 | tf_op jit(solution)/shard_map/all_to_all | solution.py:37
  35.6 0.4 fusion.29
  36.5 0.7 copy-done.4
  37.2 1.2 %fusion.9 = (f32[256]{0:T(256)S(1)}, f32[256]{0:T(256)S(1)}, f32[4,128,256]{1,0,2:T(4,128)S(1)}) fusion(f32[4,128]{1,0:T(4,128)S(1)} %copy-done.7, bf16[256,4,128]{2,1,0:T(4,128)(2,1)S(1)} %copy-done.4, f32[4,128,256]{1,0,2:T(4,128)S(1)} %copy.29, f32[4,256,128]{2,0,1:T(4,128)S(1)} %copy.24), kind=kLoop, calls=%fused_computation.21 | loop fusion | flops 916992 | bytes 1839104 | tf_op jit(solution)/shard_map/reduce_sum | solution.py:113
  38.4 1.1 %collective-permute-done = f32[2,256]{1,0:T(2,128)S(1)} collective-permute-done((f32[2,256]{1,0:T(2,128)S(1)}, f32[2,256]{1,0:T(2,128)S(1)}, u32[]{:S(2)}, u32[]{:S(2)}) %collective-permute-start) | collective-permute-done | bytes 2080 | tf_op jit(solution)/shard_map/ppermute | solution.py:116
  39.6 1.7 %fusion.14 = (bf16[256,4,128]{2,1,0:T(4,128)(2,1)S(1)}, bf16[256,4,128]{2,1,0:T(4,128)(2,1)}) fusion(f32[4,128,256]{1,0,2:T(4,128)S(1)} %get-tuple-element.12, bf16[256,4,128]{2,1,0:T(4,128)(2,1)S(1)} %copy-done.4, f32[256]{0:T(256)S(1)} %fusion.24, f32[256]{0:T(256)S(1)} %bitcast.55, f32[4,128]{1,0:T(4,128)S(1)} %copy-done.7), kind=kLoop, calls=%fused_computation.26 | loop fusion | flops 1179648 | bytes 1314816 | tf_op jit(solution)/shard_map/convert_element_type | solution.py:124
  41.5 13.5 %all_to_all.20 = f32[16,32,128]{2,1,0:T(8,128)S(1)} all-to-all(f32[16,32,128]{2,1,0:T(8,128)S(1)} %bitcast.49), channel_id=1, replica_groups=mesh['seq'=16,'head'=2] {'seq'}, dimensions={0} | all-to-all | bytes 524288 | tf_op jit(solution)/shard_map/all_to_all | solution.py:34
  55.1 0.8 reduce-window_subtract_fusion
  55.9 3.7 %all-to-all-start.3 = ((f32[16,32,128]{2,1,0:T(8,128)}), f32[16,32,128]{2,1,0:T(8,128)S(1)}, u32[]{:S(2)}, u32[]{:S(2)}) async-start(f32[16,32,128]{2,1,0:T(8,128)} %reduce-window_subtract_fusion), calls=%async_computation.3 | async-start | bytes 524288 | tf_op jit(solution)/shard_map/all_to_all | solution.py:37
  59.6 1.1 %fusion.2.bs_ref = bf16[1,4,256,256]{3,2,1,0:T(8,128)(2,1)} fusion(pred[256,256]{1,0:T(8,128)(4,1)S(1)} %iota_compare_fusion, bf16[256,4,128]{2,1,0:T(4,128)(2,1)S(1)} %get-tuple-element.13.d_ref, bf16[256,4,128]{2,1,0:T(4,128)(2,1)S(1)} %copy-done.1), kind=kOutput, calls=%fused_computation.4 | convolution fusion | flops 67633152 | bytes 1114112 | tf_op jit(solution)/shard_map/cthe,cshe->chts/dot_general | solution.py:135
  60.7 8.2 %all-to-all-done.3 = f32[16,32,128]{2,1,0:T(8,128)S(1)} async-done(((f32[16,32,128]{2,1,0:T(8,128)}), f32[16,32,128]{2,1,0:T(8,128)S(1)}, u32[]{:S(2)}, u32[]{:S(2)}) %all-to-all-start.3) | async-done | bytes 262176 | tf_op jit(solution)/shard_map/all_to_all | solution.py:37
  68.9 0.7 copy-done.6
  69.6 10.0 %shard_map.84 = (bf16[256,4,128]{2,1,0:T(4,128)(2,1)}, bf16[256,4,128]{2,1,0:T(4,128)(2,1)}, bf16[256,4,128]{2,1,0:T(4,128)(2,1)}) custom-call(bf16[256,4,128]{2,1,0:T(4,128)(2,1)} %qr_ref.1, bf16[256,4,128]{2,1,0:T(4,128)(2,1)} %kr_ref.1, bf16[256,4,128]{2,1,0:T(4,128)(2,1)} %v_ref.1, bf16[256,4,128]{2,1,0:T(4,128)(2,1)} %copy-done.2, ...), custom_call_target="tpu_custom_call" | custom-call | tf_op jit(solution)/shard_map/pallas_call | solution.py:81
  (23 shorter events, 1.4 us)
Async XLA Ops:
  1.9 1.0 %copy-start.1 = (bf16[256,4,128]{2,1,0:T(4,128)(2,1)S(1)}, bf16[256,4,128]{2,1,0:T(4,128)(2,1)}, u32[]{:S(2)}) copy-start(bf16[256,4,128]{2,1,0:T(4,128)(2,1)} %v_ref.1) | copy-start | bytes 786436
  3.7 8.5 %copy-start.5 = (bf16[256,4,128]{2,1,0:T(4,128)(2,1)S(1)}, bf16[256,4,128]{2,1,0:T(4,128)(2,1)}, u32[]{:S(2)}) copy-start(bf16[256,4,128]{2,1,0:T(4,128)(2,1)} %qr_ref.1) | copy-start | bytes 786436
  3.7 18.3 %all-to-all-start = ((f32[16,32,128]{2,1,0:T(8,128)}), f32[16,32,128]{2,1,0:T(8,128)S(1)}, u32[]{:S(2)}, u32[]{:S(2)}) async-start(f32[16,32,128]{2,1,0:T(8,128)} %bitcast.1), calls=%async_computation | async-start | bytes 524288 | tf_op jit(solution)/shard_map/all_to_all | solution.py:34
  22.8 12.8 %all-to-all-start.1 = ((f32[16,32,128]{2,1,0:T(8,128)}), f32[16,32,128]{2,1,0:T(8,128)S(1)}, u32[]{:S(2)}, u32[]{:S(2)}) async-start(f32[16,32,128]{2,1,0:T(8,128)} %reduce-window_subtract_fusion.1), calls=%async_computation.1 | async-start | bytes 524288 | tf_op jit(solution)/shard_map/all_to_all | solution.py:37
  26.7 0.8 copy-start
  35.6 0.7 copy-start.3
  36.3 0.9 %copy-start.4 = (bf16[256,4,128]{2,1,0:T(4,128)(2,1)S(1)}, bf16[256,4,128]{2,1,0:T(4,128)(2,1)}, u32[]{:S(2)}) copy-start(bf16[256,4,128]{2,1,0:T(4,128)(2,1)} %param.9) | copy-start | bytes 786436
  36.3 1.0 %copy-start.7 = (f32[4,128]{1,0:T(4,128)S(1)}, f32[4,128]{1,0:T(4,128)}, u32[]{:S(2)}) copy-start(f32[4,128]{1,0:T(4,128)} %param.8) | copy-start | bytes 6148
  38.4 1.2 %collective-permute-start = (f32[2,256]{1,0:T(2,128)S(1)}, f32[2,256]{1,0:T(2,128)S(1)}, u32[]{:S(2)}, u32[]{:S(2)}) collective-permute-start(f32[2,256]{1,0:T(2,128)S(1)} %pad_maximum_fusion), channel_id=1, source_target_pairs={{0,1},{1,0},{2,3},{3,2},{4,5},{5,4},{6,7},{7,6},{8,9},{9,8},{10,11... | collective-permute-start | bytes 6152 | tf_op jit(solution)/shard_map/ppermute | solution.py:116
  41.3 18.3 %copy-start.2 = (bf16[256,4,128]{2,1,0:T(4,128)(2,1)}, bf16[256,4,128]{2,1,0:T(4,128)(2,1)S(1)}, u32[]{:S(2)}) copy-start(bf16[256,4,128]{2,1,0:T(4,128)(2,1)S(1)} %get-tuple-element.13.d_ref) | copy-start | bytes 786436
  55.9 13.0 %all-to-all-start.3 = ((f32[16,32,128]{2,1,0:T(8,128)}), f32[16,32,128]{2,1,0:T(8,128)S(1)}, u32[]{:S(2)}, u32[]{:S(2)}) async-start(f32[16,32,128]{2,1,0:T(8,128)} %reduce-window_subtract_fusion), calls=%async_computation.3 | async-start | bytes 524288 | tf_op jit(solution)/shard_map/all_to_all | solution.py:37
  68.9 0.7 copy-start.6

commit v11 on v9

--- a/solution.py
+++ b/solution.py
@@ -47,7 +47,8 @@
 
 
 def natural(array):
-    return with_layout_constraint(array, Layout(tuple(range(array.ndim))))
+    order = tuple(range(array.ndim - 3)) + (array.ndim - 2, array.ndim - 3, array.ndim - 1)
+    return with_layout_constraint(array, Layout(order))
 
 
 def body(query_raw, key_raw, value_raw, out_gain, out_grad):

time: 77.1 us -> 71 us (0.921)
  other arithmetic: 9.7 us -> 1.8 us
  waiting for transfers between devices: 34.7 us -> 36.7 us
  local copies, waits for them, and re-layouts: 3.34 us -> 4.6 us
  matrix products: 8.46 us -> 7.29 us
    unnamed x22 -> x14, local copies, waits for them, and re-layouts: 0.7 us -> 4.6 us
    convert_element_type x6 -> x0, other arithmetic: 3.74 us -> none  [the longest x1 1.8 us: body(): (dkey.reshape(whole) * silu_grad(key_raw.astype(jnp.float32))).astype(jnp...]
    convert_element_type x1, other arithmetic: 2.82 us -> 0.22 us  [body(): delta = (grad_in * inv_rms[:, None, None] - mixed * (cross_total * inv_rm...]
    all_to_all x2, waiting for transfers between devices: 15.3 us -> 17.1 us  [exclusive_scan(): spread = lax.all_to_all(prefix, 'seq', 0, 0, tiled=True)]
    add x3 -> x0, local copies, waits for them, and re-layouts: 1.67 us -> none  [the longest x1 1.26 us: body(): dkey + jnp.einsum('cshe,chde->cshd', value_blk, grad_state, preferred_ele...]
    reduce_sum x1 -> x0, other arithmetic: 1.56 us -> none  [body(): sq_part = jnp.sum(mixed * mixed, axis=(1, 2))]
    dot_general x1, matrix products: 0.98 us -> 2.01 us  [body(): jnp.einsum('cshd,cshe->chde', key_act, value_blk, preferred_element_type=...]
    convert_element_type x2 -> x0, local copies, waits for them, and re-layouts: 0.97 us -> none  [the longest x1 0.8 us: body(): value_grad = dvalue.reshape(whole).astype(jnp.bfloat16)]
  transfers between devices with their start and end apart: 5 -> 5, of which waited for: 5 -> 5; matrix products, arithmetic and copies ran while one was open for 7% -> 5% of each run, Pallas kernels for 0% -> 0%
where the time goes in v11:
time: 71 us; the launch traced here: 70.3 us
  waiting for transfers between devices  36.7 us (52%)
  starting transfers between devices  19.1 us (27%)
  matrix products  7.29 us (10%)
  local copies, waits for them, and re-layouts  4.6 us (6%)
  other arithmetic  1.8 us (3%)
  between operations  0.81 us (1%)
    all_to_all x2, waiting for transfers between devices, exclusive_scan(): lax.all_to_all(rows.reshape(count, chunk, width), 'seq', 0, 0, tiled=True)  18.4 us
    all_to_all x2, waiting for transfers between devices, exclusive_scan(): spread = lax.all_to_all(prefix, 'seq', 0, 0, tiled=True)  17.1 us
    all_to_all x2, starting transfers between devices, exclusive_scan(): lax.all_to_all(rows.reshape(count, chunk, width), 'seq', 0, 0, tiled=True)  11.9 us
    all_to_all x2, starting transfers between devices, exclusive_scan(): spread = lax.all_to_all(prefix, 'seq', 0, 0, tiled=True)  7.21 us
    unnamed x14, local copies, waits for them, and re-layouts  4.6 us
    dot_general x1, matrix products, body(): jnp.einsum('cshd,cshe->chde', key_act, value_blk, preferred_element_type=...  2.01 us
    another operation x2, other arithmetic, exclusive_scan(): inclusive = lax.cumsum(gathered, axis=0, reverse=reverse)  1.51 us
  transfers between devices with their start and end apart: 5, of which 5 were waited for; matrix products, arithmetic and copies ran while one was open for 5% of the time, Pallas kernels for 0%

profile of v11, /device:TPU:0, one launch (start us, length us, event | category | flops | bytes accessed | tf_op | source)
XLA Modules:
  0.0 70.3 jit_solution(18444923175374161052)
XLA Ops:
  0.6 0.9 %copy-done = bf16[256,4,128]{2,1,0:T(4,128)(2,1)S(1)} copy-done((bf16[256,4,128]{2,1,0:T(4,128)(2,1)S(1)}, bf16[256,4,128]{2,1,0:T(4,128)(2,1)}, u32[]{:S(2)}) %copy-start) | copy-done | bytes 262168
  1.6 2.0 %fusion.26 = f32[4,128,128]{2,1,0:T(8,128)} fusion(bf16[256,4,128]{2,1,0:T(4,128)(2,1)S(1)} %copy-done, bf16[256,4,128]{2,1,0:T(4,128)(2,1)} %param.6), kind=kOutput, calls=%fused_computation.47 | convolution fusion | flops 34340864 | bytes 786432 | tf_op jit(solution)/shard_map/cshd,cshe->chde/dot_general | solution.py:62
  3.6 8.3 %all-to-all-start = ((f32[16,32,128]{2,1,0:T(8,128)}), f32[16,32,128]{2,1,0:T(8,128)S(1)}, u32[]{:S(2)}, u32[]{:S(2)}) async-start(f32[16,32,128]{2,1,0:T(8,128)} %bitcast.1), calls=%async_computation | async-start | bytes 524288 | tf_op jit(solution)/shard_map/all_to_all | solution.py:34
  12.0 9.8 %all-to-all-done = f32[16,32,128]{2,1,0:T(8,128)S(1)} async-done(((f32[16,32,128]{2,1,0:T(8,128)}), f32[16,32,128]{2,1,0:T(8,128)S(1)}, u32[]{:S(2)}, u32[]{:S(2)}) %all-to-all-start) | async-done | bytes 262176 | tf_op jit(solution)/shard_map/all_to_all | solution.py:34
  21.8 0.7 %reduce-window_subtract_fusion.1 = f32[16,32,128]{2,1,0:T(8,128)} fusion(f32[16,32,128]{2,1,0:T(8,128)S(1)} %all-to-all-done), kind=kOutput, calls=%fused_computation.19 | output fusion | flops 1048576 | bytes 524288 | tf_op jit(solution)/shard_map/exclusive_scan/reduce_window_sum | solution.py:35
  22.5 3.7 %all-to-all-start.1 = ((f32[16,32,128]{2,1,0:T(8,128)}), f32[16,32,128]{2,1,0:T(8,128)S(1)}, u32[]{:S(2)}, u32[]{:S(2)}) async-start(f32[16,32,128]{2,1,0:T(8,128)} %reduce-window_subtract_fusion.1), calls=%async_computation.1 | async-start | bytes 524288 | tf_op jit(solution)/shard_map/all_to_all | solution.py:37
  26.2 0.4 fusion
  27.0 8.4 %all-to-all-done.1 = f32[16,32,128]{2,1,0:T(8,128)S(1)} async-done(((f32[16,32,128]{2,1,0:T(8,128)}), f32[16,32,128]{2,1,0:T(8,128)S(1)}, u32[]{:S(2)}, u32[]{:S(2)}) %all-to-all-start.1) | async-done | bytes 262176 | tf_op jit(solution)/shard_map/all_to_all | solution.py:37
  35.4 0.6 multiply_reduce_fusion.1
  36.1 1.1 %collective-permute-done = f32[2,256]{1,0:T(2,128)S(1)} collective-permute-done((f32[2,256]{1,0:T(2,128)S(1)}, f32[2,256]{1,0:T(2,128)S(1)}, u32[]{:S(2)}, u32[]{:S(2)}) %collective-permute-start) | collective-permute-done | bytes 2080 | tf_op jit(solution)/shard_map/ppermute | solution.py:80
  37.6 1.1 %fusion.39 = f32[4,128,128]{2,1,0:T(8,128)} fusion(bf16[256,4,128]{2,0,1:T(8,128)(2,1)S(1)} %get-tuple-element.10, bf16[256,4,128]{2,1,0:T(4,128)(2,1)S(1)} %copy-done.3), kind=kOutput, calls=%fused_computation.59 | convolution fusion | flops 34340864 | bytes 786432 | tf_op jit(solution)/shard_map/cthd,cthe->chde/dot_general | solution.py:90
  38.9 0.9 %copy.20 = bf16[256,4,128]{2,1,0:T(4,128)(2,1)} copy(bf16[256,4,128]{2,0,1:T(8,128)(2,1)S(1)} %get-tuple-element.11) | data formatting | bytes 524288
  39.8 3.5 %all-to-all-start.2 = ((f32[16,32,128]{2,1,0:T(8,128)}), f32[16,32,128]{2,1,0:T(8,128)S(1)}, u32[]{:S(2)}, u32[]{:S(2)}) async-start(f32[16,32,128]{2,1,0:T(8,128)} %bitcast.15), calls=%async_computation.2 | async-start | bytes 524288 | tf_op jit(solution)/shard_map/all_to_all | solution.py:34
  43.7 0.5 fusion.8
  44.3 0.9 %copy.21 = bf16[256,4,128]{2,1,0:T(4,128)(2,1)} copy(bf16[256,4,128]{2,0,1:T(8,128)(2,1)S(1)} %fusion.8) | data formatting | bytes 524288
  45.2 8.6 %all-to-all-done.2 = f32[16,32,128]{2,1,0:T(8,128)S(1)} async-done(((f32[16,32,128]{2,1,0:T(8,128)}), f32[16,32,128]{2,1,0:T(8,128)S(1)}, u32[]{:S(2)}, u32[]{:S(2)}) %all-to-all-start.2) | async-done | bytes 262176 | tf_op jit(solution)/shard_map/all_to_all | solution.py:34
  53.8 0.8 %reduce-window_subtract_fusion = f32[16,32,128]{2,1,0:T(8,128)} fusion(f32[16,32,128]{2,1,0:T(8,128)S(1)} %all-to-all-done.2), kind=kOutput, calls=%fused_computation.18 | output fusion | flops 1048576 | bytes 524288 | tf_op jit(solution)/shard_map/exclusive_scan/reduce_window_sum | solution.py:35
  54.6 3.5 %all-to-all-start.3 = ((f32[16,32,128]{2,1,0:T(8,128)}), f32[16,32,128]{2,1,0:T(8,128)S(1)}, u32[]{:S(2)}, u32[]{:S(2)}) async-start(f32[16,32,128]{2,1,0:T(8,128)} %reduce-window_subtract_fusion), calls=%async_computation.3 | async-start | bytes 524288 | tf_op jit(solution)/shard_map/all_to_all | solution.py:37
  58.5 0.4 fusion.41
  58.9 8.6 %all-to-all-done.3 = f32[16,32,128]{2,1,0:T(8,128)S(1)} async-done(((f32[16,32,128]{2,1,0:T(8,128)}), f32[16,32,128]{2,1,0:T(8,128)S(1)}, u32[]{:S(2)}, u32[]{:S(2)}) %all-to-all-start.3) | async-done | bytes 262176 | tf_op jit(solution)/shard_map/all_to_all | solution.py:37
  67.5 0.4 fusion.11
  68.0 0.9 %copy.23 = bf16[256,4,128]{2,1,0:T(4,128)(2,1)} copy(bf16[256,4,128]{2,0,1:T(8,128)(2,1)S(1)} %fusion.11) | data formatting | bytes 524288
  68.9 0.5 fusion.9
  69.4 0.9 %copy.22 = bf16[256,4,128]{2,1,0:T(4,128)(2,1)} copy(bf16[256,4,128]{2,0,1:T(8,128)(2,1)S(1)} %fusion.9) | data formatting | bytes 524288
  (20 shorter events, 1.6 us)
Async XLA Ops:
  0.6 1.0 %copy-start = (bf16[256,4,128]{2,1,0:T(4,128)(2,1)S(1)}, bf16[256,4,128]{2,1,0:T(4,128)(2,1)}, u32[]{:S(2)}) copy-start(bf16[256,4,128]{2,1,0:T(4,128)(2,1)} %param.7) | copy-start | bytes 786436
  3.6 18.2 %all-to-all-start = ((f32[16,32,128]{2,1,0:T(8,128)}), f32[16,32,128]{2,1,0:T(8,128)S(1)}, u32[]{:S(2)}, u32[]{:S(2)}) async-start(f32[16,32,128]{2,1,0:T(8,128)} %bitcast.1), calls=%async_computation | async-start | bytes 524288 | tf_op jit(solution)/shard_map/all_to_all | solution.py:34
  22.5 3.7 %copy-start.3 = (bf16[256,4,128]{2,1,0:T(4,128)(2,1)S(1)}, bf16[256,4,128]{2,1,0:T(4,128)(2,1)}, u32[]{:S(2)}) copy-start(bf16[256,4,128]{2,1,0:T(4,128)(2,1)} %param.5) | copy-start | bytes 786436
  22.5 3.7 %copy-start.4 = (bf16[256,4,128]{2,1,0:T(4,128)(2,1)S(1)}, bf16[256,4,128]{2,1,0:T(4,128)(2,1)}, u32[]{:S(2)}) copy-start(bf16[256,4,128]{2,1,0:T(4,128)(2,1)} %param.6) | copy-start | bytes 786436
  22.5 12.9 %all-to-all-start.1 = ((f32[16,32,128]{2,1,0:T(8,128)}), f32[16,32,128]{2,1,0:T(8,128)S(1)}, u32[]{:S(2)}, u32[]{:S(2)}) async-start(f32[16,32,128]{2,1,0:T(8,128)} %reduce-window_subtract_fusion.1), calls=%async_computation.1 | async-start | bytes 524288 | tf_op jit(solution)/shard_map/all_to_all | solution.py:37
  26.7 8.8 %copy-start.1 = (bf16[256,4,128]{2,1,0:T(4,128)(2,1)S(1)}, bf16[256,4,128]{2,1,0:T(4,128)(2,1)}, u32[]{:S(2)}) copy-start(bf16[256,4,128]{2,1,0:T(4,128)(2,1)} %param.9) | copy-start | bytes 786436
  26.7 8.7 %copy-start.2 = (f32[4,128]{1,0:T(4,128)S(1)}, f32[4,128]{1,0:T(4,128)}, u32[]{:S(2)}) copy-start(f32[4,128]{1,0:T(4,128)} %param.8) | copy-start | bytes 6148
  36.1 1.2 %collective-permute-start = (f32[2,256]{1,0:T(2,128)S(1)}, f32[2,256]{1,0:T(2,128)S(1)}, u32[]{:S(2)}, u32[]{:S(2)}) collective-permute-start(f32[2,256]{1,0:T(2,128)S(1)} %pad_maximum_fusion), channel_id=1, source_target_pairs={{0,1},{1,0},{2,3},{3,2},{4,5},{5,4},{6,7},{7,6},{8,9},{9,8},{10,11... | collective-permute-start | bytes 6152 | tf_op jit(solution)/shard_map/ppermute | solution.py:80
  39.8 14.0 %all-to-all-start.2 = ((f32[16,32,128]{2,1,0:T(8,128)}), f32[16,32,128]{2,1,0:T(8,128)S(1)}, u32[]{:S(2)}, u32[]{:S(2)}) async-start(f32[16,32,128]{2,1,0:T(8,128)} %bitcast.15), calls=%async_computation.2 | async-start | bytes 524288 | tf_op jit(solution)/shard_map/all_to_all | solution.py:34
  54.6 13.0 %all-to-all-start.3 = ((f32[16,32,128]{2,1,0:T(8,128)}), f32[16,32,128]{2,1,0:T(8,128)S(1)}, u32[]{:S(2)}, u32[]{:S(2)}) async-start(f32[16,32,128]{2,1,0:T(8,128)} %reduce-window_subtract_fusion), calls=%async_computation.3 | async-start | bytes 524288 | tf_op jit(solution)/shard_map/all_to_all | solution.py:37

commit v12 on v2

--- a/solution.py
+++ b/solution.py
@@ -56,7 +56,10 @@
     block_kv = jnp.einsum("cshd,cshe->chde", key_act, value_blk, preferred_element_type=jnp.float32)
     own_total = jnp.sum(block_kv, axis=0)
     before = lower_sum(own_total)
-    state_b = (before[None] + (jnp.cumsum(block_kv, axis=0) - block_kv)).astype(jnp.bfloat16)
+    if blocks == 1:
+        state_b = lax.reduce_precision(before[None], 8, 7).astype(jnp.bfloat16)
+    else:
+        state_b = (before[None] + (jnp.cumsum(block_kv, axis=0) - block_kv)).astype(jnp.bfloat16)
     scores = jnp.einsum("cthd,cshd->chts", query_act, key_act, preferred_element_type=jnp.float32)
     attn = jnp.where(mask, scores, 0.0).astype(jnp.bfloat16)
     mixed = jnp.einsum("chts,cshe->cthe", attn, value_blk, preferred_element_type=jnp.float32)
@@ -83,8 +86,10 @@
     )
     own_grad = jnp.sum(block_grad, axis=0)
     after = upper_sum(own_grad)
-    local_after = jnp.flip(jnp.cumsum(jnp.flip(block_grad, 0), axis=0), 0) - block_grad
-    grad_state = (after[None] + local_after).astype(jnp.bfloat16)
+    if blocks == 1:
+        grad_state = lax.reduce_precision(after[None], 8, 7).astype(jnp.bfloat16)
+    else:
+        grad_state = (after[None] + (lax.cumsum(block_grad, axis=0, reverse=True) - block_grad)).astype(jnp.bfloat16)
     bscore = jnp.einsum("cthe,cshe->chts", delta_blk, value_blk, preferred_element_type=jnp.float32)
     bscore = jnp.where(mask, bscore, 0.0).astype(jnp.bfloat16)
     dquery = jnp.einsum("chts,cshd->cthd", bscore, key_act, preferred_element_type=jnp.float32)

time: 71.4 us -> 69.4 us (0.972)
  other arithmetic: 3.73 us -> 1.8 us
    convert_element_type x2, other arithmetic: 1.98 us -> 0.04 us  [the longest x1 0.02 us: body(): state_b = lax.reduce_precision(before[None], 8, 7).astype(jnp.bfloat16)]
where the time goes in v12:
time: 69.4 us; the launch traced here: 68.8 us
  waiting for transfers between devices  36 us (52%)
  starting transfers between devices  19.1 us (28%)
  local copies, waits for them, and re-layouts  5.75 us (8%)
  matrix products  5.22 us (8%)
  other arithmetic  1.8 us (3%)
  between operations  0.84 us (1%)
    all_to_all x2, waiting for transfers between devices, exclusive_scan(): lax.all_to_all(rows.reshape(count, chunk, width), 'seq', 0, 0, tiled=True)  17.6 us
    all_to_all x2, waiting for transfers between devices, exclusive_scan(): spread = lax.all_to_all(prefix, 'seq', 0, 0, tiled=True)  17.3 us
    all_to_all x2, starting transfers between devices, exclusive_scan(): lax.all_to_all(rows.reshape(count, chunk, width), 'seq', 0, 0, tiled=True)  12 us
    all_to_all x2, starting transfers between devices, exclusive_scan(): spread = lax.all_to_all(prefix, 'seq', 0, 0, tiled=True)  7.08 us
    unnamed x15, local copies, waits for them, and re-layouts  5.75 us
    another operation x2, other arithmetic, exclusive_scan(): inclusive = lax.cumsum(gathered, axis=0, reverse=reverse)  1.51 us
  transfers between devices with their start and end apart: 5, of which 5 were waited for; matrix products, arithmetic and copies ran while one was open for 5% of the time, Pallas kernels for 0%

profile of v12, /device:TPU:0, one launch (start us, length us, event | category | flops | bytes accessed | tf_op | source)
XLA Modules:
  0.0 68.8 jit_solution(17200824874472694808)
XLA Ops:
  0.6 1.1 %copy.30 = bf16[256,4,128]{0,2,1:T(8,128)(2,1)S(1)} copy(bf16[256,4,128]{2,1,0:T(4,128)(2,1)} %param.6) | data formatting | bytes 524288 | tf_op args[1]
  1.8 1.0 %fusion.26 = f32[4,128,128]{2,1,0:T(8,128)} fusion(bf16[256,4,128]{2,1,0:T(4,128)(2,1)S(1)} %copy-done, bf16[256,4,128]{0,2,1:T(8,128)(2,1)S(1)} %copy.30), kind=kOutput, calls=%fused_computation.49 | convolution fusion | flops 34340864 | bytes 786432 | tf_op jit(solution)/shard_map/cshd,cshe->chde/dot_general | solution.py:56
  2.8 8.4 %all-to-all-start = ((f32[16,32,128]{2,1,0:T(8,128)}), f32[16,32,128]{2,1,0:T(8,128)S(1)}, u32[]{:S(2)}, u32[]{:S(2)}) async-start(f32[16,32,128]{2,1,0:T(8,128)} %bitcast.1), calls=%async_computation | async-start | bytes 524288 | tf_op jit(solution)/shard_map/all_to_all | solution.py:33
  11.4 0.8 %copy-done.2 = bf16[256,4,128]{2,1,0:T(4,128)(2,1)S(1)} copy-done((bf16[256,4,128]{2,1,0:T(4,128)(2,1)S(1)}, bf16[256,4,128]{2,1,0:T(4,128)(2,1)}, u32[]{:S(2)}) %copy-start.2) | copy-done | bytes 262168
  12.4 8.7 %all-to-all-done = f32[16,32,128]{2,1,0:T(8,128)S(1)} async-done(((f32[16,32,128]{2,1,0:T(8,128)}), f32[16,32,128]{2,1,0:T(8,128)S(1)}, u32[]{:S(2)}, u32[]{:S(2)}) %all-to-all-start) | async-done | bytes 262176 | tf_op jit(solution)/shard_map/all_to_all | solution.py:33
  21.1 0.7 %reduce-window_subtract_fusion.1 = f32[16,32,128]{2,1,0:T(8,128)} fusion(f32[16,32,128]{2,1,0:T(8,128)S(1)} %all-to-all-done), kind=kOutput, calls=%fused_computation.18 | output fusion | flops 1048576 | bytes 524288 | tf_op jit(solution)/shard_map/exclusive_scan/reduce_window_sum | solution.py:34
  21.8 3.5 %all-to-all-start.1 = ((f32[16,32,128]{2,1,0:T(8,128)}), f32[16,32,128]{2,1,0:T(8,128)S(1)}, u32[]{:S(2)}, u32[]{:S(2)}) async-start(f32[16,32,128]{2,1,0:T(8,128)} %reduce-window_subtract_fusion.1), calls=%async_computation.1 | async-start | bytes 524288 | tf_op jit(solution)/shard_map/all_to_all | solution.py:36
  25.4 0.5 fusion
  26.2 8.4 %all-to-all-done.1 = f32[16,32,128]{2,1,0:T(8,128)S(1)} async-done(((f32[16,32,128]{2,1,0:T(8,128)}), f32[16,32,128]{2,1,0:T(8,128)S(1)}, u32[]{:S(2)}, u32[]{:S(2)}) %all-to-all-start.1) | async-done | bytes 262176 | tf_op jit(solution)/shard_map/all_to_all | solution.py:36
  34.6 0.3 multiply_reduce_fusion.1
  35.1 1.1 %collective-permute-done = f32[2,256]{1,0:T(2,128)S(1)} collective-permute-done((f32[2,256]{1,0:T(2,128)S(1)}, f32[2,256]{1,0:T(2,128)S(1)}, u32[]{:S(2)}, u32[]{:S(2)}) %collective-permute-start) | collective-permute-done | bytes 2080 | tf_op jit(solution)/shard_map/ppermute | solution.py:74
  36.4 1.0 %fusion.38 = f32[4,128,128]{2,1,0:T(8,128)} fusion(bf16[256,4,128]{0,2,1:T(8,128)(2,1)S(1)} %get-tuple-element.14, bf16[256,4,128]{0,2,1:T(8,128)(2,1)S(1)} %copy.29), kind=kOutput, calls=%fused_computation.60 | convolution fusion | flops 34340864 | bytes 786432 | tf_op jit(solution)/shard_map/cthd,cthe->chde/dot_general | solution.py:84
  37.4 0.3 fusion.1
  37.8 0.9 %copy.45 = bf16[256,4,128]{2,1,0:T(4,128)(2,1)} copy(bf16[256,4,128]{0,2,1:T(8,128)(2,1)S(1)} %get-tuple-element.15) | data formatting | bytes 524288
  38.6 3.5 %all-to-all-start.2 = ((f32[16,32,128]{2,1,0:T(8,128)}), f32[16,32,128]{2,1,0:T(8,128)S(1)}, u32[]{:S(2)}, u32[]{:S(2)}) async-start(f32[16,32,128]{2,1,0:T(8,128)} %bitcast.15), calls=%async_computation.2 | async-start | bytes 524288 | tf_op jit(solution)/shard_map/all_to_all | solution.py:33
  42.2 0.3 fusion.34
  42.8 0.9 %copy.46 = bf16[256,4,128]{2,1,0:T(4,128)(2,1)} copy(bf16[256,4,128]{0,2,1:T(8,128)(2,1)S(1)} %fusion.7) | data formatting | bytes 524288
  43.7 8.9 %all-to-all-done.2 = f32[16,32,128]{2,1,0:T(8,128)S(1)} async-done(((f32[16,32,128]{2,1,0:T(8,128)}), f32[16,32,128]{2,1,0:T(8,128)S(1)}, u32[]{:S(2)}, u32[]{:S(2)}) %all-to-all-start.2) | async-done | bytes 262176 | tf_op jit(solution)/shard_map/all_to_all | solution.py:33
  52.6 0.8 %reduce-window_subtract_fusion = f32[16,32,128]{2,1,0:T(8,128)} fusion(f32[16,32,128]{2,1,0:T(8,128)S(1)} %all-to-all-done.2), kind=kOutput, calls=%fused_computation.17 | output fusion | flops 1048576 | bytes 524288 | tf_op jit(solution)/shard_map/exclusive_scan/reduce_window_sum | solution.py:34
  53.4 3.5 %all-to-all-start.3 = ((f32[16,32,128]{2,1,0:T(8,128)}), f32[16,32,128]{2,1,0:T(8,128)S(1)}, u32[]{:S(2)}, u32[]{:S(2)}) async-start(f32[16,32,128]{2,1,0:T(8,128)} %reduce-window_subtract_fusion), calls=%async_computation.3 | async-start | bytes 524288 | tf_op jit(solution)/shard_map/all_to_all | solution.py:36
  57.5 8.9 %all-to-all-done.3 = f32[16,32,128]{2,1,0:T(8,128)S(1)} async-done(((f32[16,32,128]{2,1,0:T(8,128)}), f32[16,32,128]{2,1,0:T(8,128)S(1)}, u32[]{:S(2)}, u32[]{:S(2)}) %all-to-all-start.3) | async-done | bytes 262176 | tf_op jit(solution)/shard_map/all_to_all | solution.py:36
  66.4 0.3 fusion.10
  66.7 0.9 %copy.48 = bf16[256,4,128]{2,1,0:T(4,128)(2,1)} copy(bf16[256,4,128]{0,2,1:T(8,128)(2,1)S(1)} %fusion.10) | data formatting | bytes 524288
  67.9 0.9 %copy.47 = bf16[256,4,128]{2,1,0:T(4,128)(2,1)} copy(bf16[256,4,128]{0,2,1:T(8,128)(2,1)S(1)} %fusion.8) | data formatting | bytes 524288
  (23 shorter events, 2.2 us)
Async XLA Ops:
  0.6 1.2 %copy-start = (bf16[256,4,128]{2,1,0:T(4,128)(2,1)S(1)}, bf16[256,4,128]{2,1,0:T(4,128)(2,1)}, u32[]{:S(2)}) copy-start(bf16[256,4,128]{2,1,0:T(4,128)(2,1)} %param.7) | copy-start | bytes 786436
  2.8 8.5 %copy-start.1 = (bf16[256,4,128]{2,1,0:T(4,128)(2,1)S(1)}, bf16[256,4,128]{2,1,0:T(4,128)(2,1)}, u32[]{:S(2)}) copy-start(bf16[256,4,128]{2,1,0:T(4,128)(2,1)} %param.5) | copy-start | bytes 786436
  2.8 18.3 %all-to-all-start = ((f32[16,32,128]{2,1,0:T(8,128)}), f32[16,32,128]{2,1,0:T(8,128)S(1)}, u32[]{:S(2)}, u32[]{:S(2)}) async-start(f32[16,32,128]{2,1,0:T(8,128)} %bitcast.1), calls=%async_computation | async-start | bytes 524288 | tf_op jit(solution)/shard_map/all_to_all | solution.py:33
  11.3 1.0 %copy-start.2 = (bf16[256,4,128]{2,1,0:T(4,128)(2,1)S(1)}, bf16[256,4,128]{2,1,0:T(4,128)(2,1)}, u32[]{:S(2)}) copy-start(bf16[256,4,128]{2,1,0:T(4,128)(2,1)} %param.9) | copy-start | bytes 786436
  21.8 12.8 %all-to-all-start.1 = ((f32[16,32,128]{2,1,0:T(8,128)}), f32[16,32,128]{2,1,0:T(8,128)S(1)}, u32[]{:S(2)}, u32[]{:S(2)}) async-start(f32[16,32,128]{2,1,0:T(8,128)} %reduce-window_subtract_fusion.1), calls=%async_computation.1 | async-start | bytes 524288 | tf_op jit(solution)/shard_map/all_to_all | solution.py:36
  26.2 8.4 %copy-start.3 = (f32[4,128]{1,0:T(4,128)S(1)}, f32[4,128]{1,0:T(4,128)}, u32[]{:S(2)}) copy-start(f32[4,128]{1,0:T(4,128)} %param.8) | copy-start | bytes 6148
  35.0 1.2 %collective-permute-start = (f32[2,256]{1,0:T(2,128)S(1)}, f32[2,256]{1,0:T(2,128)S(1)}, u32[]{:S(2)}, u32[]{:S(2)}) collective-permute-start(f32[2,256]{1,0:T(2,128)S(1)} %pad_maximum_fusion), channel_id=1, source_target_pairs={{0,1},{1,0},{2,3},{3,2},{4,5},{5,4},{6,7},{7,6},{8,9},{9,8},{10,11... | collective-permute-start | bytes 6152 | tf_op jit(solution)/shard_map/ppermute | solution.py:74
  38.6 14.0 %all-to-all-start.2 = ((f32[16,32,128]{2,1,0:T(8,128)}), f32[16,32,128]{2,1,0:T(8,128)S(1)}, u32[]{:S(2)}, u32[]{:S(2)}) async-start(f32[16,32,128]{2,1,0:T(8,128)} %bitcast.15), calls=%async_computation.2 | async-start | bytes 524288 | tf_op jit(solution)/shard_map/all_to_all | solution.py:33
  53.4 13.0 %all-to-all-start.3 = ((f32[16,32,128]{2,1,0:T(8,128)}), f32[16,32,128]{2,1,0:T(8,128)S(1)}, u32[]{:S(2)}, u32[]{:S(2)}) async-start(f32[16,32,128]{2,1,0:T(8,128)} %reduce-window_subtract_fusion), calls=%async_computation.3 | async-start | bytes 524288 | tf_op jit(solution)/shard_map/all_to_all | solution.py:36

commit v13 on v12

--- a/solution.py
+++ b/solution.py
@@ -31,8 +31,16 @@
     chunk = -(-size // count)
     rows = jnp.pad(rows, ((0, chunk * count - size), (0, 0)))
     gathered = lax.all_to_all(rows.reshape(count, chunk, width), "seq", 0, 0, tiled=True)
-    inclusive = lax.cumsum(gathered, axis=0, reverse=reverse)
-    prefix = inclusive - gathered
+    if count > 32:
+        prefix = lax.cumsum(gathered, axis=0, reverse=reverse) - gathered
+    else:
+        order = range(count - 1, -1, -1) if reverse else range(count)
+        running = jnp.zeros_like(gathered[:1])
+        parts = [None] * count
+        for index in order:
+            parts[index] = running
+            running = running + gathered[index:index + 1]
+        prefix = jnp.concatenate(parts, axis=0)
     spread = lax.all_to_all(prefix, "seq", 0, 0, tiled=True)
     return spread.reshape(-1, width)[:size].reshape(own_total.shape)
 

time: 69.4 us -> 86.9 us (1.25)
  other arithmetic: 1.8 us -> 14.3 us
  local copies, waits for them, and re-layouts: 5.75 us -> 11.4 us
  waiting for transfers between devices: 36 us -> 34.6 us
    unnamed x0 -> x22, other arithmetic: none -> 13.4 us
    unnamed x15 -> x25, local copies, waits for them, and re-layouts: 5.75 us -> 10.8 us
    another operation x2 -> x0, other arithmetic: 1.51 us -> none  [exclusive_scan(): inclusive = lax.cumsum(gathered, axis=0, reverse=reverse)]
where the time goes in v13:
time: 86.9 us; the launch traced here: 86.3 us
  waiting for transfers between devices  34.6 us (40%)
  starting transfers between devices  19.1 us (22%)
  other arithmetic  14.3 us (16%)
  local copies, waits for them, and re-layouts  11.4 us (13%)
  matrix products  6.02 us (7%)
    all_to_all x2, waiting for transfers between devices, exclusive_scan(): lax.all_to_all(rows.reshape(count, chunk, width), 'seq', 0, 0, tiled=True)  17 us
    all_to_all x2, waiting for transfers between devices, exclusive_scan(): spread = lax.all_to_all(prefix, 'seq', 0, 0, tiled=True)  16.5 us
    unnamed x22, other arithmetic  13.4 us
    all_to_all x2, starting transfers between devices, exclusive_scan(): lax.all_to_all(rows.reshape(count, chunk, width), 'seq', 0, 0, tiled=True)  12 us
    unnamed x25, local copies, waits for them, and re-layouts  10.8 us
    all_to_all x2, starting transfers between devices, exclusive_scan(): spread = lax.all_to_all(prefix, 'seq', 0, 0, tiled=True)  7.08 us
  transfers between devices with their start and end apart: 5, of which 5 were waited for; matrix products, arithmetic and copies ran while one was open for 5% of the time, Pallas kernels for 0%

profile of v13, /device:TPU:0, one launch (start us, length us, event | category | flops | bytes accessed | tf_op | source)
XLA Modules:
  0.0 86.3 jit_solution(5985369371860864144)
XLA Ops:
  0.6 1.1 %copy.30 = bf16[256,4,128]{0,2,1:T(8,128)(2,1)S(1)} copy(bf16[256,4,128]{2,1,0:T(4,128)(2,1)} %param.6) | data formatting | bytes 524288 | tf_op args[1]
  1.8 1.0 %fusion.26 = f32[4,128,128]{2,1,0:T(8,128)} fusion(bf16[256,4,128]{2,1,0:T(4,128)(2,1)S(1)} %copy-done, bf16[256,4,128]{0,2,1:T(8,128)(2,1)S(1)} %copy.30), kind=kOutput, calls=%fused_computation.47 | convolution fusion | flops 34340864 | bytes 786432 | tf_op jit(solution)/shard_map/cshd,cshe->chde/dot_general | solution.py:64
  2.8 8.4 %all-to-all-start = ((f32[16,32,128]{2,1,0:T(8,128)}), f32[16,32,128]{2,1,0:T(8,128)S(1)}, u32[]{:S(2)}, u32[]{:S(2)}) async-start(f32[16,32,128]{2,1,0:T(8,128)} %bitcast.1), calls=%async_computation | async-start | bytes 524288 | tf_op jit(solution)/shard_map/all_to_all | solution.py:33
  11.4 0.8 copy-done.2
  13.0 8.1 %all-to-all-done = f32[16,32,128]{2,1,0:T(8,128)S(1)} async-done(((f32[16,32,128]{2,1,0:T(8,128)}), f32[16,32,128]{2,1,0:T(8,128)S(1)}, u32[]{:S(2)}, u32[]{:S(2)}) %all-to-all-start) | async-done | bytes 262176 | tf_op jit(solution)/shard_map/all_to_all | solution.py:33
  22.3 0.6 constant_dynamic-update-slice_fusion.12
  22.9 0.6 constant_dynamic-update-slice_fusion.11
  24.2 0.6 constant_dynamic-update-slice_fusion.9
  25.4 0.6 constant_dynamic-update-slice_fusion.7
  29.6 0.6 constant_dynamic-update-slice_fusion
  30.3 3.5 %all-to-all-start.1 = ((f32[16,32,128]{2,1,0:T(8,128)}), f32[16,32,128]{2,1,0:T(8,128)S(1)}, u32[]{:S(2)}, u32[]{:S(2)}) async-start(f32[16,32,128]{2,1,0:T(8,128)} %constant_dynamic-update-slice_fusion), calls=%async_computation.1 | async-start | bytes 524288 | tf_op jit(solution)/shard_map/all_to_all | solution.py:44
  34.7 8.4 %all-to-all-done.1 = f32[16,32,128]{2,1,0:T(8,128)S(1)} async-done(((f32[16,32,128]{2,1,0:T(8,128)}), f32[16,32,128]{2,1,0:T(8,128)S(1)}, u32[]{:S(2)}, u32[]{:S(2)}) %all-to-all-start.1) | async-done | bytes 262176 | tf_op jit(solution)/shard_map/all_to_all | solution.py:44
  43.5 1.1 %collective-permute-done = f32[2,256]{1,0:T(2,128)S(1)} collective-permute-done((f32[2,256]{1,0:T(2,128)S(1)}, f32[2,256]{1,0:T(2,128)S(1)}, u32[]{:S(2)}, u32[]{:S(2)}) %collective-permute-start) | collective-permute-done | bytes 2080 | tf_op jit(solution)/shard_map/ppermute | solution.py:82
  44.9 1.0 %fusion.38 = f32[4,128,128]{2,1,0:T(8,128)} fusion(bf16[256,4,128]{0,2,1:T(8,128)(2,1)S(1)} %get-tuple-element.30, bf16[256,4,128]{0,2,1:T(8,128)(2,1)S(1)} %copy.29), kind=kOutput, calls=%fused_computation.118 | convolution fusion | flops 34340864 | bytes 786432 | tf_op jit(solution)/shard_map/cthd,cthe->chde/dot_general | solution.py:92
  46.2 0.9 %copy.45 = bf16[256,4,128]{2,1,0:T(4,128)(2,1)} copy(bf16[256,4,128]{0,2,1:T(8,128)(2,1)S(1)} %get-tuple-element.31) | data formatting | bytes 524288
  47.1 3.5 %all-to-all-start.2 = ((f32[16,32,128]{2,1,0:T(8,128)}), f32[16,32,128]{2,1,0:T(8,128)S(1)}, u32[]{:S(2)}, u32[]{:S(2)}) async-start(f32[16,32,128]{2,1,0:T(8,128)} %bitcast.15), calls=%async_computation.2 | async-start | bytes 524288 | tf_op jit(solution)/shard_map/all_to_all | solution.py:33
  51.2 0.9 %copy.46 = bf16[256,4,128]{2,1,0:T(4,128)(2,1)} copy(bf16[256,4,128]{0,2,1:T(8,128)(2,1)S(1)} %fusion.7) | data formatting | bytes 524288
  52.1 8.9 %all-to-all-done.2 = f32[16,32,128]{2,1,0:T(8,128)S(1)} async-done(((f32[16,32,128]{2,1,0:T(8,128)}), f32[16,32,128]{2,1,0:T(8,128)S(1)}, u32[]{:S(2)}, u32[]{:S(2)}) %all-to-all-start.2) | async-done | bytes 262176 | tf_op jit(solution)/shard_map/all_to_all | solution.py:33
  61.0 0.6 constant_dynamic-update-slice_fusion.31
  70.8 3.5 %all-to-all-start.3 = ((f32[16,32,128]{2,1,0:T(8,128)}), f32[16,32,128]{2,1,0:T(8,128)S(1)}, u32[]{:S(2)}, u32[]{:S(2)}) async-start(f32[16,32,128]{2,1,0:T(8,128)} %constant_dynamic-update-slice_fusion.16), calls=%async_computation.3 | async-start | bytes 524288 | tf_op jit(solution)/shard_map/all_to_all | solution.py:44
  74.5 1.1 %fusion.40 = f32[4,128,256]{2,1,0:T(8,128)} fusion(bf16[4,256,256]{2,1,0:T(8,128)(2,1)S(1)} %fusion.1, bf16[256,4,128]{0,2,1:T(8,128)(2,1)S(1)} %copy.29), kind=kOutput, calls=%fused_computation.119 | convolution fusion | flops 67895296 | bytes 1310720 | tf_op jit(solution)/shard_map/chts,cthd->cshd/dot_general | solution.py:107
  75.6 8.1 %all-to-all-done.3 = f32[16,32,128]{2,1,0:T(8,128)S(1)} async-done(((f32[16,32,128]{2,1,0:T(8,128)}), f32[16,32,128]{2,1,0:T(8,128)S(1)}, u32[]{:S(2)}, u32[]{:S(2)}) %all-to-all-start.3) | async-done | bytes 262176 | tf_op jit(solution)/shard_map/all_to_all | solution.py:44
  84.1 0.9 %copy.48 = bf16[256,4,128]{2,1,0:T(4,128)(2,1)} copy(bf16[256,4,128]{0,2,1:T(8,128)(2,1)S(1)} %fusion.10) | data formatting | bytes 524288
  85.4 0.9 %copy.47 = bf16[256,4,128]{2,1,0:T(4,128)(2,1)} copy(bf16[256,4,128]{0,2,1:T(8,128)(2,1)S(1)} %fusion.8) | data formatting | bytes 524288
  (55 shorter events, 19.7 us)
Async XLA Ops:
  0.6 1.2 %copy-start = (bf16[256,4,128]{2,1,0:T(4,128)(2,1)S(1)}, bf16[256,4,128]{2,1,0:T(4,128)(2,1)}, u32[]{:S(2)}) copy-start(bf16[256,4,128]{2,1,0:T(4,128)(2,1)} %param.7) | copy-start | bytes 786436
  2.8 8.5 %copy-start.1 = (bf16[256,4,128]{2,1,0:T(4,128)(2,1)S(1)}, bf16[256,4,128]{2,1,0:T(4,128)(2,1)}, u32[]{:S(2)}) copy-start(bf16[256,4,128]{2,1,0:T(4,128)(2,1)} %param.5) | copy-start | bytes 786436
  2.8 18.3 %all-to-all-start = ((f32[16,32,128]{2,1,0:T(8,128)}), f32[16,32,128]{2,1,0:T(8,128)S(1)}, u32[]{:S(2)}, u32[]{:S(2)}) async-start(f32[16,32,128]{2,1,0:T(8,128)} %bitcast.1), calls=%async_computation | async-start | bytes 524288 | tf_op jit(solution)/shard_map/all_to_all | solution.py:33
  11.3 1.0 %copy-start.2 = (bf16[256,4,128]{2,1,0:T(4,128)(2,1)S(1)}, bf16[256,4,128]{2,1,0:T(4,128)(2,1)}, u32[]{:S(2)}) copy-start(bf16[256,4,128]{2,1,0:T(4,128)(2,1)} %param.9) | copy-start | bytes 786436
  30.3 12.8 %all-to-all-start.1 = ((f32[16,32,128]{2,1,0:T(8,128)}), f32[16,32,128]{2,1,0:T(8,128)S(1)}, u32[]{:S(2)}, u32[]{:S(2)}) async-start(f32[16,32,128]{2,1,0:T(8,128)} %constant_dynamic-update-slice_fusion), calls=%async_computation.1 | async-start | bytes 524288 | tf_op jit(solution)/shard_map/all_to_all | solution.py:44
  34.6 8.4 %copy-start.3 = (f32[4,128]{1,0:T(4,128)S(1)}, f32[4,128]{1,0:T(4,128)}, u32[]{:S(2)}) copy-start(f32[4,128]{1,0:T(4,128)} %param.8) | copy-start | bytes 6148
  43.4 1.2 %collective-permute-start = (f32[2,256]{1,0:T(2,128)S(1)}, f32[2,256]{1,0:T(2,128)S(1)}, u32[]{:S(2)}, u32[]{:S(2)}) collective-permute-start(f32[2,256]{1,0:T(2,128)S(1)} %pad_maximum_fusion), channel_id=1, source_target_pairs={{0,1},{1,0},{2,3},{3,2},{4,5},{5,4},{6,7},{7,6},{8,9},{9,8},{10,11... | collective-permute-start | bytes 6152 | tf_op jit(solution)/shard_map/ppermute | solution.py:82
  47.1 14.0 %all-to-all-start.2 = ((f32[16,32,128]{2,1,0:T(8,128)}), f32[16,32,128]{2,1,0:T(8,128)S(1)}, u32[]{:S(2)}, u32[]{:S(2)}) async-start(f32[16,32,128]{2,1,0:T(8,128)} %bitcast.15), calls=%async_computation.2 | async-start | bytes 524288 | tf_op jit(solution)/shard_map/all_to_all | solution.py:33
  70.8 13.0 %all-to-all-start.3 = ((f32[16,32,128]{2,1,0:T(8,128)}), f32[16,32,128]{2,1,0:T(8,128)S(1)}, u32[]{:S(2)}, u32[]{:S(2)}) async-start(f32[16,32,128]{2,1,0:T(8,128)} %constant_dynamic-update-slice_fusion.16), calls=%async_computation.3 | async-start | bytes 524288 | tf_op jit(solution)/shard_map/all_to_all | solution.py:44
  84.1 1.0 %copy-start.4 = (f32[4,128,256]{2,1,0:T(8,128)S(1)}, f32[4,128,256]{2,1,0:T(8,128)}, u32[]{:S(2)}) copy-start(f32[4,128,256]{2,1,0:T(8,128)} %fusion.40) | copy-start | bytes 1572868

commit v14 on v12

--- a/solution.py
+++ b/solution.py
@@ -31,8 +31,13 @@
     chunk = -(-size // count)
     rows = jnp.pad(rows, ((0, chunk * count - size), (0, 0)))
     gathered = lax.all_to_all(rows.reshape(count, chunk, width), "seq", 0, 0, tiled=True)
-    inclusive = lax.cumsum(gathered, axis=0, reverse=reverse)
-    prefix = inclusive - gathered
+    if count > 32:
+        prefix = lax.cumsum(gathered, axis=0, reverse=reverse) - gathered
+    else:
+        rows_i = lax.broadcasted_iota(jnp.int32, (count, count, 1, 1), 0)
+        cols_i = lax.broadcasted_iota(jnp.int32, (count, count, 1, 1), 1)
+        earlier = (cols_i > rows_i) if reverse else (cols_i < rows_i)
+        prefix = jnp.sum(jnp.where(earlier, gathered[None], 0.0), axis=1)
     spread = lax.all_to_all(prefix, "seq", 0, 0, tiled=True)
     return spread.reshape(-1, width)[:size].reshape(own_total.shape)
 

time: 69.4 us -> 70.5 us (1.016)
  other arithmetic: 1.8 us -> 2.76 us
  matrix products: 5.22 us -> 6.02 us
    reduce_sum x0 -> x2, other arithmetic: none -> 2.46 us  [exclusive_scan(): prefix = jnp.sum(jnp.where(earlier, gathered[None], 0.0), axis=1)]
    another operation x2 -> x0, other arithmetic: 1.51 us -> none  [exclusive_scan(): inclusive = lax.cumsum(gathered, axis=0, reverse=reverse)]
    dot_general x1, matrix products: 0.29 us -> 1.08 us  [body(): jnp.einsum('chts,cthd->cshd', bscore, query_act, preferred_element_type=j...]
    all_to_all x2, waiting for transfers between devices: 17.3 us -> 16.5 us  [exclusive_scan(): spread = lax.all_to_all(prefix, 'seq', 0, 0, tiled=True)]
    all_to_all x2, waiting for transfers between devices: 17.6 us -> 18.3 us  [exclusive_scan(): lax.all_to_all(rows.reshape(count, chunk, width), 'seq', 0, 0, tiled=True)]
    unnamed x15 -> x17, local copies, waits for them, and re-layouts: 5.75 us -> 5.15 us
  transfers between devices with their start and end apart: 5 -> 5, of which waited for: 5 -> 5; matrix products, arithmetic and copies ran while one was open for 5% -> 6% of each run, Pallas kernels for 0% -> 0%
where the time goes in v14:
time: 70.5 us; the launch traced here: 69.9 us
  waiting for transfers between devices  35.9 us (51%)
  starting transfers between devices  19.1 us (27%)
  matrix products  6.02 us (9%)
  local copies, waits for them, and re-layouts  5.15 us (7%)
  other arithmetic  2.76 us (4%)
  between operations  0.86 us (1%)
    all_to_all x2, waiting for transfers between devices, exclusive_scan(): lax.all_to_all(rows.reshape(count, chunk, width), 'seq', 0, 0, tiled=True)  18.3 us
    all_to_all x2, waiting for transfers between devices, exclusive_scan(): spread = lax.all_to_all(prefix, 'seq', 0, 0, tiled=True)  16.5 us
    all_to_all x2, starting transfers between devices, exclusive_scan(): lax.all_to_all(rows.reshape(count, chunk, width), 'seq', 0, 0, tiled=True)  12 us
    all_to_all x2, starting transfers between devices, exclusive_scan(): spread = lax.all_to_all(prefix, 'seq', 0, 0, tiled=True)  7.08 us
    unnamed x17, local copies, waits for them, and re-layouts  5.15 us
    reduce_sum x2, other arithmetic, exclusive_scan(): prefix = jnp.sum(jnp.where(earlier, gathered[None], 0.0), axis=1)  2.46 us
  transfers between devices with their start and end apart: 5, of which 5 were waited for; matrix products, arithmetic and copies ran while one was open for 6% of the time, Pallas kernels for 0%

profile of v14, /device:TPU:0, one launch (start us, length us, event | category | flops | bytes accessed | tf_op | source)
XLA Modules:
  0.0 69.9 jit_solution(14887940272549297505)
XLA Ops:
  0.6 1.1 %copy.50 = bf16[256,4,128]{0,2,1:T(8,128)(2,1)S(1)} copy(bf16[256,4,128]{2,1,0:T(4,128)(2,1)} %param.6) | data formatting | bytes 524288 | tf_op args[1]
  1.8 1.0 %fusion.26 = f32[4,128,128]{2,1,0:T(8,128)} fusion(bf16[256,4,128]{2,1,0:T(4,128)(2,1)S(1)} %copy-done, bf16[256,4,128]{0,2,1:T(8,128)(2,1)S(1)} %copy.50), kind=kOutput, calls=%fused_computation.49 | convolution fusion | flops 34340864 | bytes 786432 | tf_op jit(solution)/shard_map/cshd,cshe->chde/dot_general | solution.py:61
  2.8 8.4 %all-to-all-start = ((f32[16,32,128]{2,1,0:T(8,128)}), f32[16,32,128]{2,1,0:T(8,128)S(1)}, u32[]{:S(2)}, u32[]{:S(2)}) async-start(f32[16,32,128]{2,1,0:T(8,128)} %bitcast.1), calls=%async_computation | async-start | bytes 524288 | tf_op jit(solution)/shard_map/all_to_all | solution.py:33
  11.7 9.4 %all-to-all-done = f32[16,32,128]{2,1,0:T(8,128)S(1)} async-done(((f32[16,32,128]{2,1,0:T(8,128)}), f32[16,32,128]{2,1,0:T(8,128)S(1)}, u32[]{:S(2)}, u32[]{:S(2)}) %all-to-all-start) | async-done | bytes 262176 | tf_op jit(solution)/shard_map/all_to_all | solution.py:33
  21.1 1.2 %select_reduce_fusion.1 = f32[16,32,128]{2,1,0:T(8,128)} fusion(f32[16,32,128]{2,1,0:T(8,128)S(1)} %all-to-all-done, pred[16,16]{1,0:T(8,128)(4,1)S(1)} %iota_compare_fusion.2), kind=kLoop, calls=%fused_computation.1 | loop fusion | flops 2031616 | bytes 524544 | tf_op jit(solution)/shard_map/reduce_sum | solution.py:40
  22.3 3.5 %all-to-all-start.1 = ((f32[16,32,128]{2,1,0:T(8,128)}), f32[16,32,128]{2,1,0:T(8,128)S(1)}, u32[]{:S(2)}, u32[]{:S(2)}) async-start(f32[16,32,128]{2,1,0:T(8,128)} %select_reduce_fusion.1), calls=%async_computation.1 | async-start | bytes 524288 | tf_op jit(solution)/shard_map/all_to_all | solution.py:41
  25.9 0.5 fusion
  26.7 8.4 %all-to-all-done.1 = f32[16,32,128]{2,1,0:T(8,128)S(1)} async-done(((f32[16,32,128]{2,1,0:T(8,128)}), f32[16,32,128]{2,1,0:T(8,128)S(1)}, u32[]{:S(2)}, u32[]{:S(2)}) %all-to-all-start.1) | async-done | bytes 262176 | tf_op jit(solution)/shard_map/all_to_all | solution.py:41
  35.1 0.3 multiply_reduce_fusion.1
  35.6 1.1 %collective-permute-done = f32[2,256]{1,0:T(2,128)S(1)} collective-permute-done((f32[2,256]{1,0:T(2,128)S(1)}, f32[2,256]{1,0:T(2,128)S(1)}, u32[]{:S(2)}, u32[]{:S(2)}) %collective-permute-start) | collective-permute-done | bytes 2080 | tf_op jit(solution)/shard_map/ppermute | solution.py:79
  36.9 1.0 %fusion.38 = f32[4,128,128]{2,1,0:T(8,128)} fusion(bf16[256,4,128]{0,2,1:T(8,128)(2,1)S(1)} %get-tuple-element.18, bf16[256,4,128]{0,2,1:T(8,128)(2,1)S(1)} %copy.49), kind=kOutput, calls=%fused_computation.62 | convolution fusion | flops 34340864 | bytes 786432 | tf_op jit(solution)/shard_map/cthd,cthe->chde/dot_general | solution.py:89
  37.9 0.3 fusion.1
  38.3 0.9 %copy.65 = bf16[256,4,128]{2,1,0:T(4,128)(2,1)} copy(bf16[256,4,128]{0,2,1:T(8,128)(2,1)S(1)} %get-tuple-element.19) | data formatting | bytes 524288
  39.1 3.5 %all-to-all-start.2 = ((f32[16,32,128]{2,1,0:T(8,128)}), f32[16,32,128]{2,1,0:T(8,128)S(1)}, u32[]{:S(2)}, u32[]{:S(2)}) async-start(f32[16,32,128]{2,1,0:T(8,128)} %bitcast.15), calls=%async_computation.2 | async-start | bytes 524288 | tf_op jit(solution)/shard_map/all_to_all | solution.py:33
  42.7 0.3 fusion.34
  43.3 0.9 %copy.66 = bf16[256,4,128]{2,1,0:T(4,128)(2,1)} copy(bf16[256,4,128]{0,2,1:T(8,128)(2,1)S(1)} %fusion.7) | data formatting | bytes 524288
  44.2 8.9 %all-to-all-done.2 = f32[16,32,128]{2,1,0:T(8,128)S(1)} async-done(((f32[16,32,128]{2,1,0:T(8,128)}), f32[16,32,128]{2,1,0:T(8,128)S(1)}, u32[]{:S(2)}, u32[]{:S(2)}) %all-to-all-start.2) | async-done | bytes 262176 | tf_op jit(solution)/shard_map/all_to_all | solution.py:33
  53.1 1.2 %select_reduce_fusion = f32[16,32,128]{2,1,0:T(8,128)} fusion(f32[16,32,128]{2,1,0:T(8,128)S(1)} %all-to-all-done.2, pred[16,16]{1,0:T(8,128)(4,1)S(1)} %iota_compare_fusion.1), kind=kLoop, calls=%fused_computation | loop fusion | flops 2031616 | bytes 524544 | tf_op jit(solution)/shard_map/reduce_sum | solution.py:40
  54.3 3.5 %all-to-all-start.3 = ((f32[16,32,128]{2,1,0:T(8,128)}), f32[16,32,128]{2,1,0:T(8,128)S(1)}, u32[]{:S(2)}, u32[]{:S(2)}) async-start(f32[16,32,128]{2,1,0:T(8,128)} %select_reduce_fusion), calls=%async_computation.3 | async-start | bytes 524288 | tf_op jit(solution)/shard_map/all_to_all | solution.py:41
  58.1 1.1 %fusion.40 = f32[4,128,256]{2,1,0:T(8,128)} fusion(bf16[4,256,256]{2,1,0:T(8,128)(2,1)S(1)} %fusion.1, bf16[256,4,128]{0,2,1:T(8,128)(2,1)S(1)} %copy.49), kind=kOutput, calls=%fused_computation.63 | convolution fusion | flops 67895296 | bytes 1310720 | tf_op jit(solution)/shard_map/chts,cthd->cshd/dot_general | solution.py:104
  59.2 8.1 %all-to-all-done.3 = f32[16,32,128]{2,1,0:T(8,128)S(1)} async-done(((f32[16,32,128]{2,1,0:T(8,128)}), f32[16,32,128]{2,1,0:T(8,128)S(1)}, u32[]{:S(2)}, u32[]{:S(2)}) %all-to-all-start.3) | async-done | bytes 262176 | tf_op jit(solution)/shard_map/all_to_all | solution.py:41
  67.3 0.3 fusion.10
  67.7 0.9 %copy.68 = bf16[256,4,128]{2,1,0:T(4,128)(2,1)} copy(bf16[256,4,128]{0,2,1:T(8,128)(2,1)S(1)} %fusion.10) | data formatting | bytes 524288
  69.0 0.9 %copy.67 = bf16[256,4,128]{2,1,0:T(4,128)(2,1)} copy(bf16[256,4,128]{0,2,1:T(8,128)(2,1)S(1)} %fusion.8) | data formatting | bytes 524288
  (27 shorter events, 2.1 us)
Async XLA Ops:
  0.6 1.2 %copy-start = (bf16[256,4,128]{2,1,0:T(4,128)(2,1)S(1)}, bf16[256,4,128]{2,1,0:T(4,128)(2,1)}, u32[]{:S(2)}) copy-start(bf16[256,4,128]{2,1,0:T(4,128)(2,1)} %param.7) | copy-start | bytes 786436
  2.8 8.5 %copy-start.1 = (bf16[256,4,128]{2,1,0:T(4,128)(2,1)S(1)}, bf16[256,4,128]{2,1,0:T(4,128)(2,1)}, u32[]{:S(2)}) copy-start(bf16[256,4,128]{2,1,0:T(4,128)(2,1)} %param.5) | copy-start | bytes 786436
  2.8 8.6 %copy-start.2 = (bf16[256,4,128]{2,1,0:T(4,128)(2,1)S(1)}, bf16[256,4,128]{2,1,0:T(4,128)(2,1)}, u32[]{:S(2)}) copy-start(bf16[256,4,128]{2,1,0:T(4,128)(2,1)} %param.9) | copy-start | bytes 786436
  2.8 18.3 %all-to-all-start = ((f32[16,32,128]{2,1,0:T(8,128)}), f32[16,32,128]{2,1,0:T(8,128)S(1)}, u32[]{:S(2)}, u32[]{:S(2)}) async-start(f32[16,32,128]{2,1,0:T(8,128)} %bitcast.1), calls=%async_computation | async-start | bytes 524288 | tf_op jit(solution)/shard_map/all_to_all | solution.py:33
  22.3 12.8 %all-to-all-start.1 = ((f32[16,32,128]{2,1,0:T(8,128)}), f32[16,32,128]{2,1,0:T(8,128)S(1)}, u32[]{:S(2)}, u32[]{:S(2)}) async-start(f32[16,32,128]{2,1,0:T(8,128)} %select_reduce_fusion.1), calls=%async_computation.1 | async-start | bytes 524288 | tf_op jit(solution)/shard_map/all_to_all | solution.py:41
  26.4 8.7 %copy-start.3 = (f32[4,128]{1,0:T(4,128)S(1)}, f32[4,128]{1,0:T(4,128)}, u32[]{:S(2)}) copy-start(f32[4,128]{1,0:T(4,128)} %param.8) | copy-start | bytes 6148
  35.5 1.2 %collective-permute-start = (f32[2,256]{1,0:T(2,128)S(1)}, f32[2,256]{1,0:T(2,128)S(1)}, u32[]{:S(2)}, u32[]{:S(2)}) collective-permute-start(f32[2,256]{1,0:T(2,128)S(1)} %pad_maximum_fusion), channel_id=1, source_target_pairs={{0,1},{1,0},{2,3},{3,2},{4,5},{5,4},{6,7},{7,6},{8,9},{9,8},{10,11... | collective-permute-start | bytes 6152 | tf_op jit(solution)/shard_map/ppermute | solution.py:79
  39.1 14.0 %all-to-all-start.2 = ((f32[16,32,128]{2,1,0:T(8,128)}), f32[16,32,128]{2,1,0:T(8,128)S(1)}, u32[]{:S(2)}, u32[]{:S(2)}) async-start(f32[16,32,128]{2,1,0:T(8,128)} %bitcast.15), calls=%async_computation.2 | async-start | bytes 524288 | tf_op jit(solution)/shard_map/all_to_all | solution.py:33
  54.3 13.0 %all-to-all-start.3 = ((f32[16,32,128]{2,1,0:T(8,128)}), f32[16,32,128]{2,1,0:T(8,128)S(1)}, u32[]{:S(2)}, u32[]{:S(2)}) async-start(f32[16,32,128]{2,1,0:T(8,128)} %select_reduce_fusion), calls=%async_computation.3 | async-start | bytes 524288 | tf_op jit(solution)/shard_map/all_to_all | solution.py:41
  67.7 1.0 %copy-start.4 = (f32[4,128,256]{2,1,0:T(8,128)S(1)}, f32[4,128,256]{2,1,0:T(8,128)}, u32[]{:S(2)}) copy-start(f32[4,128,256]{2,1,0:T(8,128)} %fusion.40) | copy-start | bytes 1572868

commit v15 on v12

--- a/solution.py
+++ b/solution.py
@@ -2,6 +2,7 @@
 import jax.numpy as jnp
 from jax import lax
 from jax.sharding import PartitionSpec as P
+from jax.experimental.layout import Layout, with_layout_constraint
 
 GROUP = 256
 
@@ -45,12 +46,17 @@
     return exclusive_scan(own_total, True)
 
 
+def head_major(array):
+    order = tuple(range(array.ndim - 3)) + (array.ndim - 2, array.ndim - 3, array.ndim - 1)
+    return with_layout_constraint(array, Layout(order))
+
+
 def body(query_raw, key_raw, value_raw, out_gain, out_grad):
     tok_rows, head_count, width = query_raw.shape
     blocks = tok_rows // GROUP
     blocked = (blocks, GROUP, head_count, width)
-    query_act = jax.nn.silu(query_raw.astype(jnp.float32)).astype(jnp.bfloat16).reshape(blocked)
-    key_act = jax.nn.silu(key_raw.astype(jnp.float32)).astype(jnp.bfloat16).reshape(blocked)
+    query_act = head_major(jax.nn.silu(query_raw.astype(jnp.float32)).astype(jnp.bfloat16).reshape(blocked))
+    key_act = head_major(jax.nn.silu(key_raw.astype(jnp.float32)).astype(jnp.bfloat16).reshape(blocked))
     value_blk = value_raw.reshape(blocked)
     mask = causal_mask(GROUP)[None, None]
     block_kv = jnp.einsum("cshd,cshe->chde", key_act, value_blk, preferred_element_type=jnp.float32)
@@ -80,7 +86,7 @@
         grad_in * inv_rms[:, None, None]
         - mixed * (cross_total * inv_rms**3 / features)[:, None, None]
     ).astype(jnp.bfloat16)
-    delta_blk = delta.reshape(blocked)
+    delta_blk = head_major(delta.reshape(blocked))
     block_grad = jnp.einsum(
         "cthd,cthe->chde", query_act, delta_blk, preferred_element_type=jnp.float32
     )

time: 69.4 us -> 70.4 us (1.014)
  matrix products: 5.22 us -> 6.48 us
  local copies, waits for them, and re-layouts: 5.75 us -> 4.56 us
  waiting for transfers between devices: 36 us -> 37 us
    unnamed x15 -> x14, local copies, waits for them, and re-layouts: 5.75 us -> 4.56 us
    all_to_all x2, waiting for transfers between devices: 17.6 us -> 18.7 us  [exclusive_scan(): lax.all_to_all(rows.reshape(count, chunk, width), 'seq', 0, 0, tiled=True)]
    dot_general x1, matrix products: 0.98 us -> 2.01 us  [body(): jnp.einsum('cshd,cshe->chde', key_act, value_blk, preferred_element_type=...]
  transfers between devices with their start and end apart: 5 -> 5, of which waited for: 5 -> 5; matrix products, arithmetic and copies ran while one was open for 5% -> 4% of each run, Pallas kernels for 0% -> 0%
where the time goes in v15:
time: 70.4 us; the launch traced here: 69.8 us
  waiting for transfers between devices  37 us (53%)
  starting transfers between devices  19.1 us (27%)
  matrix products  6.48 us (9%)
  local copies, waits for them, and re-layouts  4.56 us (6%)
  other arithmetic  1.84 us (3%)
  between operations  0.83 us (1%)
    all_to_all x2, waiting for transfers between devices, exclusive_scan(): lax.all_to_all(rows.reshape(count, chunk, width), 'seq', 0, 0, tiled=True)  18.7 us
    all_to_all x2, waiting for transfers between devices, exclusive_scan(): spread = lax.all_to_all(prefix, 'seq', 0, 0, tiled=True)  17.2 us
    all_to_all x2, starting transfers between devices, exclusive_scan(): lax.all_to_all(rows.reshape(count, chunk, width), 'seq', 0, 0, tiled=True)  11.9 us
    all_to_all x2, starting transfers between devices, exclusive_scan(): spread = lax.all_to_all(prefix, 'seq', 0, 0, tiled=True)  7.21 us
    unnamed x14, local copies, waits for them, and re-layouts  4.56 us
    dot_general x1, matrix products, body(): jnp.einsum('cshd,cshe->chde', key_act, value_blk, preferred_element_type=...  2.01 us
    another operation x2, other arithmetic, exclusive_scan(): inclusive = lax.cumsum(gathered, axis=0, reverse=reverse)  1.51 us
  transfers between devices with their start and end apart: 5, of which 5 were waited for; matrix products, arithmetic and copies ran while one was open for 4% of the time, Pallas kernels for 0%

profile of v15, /device:TPU:0, one launch (start us, length us, event | category | flops | bytes accessed | tf_op | source)
XLA Modules:
  0.0 69.8 jit_solution(7427991608759633689)
XLA Ops:
  0.6 0.9 %copy-done = bf16[256,4,128]{2,1,0:T(4,128)(2,1)S(1)} copy-done((bf16[256,4,128]{2,1,0:T(4,128)(2,1)S(1)}, bf16[256,4,128]{2,1,0:T(4,128)(2,1)}, u32[]{:S(2)}) %copy-start) | copy-done | bytes 262168
  1.6 2.0 %fusion.26 = f32[4,128,128]{2,1,0:T(8,128)} fusion(bf16[256,4,128]{2,1,0:T(4,128)(2,1)S(1)} %copy-done, bf16[256,4,128]{2,1,0:T(4,128)(2,1)} %param.6), kind=kOutput, calls=%fused_computation.49 | convolution fusion | flops 34340864 | bytes 786432 | tf_op jit(solution)/shard_map/cshd,cshe->chde/dot_general | solution.py:62
  3.6 8.3 %all-to-all-start = ((f32[16,32,128]{2,1,0:T(8,128)}), f32[16,32,128]{2,1,0:T(8,128)S(1)}, u32[]{:S(2)}, u32[]{:S(2)}) async-start(f32[16,32,128]{2,1,0:T(8,128)} %bitcast.3), calls=%async_computation | async-start | bytes 524288 | tf_op jit(solution)/shard_map/all_to_all | solution.py:34
  12.0 9.8 %all-to-all-done = f32[16,32,128]{2,1,0:T(8,128)S(1)} async-done(((f32[16,32,128]{2,1,0:T(8,128)}), f32[16,32,128]{2,1,0:T(8,128)S(1)}, u32[]{:S(2)}, u32[]{:S(2)}) %all-to-all-start) | async-done | bytes 262176 | tf_op jit(solution)/shard_map/all_to_all | solution.py:34
  21.8 0.7 %reduce-window_subtract_fusion.1 = f32[16,32,128]{2,1,0:T(8,128)} fusion(f32[16,32,128]{2,1,0:T(8,128)S(1)} %all-to-all-done), kind=kOutput, calls=%fused_computation.18 | output fusion | flops 1048576 | bytes 524288 | tf_op jit(solution)/shard_map/exclusive_scan/reduce_window_sum | solution.py:35
  22.5 3.7 %all-to-all-start.1 = ((f32[16,32,128]{2,1,0:T(8,128)}), f32[16,32,128]{2,1,0:T(8,128)S(1)}, u32[]{:S(2)}, u32[]{:S(2)}) async-start(f32[16,32,128]{2,1,0:T(8,128)} %reduce-window_subtract_fusion.1), calls=%async_computation.1 | async-start | bytes 524288 | tf_op jit(solution)/shard_map/all_to_all | solution.py:37
  26.2 0.4 fusion
  27.0 8.4 %all-to-all-done.1 = f32[16,32,128]{2,1,0:T(8,128)S(1)} async-done(((f32[16,32,128]{2,1,0:T(8,128)}), f32[16,32,128]{2,1,0:T(8,128)S(1)}, u32[]{:S(2)}, u32[]{:S(2)}) %all-to-all-start.1) | async-done | bytes 262176 | tf_op jit(solution)/shard_map/all_to_all | solution.py:37
  35.5 0.4 multiply_reduce_fusion.1
  36.0 1.1 %collective-permute-done = f32[2,256]{1,0:T(2,128)S(1)} collective-permute-done((f32[2,256]{1,0:T(2,128)S(1)}, f32[2,256]{1,0:T(2,128)S(1)}, u32[]{:S(2)}, u32[]{:S(2)}) %collective-permute-start) | collective-permute-done | bytes 2080 | tf_op jit(solution)/shard_map/ppermute | solution.py:80
  37.4 1.1 %fusion.42 = f32[4,128,128]{2,1,0:T(8,128)} fusion(bf16[256,4,128]{2,0,1:T(8,128)(2,1)S(1)} %get-tuple-element.14, bf16[256,4,128]{2,1,0:T(4,128)(2,1)S(1)} %copy-done.3), kind=kOutput, calls=%fused_computation.61 | convolution fusion | flops 34340864 | bytes 786432 | tf_op jit(solution)/shard_map/cthd,cthe->chde/dot_general | solution.py:90
  38.7 0.9 %copy.43 = bf16[256,4,128]{2,1,0:T(4,128)(2,1)} copy(bf16[256,4,128]{2,0,1:T(8,128)(2,1)S(1)} %get-tuple-element.15) | data formatting | bytes 524288
  39.6 3.5 %all-to-all-start.2 = ((f32[16,32,128]{2,1,0:T(8,128)}), f32[16,32,128]{2,1,0:T(8,128)S(1)}, u32[]{:S(2)}, u32[]{:S(2)}) async-start(f32[16,32,128]{2,1,0:T(8,128)} %bitcast.18), calls=%async_computation.2 | async-start | bytes 524288 | tf_op jit(solution)/shard_map/all_to_all | solution.py:34
  43.2 0.4 fusion.33
  43.5 0.3 fusion.7
  43.9 0.9 %copy.44 = bf16[256,4,128]{2,1,0:T(4,128)(2,1)} copy(bf16[256,4,128]{2,0,1:T(8,128)(2,1)S(1)} %fusion.7) | data formatting | bytes 524288
  44.8 8.8 %all-to-all-done.2 = f32[16,32,128]{2,1,0:T(8,128)S(1)} async-done(((f32[16,32,128]{2,1,0:T(8,128)}), f32[16,32,128]{2,1,0:T(8,128)S(1)}, u32[]{:S(2)}, u32[]{:S(2)}) %all-to-all-start.2) | async-done | bytes 262176 | tf_op jit(solution)/shard_map/all_to_all | solution.py:34
  53.6 0.8 %reduce-window_subtract_fusion = f32[16,32,128]{2,1,0:T(8,128)} fusion(f32[16,32,128]{2,1,0:T(8,128)S(1)} %all-to-all-done.2), kind=kOutput, calls=%fused_computation.17 | output fusion | flops 1048576 | bytes 524288 | tf_op jit(solution)/shard_map/exclusive_scan/reduce_window_sum | solution.py:35
  54.4 3.5 %all-to-all-start.3 = ((f32[16,32,128]{2,1,0:T(8,128)}), f32[16,32,128]{2,1,0:T(8,128)S(1)}, u32[]{:S(2)}, u32[]{:S(2)}) async-start(f32[16,32,128]{2,1,0:T(8,128)} %reduce-window_subtract_fusion), calls=%async_computation.3 | async-start | bytes 524288 | tf_op jit(solution)/shard_map/all_to_all | solution.py:37
  58.2 0.4 fusion.38
  58.6 8.7 %all-to-all-done.3 = f32[16,32,128]{2,1,0:T(8,128)S(1)} async-done(((f32[16,32,128]{2,1,0:T(8,128)}), f32[16,32,128]{2,1,0:T(8,128)S(1)}, u32[]{:S(2)}, u32[]{:S(2)}) %all-to-all-start.3) | async-done | bytes 262176 | tf_op jit(solution)/shard_map/all_to_all | solution.py:37
  67.4 0.3 fusion.10
  67.7 0.9 %copy.46 = bf16[256,4,128]{2,1,0:T(4,128)(2,1)} copy(bf16[256,4,128]{0,2,1:T(8,128)(2,1)S(1)} %fusion.10) | data formatting | bytes 524288
  68.9 0.9 %copy.45 = bf16[256,4,128]{2,1,0:T(4,128)(2,1)} copy(bf16[256,4,128]{2,0,1:T(8,128)(2,1)S(1)} %fusion.8) | data formatting | bytes 524288
  (22 shorter events, 1.6 us)
Async XLA Ops:
  0.6 1.0 %copy-start = (bf16[256,4,128]{2,1,0:T(4,128)(2,1)S(1)}, bf16[256,4,128]{2,1,0:T(4,128)(2,1)}, u32[]{:S(2)}) copy-start(bf16[256,4,128]{2,1,0:T(4,128)(2,1)} %param.7) | copy-start | bytes 786436
  3.6 18.2 %all-to-all-start = ((f32[16,32,128]{2,1,0:T(8,128)}), f32[16,32,128]{2,1,0:T(8,128)S(1)}, u32[]{:S(2)}, u32[]{:S(2)}) async-start(f32[16,32,128]{2,1,0:T(8,128)} %bitcast.3), calls=%async_computation | async-start | bytes 524288 | tf_op jit(solution)/shard_map/all_to_all | solution.py:34
  22.5 3.7 %copy-start.3 = (bf16[256,4,128]{2,1,0:T(4,128)(2,1)S(1)}, bf16[256,4,128]{2,1,0:T(4,128)(2,1)}, u32[]{:S(2)}) copy-start(bf16[256,4,128]{2,1,0:T(4,128)(2,1)} %param.5) | copy-start | bytes 786436
  22.5 3.7 %copy-start.4 = (bf16[256,4,128]{2,1,0:T(4,128)(2,1)S(1)}, bf16[256,4,128]{2,1,0:T(4,128)(2,1)}, u32[]{:S(2)}) copy-start(bf16[256,4,128]{2,1,0:T(4,128)(2,1)} %param.6) | copy-start | bytes 786436
  22.5 12.9 %all-to-all-start.1 = ((f32[16,32,128]{2,1,0:T(8,128)}), f32[16,32,128]{2,1,0:T(8,128)S(1)}, u32[]{:S(2)}, u32[]{:S(2)}) async-start(f32[16,32,128]{2,1,0:T(8,128)} %reduce-window_subtract_fusion.1), calls=%async_computation.1 | async-start | bytes 524288 | tf_op jit(solution)/shard_map/all_to_all | solution.py:37
  27.0 8.5 %copy-start.1 = (bf16[256,4,128]{2,1,0:T(4,128)(2,1)S(1)}, bf16[256,4,128]{2,1,0:T(4,128)(2,1)}, u32[]{:S(2)}) copy-start(bf16[256,4,128]{2,1,0:T(4,128)(2,1)} %param.9) | copy-start | bytes 786436
  27.0 8.5 %copy-start.2 = (f32[4,128]{1,0:T(4,128)S(1)}, f32[4,128]{1,0:T(4,128)}, u32[]{:S(2)}) copy-start(f32[4,128]{1,0:T(4,128)} %param.8) | copy-start | bytes 6148
  35.9 1.2 %collective-permute-start = (f32[2,256]{1,0:T(2,128)S(1)}, f32[2,256]{1,0:T(2,128)S(1)}, u32[]{:S(2)}, u32[]{:S(2)}) collective-permute-start(f32[2,256]{1,0:T(2,128)S(1)} %pad_maximum_fusion), channel_id=1, source_target_pairs={{0,1},{1,0},{2,3},{3,2},{4,5},{5,4},{6,7},{7,6},{8,9},{9,8},{10,11... | collective-permute-start | bytes 6152 | tf_op jit(solution)/shard_map/ppermute | solution.py:80
  39.6 14.0 %all-to-all-start.2 = ((f32[16,32,128]{2,1,0:T(8,128)}), f32[16,32,128]{2,1,0:T(8,128)S(1)}, u32[]{:S(2)}, u32[]{:S(2)}) async-start(f32[16,32,128]{2,1,0:T(8,128)} %bitcast.18), calls=%async_computation.2 | async-start | bytes 524288 | tf_op jit(solution)/shard_map/all_to_all | solution.py:34
  54.4 13.0 %all-to-all-start.3 = ((f32[16,32,128]{2,1,0:T(8,128)}), f32[16,32,128]{2,1,0:T(8,128)S(1)}, u32[]{:S(2)}, u32[]{:S(2)}) async-start(f32[16,32,128]{2,1,0:T(8,128)} %reduce-window_subtract_fusion), calls=%async_computation.3 | async-start | bytes 524288 | tf_op jit(solution)/shard_map/all_to_all | solution.py:37

commit v16 on v12

--- a/solution.py
+++ b/solution.py
@@ -23,7 +23,7 @@
     return cols <= rows
 
 
-def exclusive_scan(own_total, reverse):
+def exclusive_scan(own_total, reverse, early=None, late=None):
     count = lax.axis_size("seq")
     width = own_total.shape[-1]
     rows = own_total.reshape(-1, width)
@@ -31,18 +31,25 @@
     chunk = -(-size // count)
     rows = jnp.pad(rows, ((0, chunk * count - size), (0, 0)))
     gathered = lax.all_to_all(rows.reshape(count, chunk, width), "seq", 0, 0, tiled=True)
+    if early is not None:
+        gathered, early = lax.optimization_barrier((gathered, early))
     inclusive = lax.cumsum(gathered, axis=0, reverse=reverse)
     prefix = inclusive - gathered
+    if late is not None:
+        prefix, late = lax.optimization_barrier((prefix, late))
     spread = lax.all_to_all(prefix, "seq", 0, 0, tiled=True)
-    return spread.reshape(-1, width)[:size].reshape(own_total.shape)
+    spread = spread.reshape(-1, width)[:size].reshape(own_total.shape)
+    if early is None:
+        return spread
+    return spread, early, late
 
 
 def lower_sum(own_total):
     return exclusive_scan(own_total, False)
 
 
-def upper_sum(own_total):
-    return exclusive_scan(own_total, True)
+def upper_sum(own_total, early, late):
+    return exclusive_scan(own_total, True, early, late)
 
 
 def body(query_raw, key_raw, value_raw, out_gain, out_grad):
@@ -75,7 +82,6 @@
     sq_total, cross_total = both[0], both[1]
     features = head_count * width * lax.axis_size("head")
     inv_rms = lax.rsqrt(sq_total / features + 1e-06)
-    normed_out = (mixed * inv_rms[:, None, None] * out_gain).astype(jnp.bfloat16)
     delta = (
         grad_in * inv_rms[:, None, None]
         - mixed * (cross_total * inv_rms**3 / features)[:, None, None]
@@ -85,12 +91,13 @@
         "cthd,cthe->chde", query_act, delta_blk, preferred_element_type=jnp.float32
     )
     own_grad = jnp.sum(block_grad, axis=0)
-    after = upper_sum(own_grad)
+    normed_out = (mixed * inv_rms[:, None, None] * out_gain).astype(jnp.bfloat16)
+    after, delta_late, _ = upper_sum(own_grad, delta_blk, None)
     if blocks == 1:
         grad_state = lax.reduce_precision(after[None], 8, 7).astype(jnp.bfloat16)
     else:
         grad_state = (after[None] + (lax.cumsum(block_grad, axis=0, reverse=True) - block_grad)).astype(jnp.bfloat16)
-    bscore = jnp.einsum("cthe,cshe->chts", delta_blk, value_blk, preferred_element_type=jnp.float32)
+    bscore = jnp.einsum("cthe,cshe->chts", delta_late, value_blk, preferred_element_type=jnp.float32)
     bscore = jnp.where(mask, bscore, 0.0).astype(jnp.bfloat16)
     dquery = jnp.einsum("chts,cshd->cthd", bscore, key_act, preferred_element_type=jnp.float32)
     dquery = dquery + jnp.einsum(

time: 69.4 us -> 68.1 us (0.981)
  waiting for transfers between devices: 36 us -> 34.8 us
    all_to_all x2, waiting for transfers between devices: 17.3 us -> 15.6 us  [exclusive_scan(): spread = lax.all_to_all(prefix, 'seq', 0, 0, tiled=True)]
  transfers between devices with their start and end apart: 5 -> 5, of which waited for: 5 -> 5; matrix products, arithmetic and copies ran while one was open for 5% -> 7% of each run, Pallas kernels for 0% -> 0%
where the time goes in v16:
time: 68.1 us; the launch traced here: 67.5 us
  waiting for transfers between devices  34.8 us (51%)
  starting transfers between devices  19.1 us (28%)
  local copies, waits for them, and re-layouts  5.75 us (8%)
  matrix products  5.23 us (8%)
  other arithmetic  1.8 us (3%)
  between operations  0.84 us (1%)
    all_to_all x2, waiting for transfers between devices, exclusive_scan(): lax.all_to_all(rows.reshape(count, chunk, width), 'seq', 0, 0, tiled=True)  18 us
    all_to_all x2, waiting for transfers between devices, exclusive_scan(): spread = lax.all_to_all(prefix, 'seq', 0, 0, tiled=True)  15.6 us
    all_to_all x2, starting transfers between devices, exclusive_scan(): lax.all_to_all(rows.reshape(count, chunk, width), 'seq', 0, 0, tiled=True)  12 us
    all_to_all x2, starting transfers between devices, exclusive_scan(): spread = lax.all_to_all(prefix, 'seq', 0, 0, tiled=True)  7.08 us
    unnamed x15, local copies, waits for them, and re-layouts  5.75 us
    another operation x2, other arithmetic, exclusive_scan(): inclusive = lax.cumsum(gathered, axis=0, reverse=reverse)  1.51 us
  transfers between devices with their start and end apart: 5, of which 5 were waited for; matrix products, arithmetic and copies ran while one was open for 7% of the time, Pallas kernels for 0%

profile of v16, /device:TPU:0, one launch (start us, length us, event | category | flops | bytes accessed | tf_op | source)
XLA Modules:
  0.0 67.5 jit_solution(12655289496760834081)
XLA Ops:
  0.6 1.1 %copy.30 = bf16[256,4,128]{0,2,1:T(8,128)(2,1)S(1)} copy(bf16[256,4,128]{2,1,0:T(4,128)(2,1)} %param.6) | data formatting | bytes 524288 | tf_op args[1]
  1.8 1.0 %fusion.27 = f32[4,128,128]{2,1,0:T(8,128)} fusion(bf16[256,4,128]{2,1,0:T(4,128)(2,1)S(1)} %copy-done, bf16[256,4,128]{0,2,1:T(8,128)(2,1)S(1)} %copy.30), kind=kOutput, calls=%fused_computation.50 | convolution fusion | flops 34340864 | bytes 786432 | tf_op jit(solution)/shard_map/cshd,cshe->chde/dot_general | solution.py:63
  2.8 8.4 %all-to-all-start = ((f32[16,32,128]{2,1,0:T(8,128)}), f32[16,32,128]{2,1,0:T(8,128)S(1)}, u32[]{:S(2)}, u32[]{:S(2)}) async-start(f32[16,32,128]{2,1,0:T(8,128)} %bitcast.1), calls=%async_computation | async-start | bytes 524288 | tf_op jit(solution)/shard_map/all_to_all | solution.py:33
  11.4 0.8 %copy-done.2 = bf16[256,4,128]{2,1,0:T(4,128)(2,1)S(1)} copy-done((bf16[256,4,128]{2,1,0:T(4,128)(2,1)S(1)}, bf16[256,4,128]{2,1,0:T(4,128)(2,1)}, u32[]{:S(2)}) %copy-start.2) | copy-done | bytes 262168
  12.4 8.7 %all-to-all-done = f32[16,32,128]{2,1,0:T(8,128)S(1)} async-done(((f32[16,32,128]{2,1,0:T(8,128)}), f32[16,32,128]{2,1,0:T(8,128)S(1)}, u32[]{:S(2)}, u32[]{:S(2)}) %all-to-all-start) | async-done | bytes 262176 | tf_op jit(solution)/shard_map/all_to_all | solution.py:33
  21.1 0.7 %reduce-window_subtract_fusion.1 = f32[16,32,128]{2,1,0:T(8,128)} fusion(f32[16,32,128]{2,1,0:T(8,128)S(1)} %all-to-all-done), kind=kOutput, calls=%fused_computation.18 | output fusion | flops 1048576 | bytes 524288 | tf_op jit(solution)/shard_map/exclusive_scan/reduce_window_sum | solution.py:36
  21.8 3.5 %all-to-all-start.1 = ((f32[16,32,128]{2,1,0:T(8,128)}), f32[16,32,128]{2,1,0:T(8,128)S(1)}, u32[]{:S(2)}, u32[]{:S(2)}) async-start(f32[16,32,128]{2,1,0:T(8,128)} %reduce-window_subtract_fusion.1), calls=%async_computation.1 | async-start | bytes 524288 | tf_op jit(solution)/shard_map/all_to_all | solution.py:40
  25.4 0.5 fusion
  26.2 8.4 %all-to-all-done.1 = f32[16,32,128]{2,1,0:T(8,128)S(1)} async-done(((f32[16,32,128]{2,1,0:T(8,128)}), f32[16,32,128]{2,1,0:T(8,128)S(1)}, u32[]{:S(2)}, u32[]{:S(2)}) %all-to-all-start.1) | async-done | bytes 262176 | tf_op jit(solution)/shard_map/all_to_all | solution.py:40
  34.6 0.3 multiply_reduce_fusion.1
  35.1 1.1 %collective-permute-done = f32[2,256]{1,0:T(2,128)S(1)} collective-permute-done((f32[2,256]{1,0:T(2,128)S(1)}, f32[2,256]{1,0:T(2,128)S(1)}, u32[]{:S(2)}, u32[]{:S(2)}) %collective-permute-start) | collective-permute-done | bytes 2080 | tf_op jit(solution)/shard_map/ppermute | solution.py:81
  36.4 1.0 %fusion.41 = f32[4,128,128]{2,1,0:T(8,128)} fusion(bf16[256,4,128]{0,2,1:T(8,128)(2,1)S(1)} %get-tuple-element.18, bf16[256,4,128]{0,2,1:T(8,128)(2,1)S(1)} %copy.29), kind=kOutput, calls=%fused_computation.62 | convolution fusion | flops 34340864 | bytes 786432 | tf_op jit(solution)/shard_map/cthd,cthe->chde/dot_general | solution.py:90
  37.4 3.5 %all-to-all-start.2 = ((f32[16,32,128]{2,1,0:T(8,128)}), f32[16,32,128]{2,1,0:T(8,128)S(1)}, u32[]{:S(2)}, u32[]{:S(2)}) async-start(f32[16,32,128]{2,1,0:T(8,128)} %bitcast.12), calls=%async_computation.2 | async-start | bytes 524288 | tf_op jit(solution)/shard_map/all_to_all | solution.py:33
  41.0 0.9 %copy.45 = bf16[256,4,128]{2,1,0:T(4,128)(2,1)} copy(bf16[256,4,128]{0,2,1:T(8,128)(2,1)S(1)} %get-tuple-element.19) | data formatting | bytes 524288
  42.1 9.3 %all-to-all-done.2 = f32[16,32,128]{2,1,0:T(8,128)S(1)} async-done(((f32[16,32,128]{2,1,0:T(8,128)}), f32[16,32,128]{2,1,0:T(8,128)S(1)}, u32[]{:S(2)}, u32[]{:S(2)}) %all-to-all-start.2) | async-done | bytes 262176 | tf_op jit(solution)/shard_map/all_to_all | solution.py:33
  51.4 0.8 %reduce-window_subtract_fusion = f32[16,32,128]{2,1,0:T(8,128)} fusion(f32[16,32,128]{2,1,0:T(8,128)S(1)} %all-to-all-done.2), kind=kOutput, calls=%fused_computation.17 | output fusion | flops 1048576 | bytes 524288 | tf_op jit(solution)/shard_map/exclusive_scan/reduce_window_sum | solution.py:36
  52.2 3.5 %all-to-all-start.3 = ((f32[16,32,128]{2,1,0:T(8,128)}), f32[16,32,128]{2,1,0:T(8,128)S(1)}, u32[]{:S(2)}, u32[]{:S(2)}) async-start(f32[16,32,128]{2,1,0:T(8,128)} %reduce-window_subtract_fusion), calls=%async_computation.3 | async-start | bytes 524288 | tf_op jit(solution)/shard_map/all_to_all | solution.py:40
  55.7 0.3 fusion.1
  56.1 0.3 fusion.35
  56.7 0.9 %copy.46 = bf16[256,4,128]{2,1,0:T(4,128)(2,1)} copy(bf16[256,4,128]{0,2,1:T(8,128)(2,1)S(1)} %fusion.7) | data formatting | bytes 524288
  57.9 7.3 %all-to-all-done.3 = f32[16,32,128]{2,1,0:T(8,128)S(1)} async-done(((f32[16,32,128]{2,1,0:T(8,128)}), f32[16,32,128]{2,1,0:T(8,128)S(1)}, u32[]{:S(2)}, u32[]{:S(2)}) %all-to-all-start.3) | async-done | bytes 262176 | tf_op jit(solution)/shard_map/all_to_all | solution.py:40
  65.1 0.3 fusion.10
  65.5 0.9 %copy.48 = bf16[256,4,128]{2,1,0:T(4,128)(2,1)} copy(bf16[256,4,128]{0,2,1:T(8,128)(2,1)S(1)} %fusion.10) | data formatting | bytes 524288
  66.7 0.9 %copy.47 = bf16[256,4,128]{2,1,0:T(4,128)(2,1)} copy(bf16[256,4,128]{0,2,1:T(8,128)(2,1)S(1)} %fusion.8) | data formatting | bytes 524288
  (23 shorter events, 2.2 us)
Async XLA Ops:
  0.6 1.2 %copy-start = (bf16[256,4,128]{2,1,0:T(4,128)(2,1)S(1)}, bf16[256,4,128]{2,1,0:T(4,128)(2,1)}, u32[]{:S(2)}) copy-start(bf16[256,4,128]{2,1,0:T(4,128)(2,1)} %param.7) | copy-start | bytes 786436
  2.8 8.5 %copy-start.1 = (bf16[256,4,128]{2,1,0:T(4,128)(2,1)S(1)}, bf16[256,4,128]{2,1,0:T(4,128)(2,1)}, u32[]{:S(2)}) copy-start(bf16[256,4,128]{2,1,0:T(4,128)(2,1)} %param.5) | copy-start | bytes 786436
  2.8 18.3 %all-to-all-start = ((f32[16,32,128]{2,1,0:T(8,128)}), f32[16,32,128]{2,1,0:T(8,128)S(1)}, u32[]{:S(2)}, u32[]{:S(2)}) async-start(f32[16,32,128]{2,1,0:T(8,128)} %bitcast.1), calls=%async_computation | async-start | bytes 524288 | tf_op jit(solution)/shard_map/all_to_all | solution.py:33
  11.3 1.0 %copy-start.2 = (bf16[256,4,128]{2,1,0:T(4,128)(2,1)S(1)}, bf16[256,4,128]{2,1,0:T(4,128)(2,1)}, u32[]{:S(2)}) copy-start(bf16[256,4,128]{2,1,0:T(4,128)(2,1)} %param.9) | copy-start | bytes 786436
  21.8 12.8 %all-to-all-start.1 = ((f32[16,32,128]{2,1,0:T(8,128)}), f32[16,32,128]{2,1,0:T(8,128)S(1)}, u32[]{:S(2)}, u32[]{:S(2)}) async-start(f32[16,32,128]{2,1,0:T(8,128)} %reduce-window_subtract_fusion.1), calls=%async_computation.1 | async-start | bytes 524288 | tf_op jit(solution)/shard_map/all_to_all | solution.py:40
  26.2 8.4 %copy-start.3 = (f32[4,128]{1,0:T(4,128)S(1)}, f32[4,128]{1,0:T(4,128)}, u32[]{:S(2)}) copy-start(f32[4,128]{1,0:T(4,128)} %param.8) | copy-start | bytes 6148
  35.0 1.2 %collective-permute-start = (f32[2,256]{1,0:T(2,128)S(1)}, f32[2,256]{1,0:T(2,128)S(1)}, u32[]{:S(2)}, u32[]{:S(2)}) collective-permute-start(f32[2,256]{1,0:T(2,128)S(1)} %pad_maximum_fusion), channel_id=1, source_target_pairs={{0,1},{1,0},{2,3},{3,2},{4,5},{5,4},{6,7},{7,6},{8,9},{9,8},{10,11... | collective-permute-start | bytes 6152 | tf_op jit(solution)/shard_map/ppermute | solution.py:81
  37.4 14.0 %all-to-all-start.2 = ((f32[16,32,128]{2,1,0:T(8,128)}), f32[16,32,128]{2,1,0:T(8,128)S(1)}, u32[]{:S(2)}, u32[]{:S(2)}) async-start(f32[16,32,128]{2,1,0:T(8,128)} %bitcast.12), calls=%async_computation.2 | async-start | bytes 524288 | tf_op jit(solution)/shard_map/all_to_all | solution.py:33
  52.2 13.0 %all-to-all-start.3 = ((f32[16,32,128]{2,1,0:T(8,128)}), f32[16,32,128]{2,1,0:T(8,128)S(1)}, u32[]{:S(2)}, u32[]{:S(2)}) async-start(f32[16,32,128]{2,1,0:T(8,128)} %reduce-window_subtract_fusion), calls=%async_computation.3 | async-start | bytes 524288 | tf_op jit(solution)/shard_map/all_to_all | solution.py:40

commit v17 on v16

--- a/solution.py
+++ b/solution.py
@@ -82,13 +82,15 @@
     sq_total, cross_total = both[0], both[1]
     features = head_count * width * lax.axis_size("head")
     inv_rms = lax.rsqrt(sq_total / features + 1e-06)
-    delta = (
+    delta_f32 = (
         grad_in * inv_rms[:, None, None]
         - mixed * (cross_total * inv_rms**3 / features)[:, None, None]
-    ).astype(jnp.bfloat16)
+    )
+    delta = delta_f32.astype(jnp.bfloat16)
     delta_blk = delta.reshape(blocked)
     block_grad = jnp.einsum(
-        "cthd,cthe->chde", query_act, delta_blk, preferred_element_type=jnp.float32
+        "cthd,cthe->chde", query_act.astype(jnp.float32), delta_f32.reshape(blocked),
+        preferred_element_type=jnp.float32, precision=lax.Precision.HIGHEST,
     )
     own_grad = jnp.sum(block_grad, axis=0)
     normed_out = (mixed * inv_rms[:, None, None] * out_gain).astype(jnp.bfloat16)

time: 68.1 us -> 68.4 us (level)
    unnamed x15 -> x19, local copies, waits for them, and re-layouts: 5.75 us -> 5.76 us
where the time goes in v17:
time: 68.4 us; the launch traced here: 67.8 us
  waiting for transfers between devices  34.6 us (51%)
  starting transfers between devices  19.3 us (28%)
  local copies, waits for them, and re-layouts  5.76 us (8%)
  matrix products  5.57 us (8%)
  other arithmetic  1.8 us (3%)
  between operations  0.87 us (1%)
    all_to_all x2, waiting for transfers between devices, exclusive_scan(): lax.all_to_all(rows.reshape(count, chunk, width), 'seq', 0, 0, tiled=True)  17.8 us
    all_to_all x2, waiting for transfers between devices, exclusive_scan(): spread = lax.all_to_all(prefix, 'seq', 0, 0, tiled=True)  15.6 us
    all_to_all x2, starting transfers between devices, exclusive_scan(): lax.all_to_all(rows.reshape(count, chunk, width), 'seq', 0, 0, tiled=True)  12 us
    all_to_all x2, starting transfers between devices, exclusive_scan(): spread = lax.all_to_all(prefix, 'seq', 0, 0, tiled=True)  7.21 us
    unnamed x19, local copies, waits for them, and re-layouts  5.76 us
    another operation x2, other arithmetic, exclusive_scan(): inclusive = lax.cumsum(gathered, axis=0, reverse=reverse)  1.51 us
  transfers between devices with their start and end apart: 5, of which 5 were waited for; matrix products, arithmetic and copies ran while one was open for 7% of the time, Pallas kernels for 0%

profile of v17, /device:TPU:0, one launch (start us, length us, event | category | flops | bytes accessed | tf_op | source)
XLA Modules:
  0.0 67.8 jit_solution(9012242100626159381)
XLA Ops:
  0.6 1.1 %copy.30 = bf16[256,4,128]{0,2,1:T(8,128)(2,1)S(1)} copy(bf16[256,4,128]{2,1,0:T(4,128)(2,1)} %param.6) | data formatting | bytes 524288 | tf_op args[1]
  1.8 1.0 %fusion.32 = f32[4,128,128]{2,1,0:T(8,128)} fusion(bf16[256,4,128]{2,1,0:T(4,128)(2,1)S(1)} %copy-done, bf16[256,4,128]{0,2,1:T(8,128)(2,1)S(1)} %copy.30), kind=kOutput, calls=%fused_computation.55 | convolution fusion | flops 34340864 | bytes 786432 | tf_op jit(solution)/shard_map/cshd,cshe->chde/dot_general | solution.py:63
  2.8 8.4 %all-to-all-start = ((f32[16,32,128]{2,1,0:T(8,128)}), f32[16,32,128]{2,1,0:T(8,128)S(1)}, u32[]{:S(2)}, u32[]{:S(2)}) async-start(f32[16,32,128]{2,1,0:T(8,128)} %bitcast.1), calls=%async_computation | async-start | bytes 524288 | tf_op jit(solution)/shard_map/all_to_all | solution.py:33
  11.4 0.8 %copy-done.2 = bf16[256,4,128]{2,1,0:T(4,128)(2,1)S(1)} copy-done((bf16[256,4,128]{2,1,0:T(4,128)(2,1)S(1)}, bf16[256,4,128]{2,1,0:T(4,128)(2,1)}, u32[]{:S(2)}) %copy-start.2) | copy-done | bytes 262168
  12.4 8.7 %all-to-all-done = f32[16,32,128]{2,1,0:T(8,128)S(1)} async-done(((f32[16,32,128]{2,1,0:T(8,128)}), f32[16,32,128]{2,1,0:T(8,128)S(1)}, u32[]{:S(2)}, u32[]{:S(2)}) %all-to-all-start) | async-done | bytes 262176 | tf_op jit(solution)/shard_map/all_to_all | solution.py:33
  21.1 0.7 %reduce-window_subtract_fusion.1 = f32[16,32,128]{2,1,0:T(8,128)} fusion(f32[16,32,128]{2,1,0:T(8,128)S(1)} %all-to-all-done), kind=kOutput, calls=%fused_computation.18 | output fusion | flops 1048576 | bytes 524288 | tf_op jit(solution)/shard_map/exclusive_scan/reduce_window_sum | solution.py:36
  21.8 3.5 %all-to-all-start.1 = ((f32[16,32,128]{2,1,0:T(8,128)}), f32[16,32,128]{2,1,0:T(8,128)S(1)}, u32[]{:S(2)}, u32[]{:S(2)}) async-start(f32[16,32,128]{2,1,0:T(8,128)} %reduce-window_subtract_fusion.1), calls=%async_computation.1 | async-start | bytes 524288 | tf_op jit(solution)/shard_map/all_to_all | solution.py:40
  25.4 0.5 fusion
  26.2 8.4 %all-to-all-done.1 = f32[16,32,128]{2,1,0:T(8,128)S(1)} async-done(((f32[16,32,128]{2,1,0:T(8,128)}), f32[16,32,128]{2,1,0:T(8,128)S(1)}, u32[]{:S(2)}, u32[]{:S(2)}) %all-to-all-start.1) | async-done | bytes 262176 | tf_op jit(solution)/shard_map/all_to_all | solution.py:40
  34.6 0.3 multiply_reduce_fusion.1
  35.1 1.1 %collective-permute-done = f32[2,256]{1,0:T(2,128)S(1)} collective-permute-done((f32[2,256]{1,0:T(2,128)S(1)}, f32[2,256]{1,0:T(2,128)S(1)}, u32[]{:S(2)}, u32[]{:S(2)}) %collective-permute-start) | collective-permute-done | bytes 2080 | tf_op jit(solution)/shard_map/ppermute | solution.py:81
  36.2 1.3 %fusion.24 = f32[4,128,128]{2,1,0:T(8,128)} fusion(f32[256,4,128]{0,2,1:T(8,128)S(1)} %get-tuple-element.22, bf16[256,4,128]{0,2,1:T(8,128)(2,1)S(1)} %copy.37, f32[256]{0:T(256)S(1)} %fusion.35, f32[256]{0:T(256)S(1)} %bitcast.64, f32[4,128]{1,0:T(4,128)S(1)} %copy-done.5, bf16[256,4,128]{0,2,1:T(8,128)(2,1)S(1)} %copy.29), kind=kOutput, calls=%fused_computation.44 | convolution fusion | flops 202768384 | bytes 1314816 | tf_op jit(solution)/shard_map/cthd,cthe->chde/dot_general | solution.py:91
  37.6 3.5 %all-to-all-start.2 = ((f32[16,32,128]{2,1,0:T(8,128)}), f32[16,32,128]{2,1,0:T(8,128)S(1)}, u32[]{:S(2)}, u32[]{:S(2)}) async-start(f32[16,32,128]{2,1,0:T(8,128)} %bitcast.12), calls=%async_computation.2 | async-start | bytes 524288 | tf_op jit(solution)/shard_map/all_to_all | solution.py:33
  41.3 0.9 %copy.45 = bf16[256,4,128]{2,1,0:T(4,128)(2,1)} copy(bf16[256,4,128]{0,2,1:T(8,128)(2,1)S(1)} %get-tuple-element.19) | data formatting | bytes 524288
  42.4 9.1 %all-to-all-done.2 = f32[16,32,128]{2,1,0:T(8,128)S(1)} async-done(((f32[16,32,128]{2,1,0:T(8,128)}), f32[16,32,128]{2,1,0:T(8,128)S(1)}, u32[]{:S(2)}, u32[]{:S(2)}) %all-to-all-start.2) | async-done | bytes 262176 | tf_op jit(solution)/shard_map/all_to_all | solution.py:33
  51.5 0.8 %reduce-window_subtract_fusion = f32[16,32,128]{2,1,0:T(8,128)} fusion(f32[16,32,128]{2,1,0:T(8,128)S(1)} %all-to-all-done.2), kind=kOutput, calls=%fused_computation.17 | output fusion | flops 1048576 | bytes 524288 | tf_op jit(solution)/shard_map/exclusive_scan/reduce_window_sum | solution.py:36
  52.3 3.7 %all-to-all-start.3 = ((f32[16,32,128]{2,1,0:T(8,128)}), f32[16,32,128]{2,1,0:T(8,128)S(1)}, u32[]{:S(2)}, u32[]{:S(2)}) async-start(f32[16,32,128]{2,1,0:T(8,128)} %reduce-window_subtract_fusion), calls=%async_computation.3 | async-start | bytes 524288 | tf_op jit(solution)/shard_map/all_to_all | solution.py:40
  56.0 0.3 fusion.1
  56.4 0.3 fusion.45
  57.0 0.9 %copy.46 = bf16[256,4,128]{2,1,0:T(4,128)(2,1)} copy(bf16[256,4,128]{0,2,1:T(8,128)(2,1)S(1)} %fusion.7) | data formatting | bytes 524288
  58.2 7.3 %all-to-all-done.3 = f32[16,32,128]{2,1,0:T(8,128)S(1)} async-done(((f32[16,32,128]{2,1,0:T(8,128)}), f32[16,32,128]{2,1,0:T(8,128)S(1)}, u32[]{:S(2)}, u32[]{:S(2)}) %all-to-all-start.3) | async-done | bytes 262176 | tf_op jit(solution)/shard_map/all_to_all | solution.py:40
  65.4 0.3 fusion.10
  65.8 0.9 %copy.48 = bf16[256,4,128]{2,1,0:T(4,128)(2,1)} copy(bf16[256,4,128]{0,2,1:T(8,128)(2,1)S(1)} %fusion.10) | data formatting | bytes 524288
  67.0 0.9 %copy.47 = bf16[256,4,128]{2,1,0:T(4,128)(2,1)} copy(bf16[256,4,128]{0,2,1:T(8,128)(2,1)S(1)} %fusion.8) | data formatting | bytes 524288
  (27 shorter events, 2.2 us)
Async XLA Ops:
  0.6 1.2 %copy-start = (bf16[256,4,128]{2,1,0:T(4,128)(2,1)S(1)}, bf16[256,4,128]{2,1,0:T(4,128)(2,1)}, u32[]{:S(2)}) copy-start(bf16[256,4,128]{2,1,0:T(4,128)(2,1)} %param.7) | copy-start | bytes 786436
  2.8 8.5 %copy-start.1 = (bf16[256,4,128]{2,1,0:T(4,128)(2,1)S(1)}, bf16[256,4,128]{2,1,0:T(4,128)(2,1)}, u32[]{:S(2)}) copy-start(bf16[256,4,128]{2,1,0:T(4,128)(2,1)} %param.5) | copy-start | bytes 786436
  2.8 18.3 %all-to-all-start = ((f32[16,32,128]{2,1,0:T(8,128)}), f32[16,32,128]{2,1,0:T(8,128)S(1)}, u32[]{:S(2)}, u32[]{:S(2)}) async-start(f32[16,32,128]{2,1,0:T(8,128)} %bitcast.1), calls=%async_computation | async-start | bytes 524288 | tf_op jit(solution)/shard_map/all_to_all | solution.py:33
  11.3 1.0 %copy-start.2 = (bf16[256,4,128]{2,1,0:T(4,128)(2,1)S(1)}, bf16[256,4,128]{2,1,0:T(4,128)(2,1)}, u32[]{:S(2)}) copy-start(bf16[256,4,128]{2,1,0:T(4,128)(2,1)} %param.9) | copy-start | bytes 786436
  12.4 13.0 %copy-start.3 = (pred[256,256]{1,0:T(8,128)(4,1)}, pred[256,256]{1,0:T(8,128)(4,1)S(1)}, u32[]{:S(2)}) copy-start(pred[256,256]{1,0:T(8,128)(4,1)S(1)} %iota_compare_fusion) | copy-start | bytes 196612
  21.8 12.8 %all-to-all-start.1 = ((f32[16,32,128]{2,1,0:T(8,128)}), f32[16,32,128]{2,1,0:T(8,128)S(1)}, u32[]{:S(2)}, u32[]{:S(2)}) async-start(f32[16,32,128]{2,1,0:T(8,128)} %reduce-window_subtract_fusion.1), calls=%async_computation.1 | async-start | bytes 524288 | tf_op jit(solution)/shard_map/all_to_all | solution.py:40
  26.2 8.4 %copy-start.5 = (f32[4,128]{1,0:T(4,128)S(1)}, f32[4,128]{1,0:T(4,128)}, u32[]{:S(2)}) copy-start(f32[4,128]{1,0:T(4,128)} %param.8) | copy-start | bytes 6148
  35.0 1.2 %collective-permute-start = (f32[2,256]{1,0:T(2,128)S(1)}, f32[2,256]{1,0:T(2,128)S(1)}, u32[]{:S(2)}, u32[]{:S(2)}) collective-permute-start(f32[2,256]{1,0:T(2,128)S(1)} %pad_maximum_fusion), channel_id=1, source_target_pairs={{0,1},{1,0},{2,3},{3,2},{4,5},{5,4},{6,7},{7,6},{8,9},{9,8},{10,11... | collective-permute-start | bytes 6152 | tf_op jit(solution)/shard_map/ppermute | solution.py:81
  37.6 14.0 %all-to-all-start.2 = ((f32[16,32,128]{2,1,0:T(8,128)}), f32[16,32,128]{2,1,0:T(8,128)S(1)}, u32[]{:S(2)}, u32[]{:S(2)}) async-start(f32[16,32,128]{2,1,0:T(8,128)} %bitcast.12), calls=%async_computation.2 | async-start | bytes 524288 | tf_op jit(solution)/shard_map/all_to_all | solution.py:33
  52.3 3.7 %copy-start.4 = (pred[256,256]{1,0:T(8,128)(4,1)S(1)}, pred[256,256]{1,0:T(8,128)(4,1)}, u32[]{:S(2)}) copy-start(pred[256,256]{1,0:T(8,128)(4,1)} %copy-done.3) | copy-start | bytes 196612
  52.3 13.1 %all-to-all-start.3 = ((f32[16,32,128]{2,1,0:T(8,128)}), f32[16,32,128]{2,1,0:T(8,128)S(1)}, u32[]{:S(2)}, u32[]{:S(2)}) async-start(f32[16,32,128]{2,1,0:T(8,128)} %reduce-window_subtract_fusion), calls=%async_computation.3 | async-start | bytes 524288 | tf_op jit(solution)/shard_map/all_to_all | solution.py:40

commit v18 on v17

--- a/solution.py
+++ b/solution.py
@@ -90,7 +90,7 @@
     delta_blk = delta.reshape(blocked)
     block_grad = jnp.einsum(
         "cthd,cthe->chde", query_act.astype(jnp.float32), delta_f32.reshape(blocked),
-        preferred_element_type=jnp.float32, precision=lax.Precision.HIGHEST,
+        preferred_element_type=jnp.float32,
     )
     own_grad = jnp.sum(block_grad, axis=0)
     normed_out = (mixed * inv_rms[:, None, None] * out_gain).astype(jnp.bfloat16)

time: 68.4 us -> 68.2 us (level)
  no operation moved by 1% of the time
where the time goes in v18:
time: 68.2 us; the launch traced here: 67.6 us
  waiting for transfers between devices  34.6 us (51%)
  starting transfers between devices  19.3 us (28%)
  local copies, waits for them, and re-layouts  5.76 us (8%)
  matrix products  5.32 us (8%)
  other arithmetic  1.8 us (3%)
  between operations  0.87 us (1%)
    all_to_all x2, waiting for transfers between devices, exclusive_scan(): lax.all_to_all(rows.reshape(count, chunk, width), 'seq', 0, 0, tiled=True)  17.8 us
    all_to_all x2, waiting for transfers between devices, exclusive_scan(): spread = lax.all_to_all(prefix, 'seq', 0, 0, tiled=True)  15.6 us
    all_to_all x2, starting transfers between devices, exclusive_scan(): lax.all_to_all(rows.reshape(count, chunk, width), 'seq', 0, 0, tiled=True)  12 us
    all_to_all x2, starting transfers between devices, exclusive_scan(): spread = lax.all_to_all(prefix, 'seq', 0, 0, tiled=True)  7.21 us
    unnamed x19, local copies, waits for them, and re-layouts  5.76 us
    another operation x2, other arithmetic, exclusive_scan(): inclusive = lax.cumsum(gathered, axis=0, reverse=reverse)  1.51 us
  transfers between devices with their start and end apart: 5, of which 5 were waited for; matrix products, arithmetic and copies ran while one was open for 7% of the time, Pallas kernels for 0%

profile of v18, /device:TPU:0, one launch (start us, length us, event | category | flops | bytes accessed | tf_op | source)
XLA Modules:
  0.0 67.6 jit_solution(4190828408093938219)
XLA Ops:
  0.6 1.1 %copy.30 = bf16[256,4,128]{0,2,1:T(8,128)(2,1)S(1)} copy(bf16[256,4,128]{2,1,0:T(4,128)(2,1)} %param.6) | data formatting | bytes 524288 | tf_op args[1]
  1.8 1.0 %fusion.32 = f32[4,128,128]{2,1,0:T(8,128)} fusion(bf16[256,4,128]{2,1,0:T(4,128)(2,1)S(1)} %copy-done, bf16[256,4,128]{0,2,1:T(8,128)(2,1)S(1)} %copy.30), kind=kOutput, calls=%fused_computation.55 | convolution fusion | flops 34340864 | bytes 786432 | tf_op jit(solution)/shard_map/cshd,cshe->chde/dot_general | solution.py:63
  2.8 8.4 %all-to-all-start = ((f32[16,32,128]{2,1,0:T(8,128)}), f32[16,32,128]{2,1,0:T(8,128)S(1)}, u32[]{:S(2)}, u32[]{:S(2)}) async-start(f32[16,32,128]{2,1,0:T(8,128)} %bitcast.1), calls=%async_computation | async-start | bytes 524288 | tf_op jit(solution)/shard_map/all_to_all | solution.py:33
  11.4 0.8 %copy-done.2 = bf16[256,4,128]{2,1,0:T(4,128)(2,1)S(1)} copy-done((bf16[256,4,128]{2,1,0:T(4,128)(2,1)S(1)}, bf16[256,4,128]{2,1,0:T(4,128)(2,1)}, u32[]{:S(2)}) %copy-start.2) | copy-done | bytes 262168
  12.4 8.7 %all-to-all-done = f32[16,32,128]{2,1,0:T(8,128)S(1)} async-done(((f32[16,32,128]{2,1,0:T(8,128)}), f32[16,32,128]{2,1,0:T(8,128)S(1)}, u32[]{:S(2)}, u32[]{:S(2)}) %all-to-all-start) | async-done | bytes 262176 | tf_op jit(solution)/shard_map/all_to_all | solution.py:33
  21.1 0.7 %reduce-window_subtract_fusion.1 = f32[16,32,128]{2,1,0:T(8,128)} fusion(f32[16,32,128]{2,1,0:T(8,128)S(1)} %all-to-all-done), kind=kOutput, calls=%fused_computation.18 | output fusion | flops 1048576 | bytes 524288 | tf_op jit(solution)/shard_map/exclusive_scan/reduce_window_sum | solution.py:36
  21.8 3.5 %all-to-all-start.1 = ((f32[16,32,128]{2,1,0:T(8,128)}), f32[16,32,128]{2,1,0:T(8,128)S(1)}, u32[]{:S(2)}, u32[]{:S(2)}) async-start(f32[16,32,128]{2,1,0:T(8,128)} %reduce-window_subtract_fusion.1), calls=%async_computation.1 | async-start | bytes 524288 | tf_op jit(solution)/shard_map/all_to_all | solution.py:40
  25.4 0.5 fusion
  26.2 8.4 %all-to-all-done.1 = f32[16,32,128]{2,1,0:T(8,128)S(1)} async-done(((f32[16,32,128]{2,1,0:T(8,128)}), f32[16,32,128]{2,1,0:T(8,128)S(1)}, u32[]{:S(2)}, u32[]{:S(2)}) %all-to-all-start.1) | async-done | bytes 262176 | tf_op jit(solution)/shard_map/all_to_all | solution.py:40
  34.6 0.3 multiply_reduce_fusion.1
  35.1 1.1 %collective-permute-done = f32[2,256]{1,0:T(2,128)S(1)} collective-permute-done((f32[2,256]{1,0:T(2,128)S(1)}, f32[2,256]{1,0:T(2,128)S(1)}, u32[]{:S(2)}, u32[]{:S(2)}) %collective-permute-start) | collective-permute-done | bytes 2080 | tf_op jit(solution)/shard_map/ppermute | solution.py:81
  36.2 1.1 %fusion.24 = f32[4,128,128]{2,1,0:T(8,128)} fusion(f32[256,4,128]{0,2,1:T(8,128)S(1)} %get-tuple-element.22, bf16[256,4,128]{0,2,1:T(8,128)(2,1)S(1)} %copy.37, f32[256]{0:T(256)S(1)} %fusion.35, f32[256]{0:T(256)S(1)} %bitcast.64, f32[4,128]{1,0:T(4,128)S(1)} %copy-done.5, bf16[256,4,128]{0,2,1:T(8,128)(2,1)S(1)} %copy.29), kind=kOutput, calls=%fused_computation.44 | convolution fusion | flops 34996224 | bytes 1314816 | tf_op jit(solution)/shard_map/cthd,cthe->chde/dot_general | solution.py:91
  37.3 3.5 %all-to-all-start.2 = ((f32[16,32,128]{2,1,0:T(8,128)}), f32[16,32,128]{2,1,0:T(8,128)S(1)}, u32[]{:S(2)}, u32[]{:S(2)}) async-start(f32[16,32,128]{2,1,0:T(8,128)} %bitcast.12), calls=%async_computation.2 | async-start | bytes 524288 | tf_op jit(solution)/shard_map/all_to_all | solution.py:33
  41.1 0.9 %copy.45 = bf16[256,4,128]{2,1,0:T(4,128)(2,1)} copy(bf16[256,4,128]{0,2,1:T(8,128)(2,1)S(1)} %get-tuple-element.19) | data formatting | bytes 524288
  42.2 9.1 %all-to-all-done.2 = f32[16,32,128]{2,1,0:T(8,128)S(1)} async-done(((f32[16,32,128]{2,1,0:T(8,128)}), f32[16,32,128]{2,1,0:T(8,128)S(1)}, u32[]{:S(2)}, u32[]{:S(2)}) %all-to-all-start.2) | async-done | bytes 262176 | tf_op jit(solution)/shard_map/all_to_all | solution.py:33
  51.3 0.8 %reduce-window_subtract_fusion = f32[16,32,128]{2,1,0:T(8,128)} fusion(f32[16,32,128]{2,1,0:T(8,128)S(1)} %all-to-all-done.2), kind=kOutput, calls=%fused_computation.17 | output fusion | flops 1048576 | bytes 524288 | tf_op jit(solution)/shard_map/exclusive_scan/reduce_window_sum | solution.py:36
  52.1 3.7 %all-to-all-start.3 = ((f32[16,32,128]{2,1,0:T(8,128)}), f32[16,32,128]{2,1,0:T(8,128)S(1)}, u32[]{:S(2)}, u32[]{:S(2)}) async-start(f32[16,32,128]{2,1,0:T(8,128)} %reduce-window_subtract_fusion), calls=%async_computation.3 | async-start | bytes 524288 | tf_op jit(solution)/shard_map/all_to_all | solution.py:40
  55.8 0.3 fusion.1
  56.1 0.3 fusion.45
  56.8 0.9 %copy.46 = bf16[256,4,128]{2,1,0:T(4,128)(2,1)} copy(bf16[256,4,128]{0,2,1:T(8,128)(2,1)S(1)} %fusion.7) | data formatting | bytes 524288
  57.9 7.3 %all-to-all-done.3 = f32[16,32,128]{2,1,0:T(8,128)S(1)} async-done(((f32[16,32,128]{2,1,0:T(8,128)}), f32[16,32,128]{2,1,0:T(8,128)S(1)}, u32[]{:S(2)}, u32[]{:S(2)}) %all-to-all-start.3) | async-done | bytes 262176 | tf_op jit(solution)/shard_map/all_to_all | solution.py:40
  65.2 0.3 fusion.10
  65.5 0.9 %copy.48 = bf16[256,4,128]{2,1,0:T(4,128)(2,1)} copy(bf16[256,4,128]{0,2,1:T(8,128)(2,1)S(1)} %fusion.10) | data formatting | bytes 524288
  66.7 0.9 %copy.47 = bf16[256,4,128]{2,1,0:T(4,128)(2,1)} copy(bf16[256,4,128]{0,2,1:T(8,128)(2,1)S(1)} %fusion.8) | data formatting | bytes 524288
  (27 shorter events, 2.2 us)
Async XLA Ops:
  0.6 1.2 %copy-start = (bf16[256,4,128]{2,1,0:T(4,128)(2,1)S(1)}, bf16[256,4,128]{2,1,0:T(4,128)(2,1)}, u32[]{:S(2)}) copy-start(bf16[256,4,128]{2,1,0:T(4,128)(2,1)} %param.7) | copy-start | bytes 786436
  2.8 8.5 %copy-start.1 = (bf16[256,4,128]{2,1,0:T(4,128)(2,1)S(1)}, bf16[256,4,128]{2,1,0:T(4,128)(2,1)}, u32[]{:S(2)}) copy-start(bf16[256,4,128]{2,1,0:T(4,128)(2,1)} %param.5) | copy-start | bytes 786436
  2.8 18.3 %all-to-all-start = ((f32[16,32,128]{2,1,0:T(8,128)}), f32[16,32,128]{2,1,0:T(8,128)S(1)}, u32[]{:S(2)}, u32[]{:S(2)}) async-start(f32[16,32,128]{2,1,0:T(8,128)} %bitcast.1), calls=%async_computation | async-start | bytes 524288 | tf_op jit(solution)/shard_map/all_to_all | solution.py:33
  11.3 1.0 %copy-start.2 = (bf16[256,4,128]{2,1,0:T(4,128)(2,1)S(1)}, bf16[256,4,128]{2,1,0:T(4,128)(2,1)}, u32[]{:S(2)}) copy-start(bf16[256,4,128]{2,1,0:T(4,128)(2,1)} %param.9) | copy-start | bytes 786436
  12.4 13.0 %copy-start.3 = (pred[256,256]{1,0:T(8,128)(4,1)}, pred[256,256]{1,0:T(8,128)(4,1)S(1)}, u32[]{:S(2)}) copy-start(pred[256,256]{1,0:T(8,128)(4,1)S(1)} %iota_compare_fusion) | copy-start | bytes 196612
  21.8 12.8 %all-to-all-start.1 = ((f32[16,32,128]{2,1,0:T(8,128)}), f32[16,32,128]{2,1,0:T(8,128)S(1)}, u32[]{:S(2)}, u32[]{:S(2)}) async-start(f32[16,32,128]{2,1,0:T(8,128)} %reduce-window_subtract_fusion.1), calls=%async_computation.1 | async-start | bytes 524288 | tf_op jit(solution)/shard_map/all_to_all | solution.py:40
  26.2 8.4 %copy-start.5 = (f32[4,128]{1,0:T(4,128)S(1)}, f32[4,128]{1,0:T(4,128)}, u32[]{:S(2)}) copy-start(f32[4,128]{1,0:T(4,128)} %param.8) | copy-start | bytes 6148
  35.0 1.2 %collective-permute-start = (f32[2,256]{1,0:T(2,128)S(1)}, f32[2,256]{1,0:T(2,128)S(1)}, u32[]{:S(2)}, u32[]{:S(2)}) collective-permute-start(f32[2,256]{1,0:T(2,128)S(1)} %pad_maximum_fusion), channel_id=1, source_target_pairs={{0,1},{1,0},{2,3},{3,2},{4,5},{5,4},{6,7},{7,6},{8,9},{9,8},{10,11... | collective-permute-start | bytes 6152 | tf_op jit(solution)/shard_map/ppermute | solution.py:81
  37.3 14.0 %all-to-all-start.2 = ((f32[16,32,128]{2,1,0:T(8,128)}), f32[16,32,128]{2,1,0:T(8,128)S(1)}, u32[]{:S(2)}, u32[]{:S(2)}) async-start(f32[16,32,128]{2,1,0:T(8,128)} %bitcast.12), calls=%async_computation.2 | async-start | bytes 524288 | tf_op jit(solution)/shard_map/all_to_all | solution.py:33
  52.1 3.7 %copy-start.4 = (pred[256,256]{1,0:T(8,128)(4,1)S(1)}, pred[256,256]{1,0:T(8,128)(4,1)}, u32[]{:S(2)}) copy-start(pred[256,256]{1,0:T(8,128)(4,1)} %copy-done.3) | copy-start | bytes 196612
  52.1 13.1 %all-to-all-start.3 = ((f32[16,32,128]{2,1,0:T(8,128)}), f32[16,32,128]{2,1,0:T(8,128)S(1)}, u32[]{:S(2)}, u32[]{:S(2)}) async-start(f32[16,32,128]{2,1,0:T(8,128)} %reduce-window_subtract_fusion), calls=%async_computation.3 | async-start | bytes 524288 | tf_op jit(solution)/shard_map/all_to_all | solution.py:40

commit v19 on v16

--- a/solution.py
+++ b/solution.py
@@ -33,8 +33,11 @@
     gathered = lax.all_to_all(rows.reshape(count, chunk, width), "seq", 0, 0, tiled=True)
     if early is not None:
         gathered, early = lax.optimization_barrier((gathered, early))
-    inclusive = lax.cumsum(gathered, axis=0, reverse=reverse)
-    prefix = inclusive - gathered
+    inclusive = lax.cumsum(gathered, axis=0)
+    if reverse:
+        prefix = inclusive[-1:] - inclusive
+    else:
+        prefix = inclusive - gathered
     if late is not None:
         prefix, late = lax.optimization_barrier((prefix, late))
     spread = lax.all_to_all(prefix, "seq", 0, 0, tiled=True)

time: 68.1 us -> 68.8 us (1.010)
    sub x0 -> x1, other arithmetic: none -> 0.72 us  [exclusive_scan(): prefix = inclusive[-1:] - inclusive]
  transfers between devices with their start and end apart: 5 -> 5, of which waited for: 5 -> 5; matrix products, arithmetic and copies ran while one was open for 7% -> 6% of each run, Pallas kernels for 0% -> 0%
where the time goes in v19:
time: 68.8 us; the launch traced here: 68.2 us
  waiting for transfers between devices  34.8 us (51%)
  starting transfers between devices  19.1 us (28%)
  local copies, waits for them, and re-layouts  5.75 us (8%)
  matrix products  5.23 us (8%)
  other arithmetic  2.39 us (3%)
  between operations  0.86 us (1%)
    all_to_all x2, waiting for transfers between devices, exclusive_scan(): lax.all_to_all(rows.reshape(count, chunk, width), 'seq', 0, 0, tiled=True)  18 us
    all_to_all x2, waiting for transfers between devices, exclusive_scan(): spread = lax.all_to_all(prefix, 'seq', 0, 0, tiled=True)  15.6 us
    all_to_all x2, starting transfers between devices, exclusive_scan(): lax.all_to_all(rows.reshape(count, chunk, width), 'seq', 0, 0, tiled=True)  12 us
    all_to_all x2, starting transfers between devices, exclusive_scan(): spread = lax.all_to_all(prefix, 'seq', 0, 0, tiled=True)  7.08 us
    unnamed x15, local copies, waits for them, and re-layouts  5.75 us
    another operation x2, other arithmetic, exclusive_scan(): inclusive = lax.cumsum(gathered, axis=0)  1.38 us
  transfers between devices with their start and end apart: 5, of which 5 were waited for; matrix products, arithmetic and copies ran while one was open for 6% of the time, Pallas kernels for 0%

profile of v19, /device:TPU:0, one launch (start us, length us, event | category | flops | bytes accessed | tf_op | source)
XLA Modules:
  0.0 68.2 jit_solution(6225258644101304394)
XLA Ops:
  0.6 1.1 %copy.30 = bf16[256,4,128]{0,2,1:T(8,128)(2,1)S(1)} copy(bf16[256,4,128]{2,1,0:T(4,128)(2,1)} %param.6) | data formatting | bytes 524288 | tf_op args[1]
  1.8 1.0 %fusion.27 = f32[4,128,128]{2,1,0:T(8,128)} fusion(bf16[256,4,128]{2,1,0:T(4,128)(2,1)S(1)} %copy-done, bf16[256,4,128]{0,2,1:T(8,128)(2,1)S(1)} %copy.30), kind=kOutput, calls=%fused_computation.49 | convolution fusion | flops 34340864 | bytes 786432 | tf_op jit(solution)/shard_map/cshd,cshe->chde/dot_general | solution.py:66
  2.8 8.4 %all-to-all-start = ((f32[16,32,128]{2,1,0:T(8,128)}), f32[16,32,128]{2,1,0:T(8,128)S(1)}, u32[]{:S(2)}, u32[]{:S(2)}) async-start(f32[16,32,128]{2,1,0:T(8,128)} %bitcast.1), calls=%async_computation | async-start | bytes 524288 | tf_op jit(solution)/shard_map/all_to_all | solution.py:33
  11.4 0.8 %copy-done.2 = bf16[256,4,128]{2,1,0:T(4,128)(2,1)S(1)} copy-done((bf16[256,4,128]{2,1,0:T(4,128)(2,1)S(1)}, bf16[256,4,128]{2,1,0:T(4,128)(2,1)}, u32[]{:S(2)}) %copy-start.2) | copy-done | bytes 262168
  12.4 8.7 %all-to-all-done = f32[16,32,128]{2,1,0:T(8,128)S(1)} async-done(((f32[16,32,128]{2,1,0:T(8,128)}), f32[16,32,128]{2,1,0:T(8,128)S(1)}, u32[]{:S(2)}, u32[]{:S(2)}) %all-to-all-start) | async-done | bytes 262176 | tf_op jit(solution)/shard_map/all_to_all | solution.py:33
  21.1 0.7 %reduce-window_subtract_fusion = f32[16,32,128]{2,1,0:T(8,128)} fusion(f32[16,32,128]{2,1,0:T(8,128)S(1)} %all-to-all-done), kind=kOutput, calls=%fused_computation.17 | output fusion | flops 1048576 | bytes 524288 | tf_op jit(solution)/shard_map/exclusive_scan/reduce_window_sum | solution.py:36
  21.8 3.5 %all-to-all-start.1 = ((f32[16,32,128]{2,1,0:T(8,128)}), f32[16,32,128]{2,1,0:T(8,128)S(1)}, u32[]{:S(2)}, u32[]{:S(2)}) async-start(f32[16,32,128]{2,1,0:T(8,128)} %reduce-window_subtract_fusion), calls=%async_computation.1 | async-start | bytes 524288 | tf_op jit(solution)/shard_map/all_to_all | solution.py:43
  25.4 0.5 fusion
  26.2 8.4 %all-to-all-done.1 = f32[16,32,128]{2,1,0:T(8,128)S(1)} async-done(((f32[16,32,128]{2,1,0:T(8,128)}), f32[16,32,128]{2,1,0:T(8,128)S(1)}, u32[]{:S(2)}, u32[]{:S(2)}) %all-to-all-start.1) | async-done | bytes 262176 | tf_op jit(solution)/shard_map/all_to_all | solution.py:43
  34.6 0.3 multiply_reduce_fusion.1
  35.1 1.1 %collective-permute-done = f32[2,256]{1,0:T(2,128)S(1)} collective-permute-done((f32[2,256]{1,0:T(2,128)S(1)}, f32[2,256]{1,0:T(2,128)S(1)}, u32[]{:S(2)}, u32[]{:S(2)}) %collective-permute-start) | collective-permute-done | bytes 2080 | tf_op jit(solution)/shard_map/ppermute | solution.py:84
  36.4 1.0 %fusion.41 = f32[4,128,128]{2,1,0:T(8,128)} fusion(bf16[256,4,128]{0,2,1:T(8,128)(2,1)S(1)} %get-tuple-element.18, bf16[256,4,128]{0,2,1:T(8,128)(2,1)S(1)} %copy.29), kind=kOutput, calls=%fused_computation.63 | convolution fusion | flops 34340864 | bytes 786432 | tf_op jit(solution)/shard_map/cthd,cthe->chde/dot_general | solution.py:93
  37.4 3.5 %all-to-all-start.2 = ((f32[16,32,128]{2,1,0:T(8,128)}), f32[16,32,128]{2,1,0:T(8,128)S(1)}, u32[]{:S(2)}, u32[]{:S(2)}) async-start(f32[16,32,128]{2,1,0:T(8,128)} %bitcast.12), calls=%async_computation.2 | async-start | bytes 524288 | tf_op jit(solution)/shard_map/all_to_all | solution.py:33
  41.0 0.9 %copy.45 = bf16[256,4,128]{2,1,0:T(4,128)(2,1)} copy(bf16[256,4,128]{0,2,1:T(8,128)(2,1)S(1)} %get-tuple-element.19) | data formatting | bytes 524288
  42.1 9.3 %all-to-all-done.2 = f32[16,32,128]{2,1,0:T(8,128)S(1)} async-done(((f32[16,32,128]{2,1,0:T(8,128)}), f32[16,32,128]{2,1,0:T(8,128)S(1)}, u32[]{:S(2)}, u32[]{:S(2)}) %all-to-all-start.2) | async-done | bytes 262176 | tf_op jit(solution)/shard_map/all_to_all | solution.py:33
  51.4 0.7 fusion.46
  52.1 0.7 %broadcast_subtract_fusion = f32[16,32,128]{2,1,0:T(8,128)} fusion(f32[16,32,128]{2,1,0:T(8,128)S(1)} %fusion.46, f32[32,128]{1,0:T(8,128)S(1)} %slice_bitcast_fusion), kind=kLoop, calls=%fused_computation.51 | loop fusion | flops 65536 | bytes 540672 | tf_op jit(solution)/shard_map/sub | solution.py:38
  52.8 3.5 %all-to-all-start.3 = ((f32[16,32,128]{2,1,0:T(8,128)}), f32[16,32,128]{2,1,0:T(8,128)S(1)}, u32[]{:S(2)}, u32[]{:S(2)}) async-start(f32[16,32,128]{2,1,0:T(8,128)} %broadcast_subtract_fusion), calls=%async_computation.3 | async-start | bytes 524288 | tf_op jit(solution)/shard_map/all_to_all | solution.py:43
  56.3 0.3 fusion.1
  57.3 0.9 %copy.46 = bf16[256,4,128]{2,1,0:T(4,128)(2,1)} copy(bf16[256,4,128]{0,2,1:T(8,128)(2,1)S(1)} %fusion.7) | data formatting | bytes 524288
  58.5 7.3 %all-to-all-done.3 = f32[16,32,128]{2,1,0:T(8,128)S(1)} async-done(((f32[16,32,128]{2,1,0:T(8,128)}), f32[16,32,128]{2,1,0:T(8,128)S(1)}, u32[]{:S(2)}, u32[]{:S(2)}) %all-to-all-start.3) | async-done | bytes 262176 | tf_op jit(solution)/shard_map/all_to_all | solution.py:43
  65.8 0.3 fusion.10
  66.1 0.9 %copy.48 = bf16[256,4,128]{2,1,0:T(4,128)(2,1)} copy(bf16[256,4,128]{0,2,1:T(8,128)(2,1)S(1)} %fusion.10) | data formatting | bytes 524288
  67.3 0.9 %copy.47 = bf16[256,4,128]{2,1,0:T(4,128)(2,1)} copy(bf16[256,4,128]{0,2,1:T(8,128)(2,1)S(1)} %fusion.8) | data formatting | bytes 524288
  (25 shorter events, 2.5 us)
Async XLA Ops:
  0.6 1.2 %copy-start = (bf16[256,4,128]{2,1,0:T(4,128)(2,1)S(1)}, bf16[256,4,128]{2,1,0:T(4,128)(2,1)}, u32[]{:S(2)}) copy-start(bf16[256,4,128]{2,1,0:T(4,128)(2,1)} %param.7) | copy-start | bytes 786436
  2.8 8.5 %copy-start.1 = (bf16[256,4,128]{2,1,0:T(4,128)(2,1)S(1)}, bf16[256,4,128]{2,1,0:T(4,128)(2,1)}, u32[]{:S(2)}) copy-start(bf16[256,4,128]{2,1,0:T(4,128)(2,1)} %param.5) | copy-start | bytes 786436
  2.8 18.3 %all-to-all-start = ((f32[16,32,128]{2,1,0:T(8,128)}), f32[16,32,128]{2,1,0:T(8,128)S(1)}, u32[]{:S(2)}, u32[]{:S(2)}) async-start(f32[16,32,128]{2,1,0:T(8,128)} %bitcast.1), calls=%async_computation | async-start | bytes 524288 | tf_op jit(solution)/shard_map/all_to_all | solution.py:33
  11.3 1.0 %copy-start.2 = (bf16[256,4,128]{2,1,0:T(4,128)(2,1)S(1)}, bf16[256,4,128]{2,1,0:T(4,128)(2,1)}, u32[]{:S(2)}) copy-start(bf16[256,4,128]{2,1,0:T(4,128)(2,1)} %param.9) | copy-start | bytes 786436
  21.8 12.8 %all-to-all-start.1 = ((f32[16,32,128]{2,1,0:T(8,128)}), f32[16,32,128]{2,1,0:T(8,128)S(1)}, u32[]{:S(2)}, u32[]{:S(2)}) async-start(f32[16,32,128]{2,1,0:T(8,128)} %reduce-window_subtract_fusion), calls=%async_computation.1 | async-start | bytes 524288 | tf_op jit(solution)/shard_map/all_to_all | solution.py:43
  26.2 8.4 %copy-start.3 = (f32[4,128]{1,0:T(4,128)S(1)}, f32[4,128]{1,0:T(4,128)}, u32[]{:S(2)}) copy-start(f32[4,128]{1,0:T(4,128)} %param.8) | copy-start | bytes 6148
  35.0 1.2 %collective-permute-start = (f32[2,256]{1,0:T(2,128)S(1)}, f32[2,256]{1,0:T(2,128)S(1)}, u32[]{:S(2)}, u32[]{:S(2)}) collective-permute-start(f32[2,256]{1,0:T(2,128)S(1)} %pad_maximum_fusion), channel_id=1, source_target_pairs={{0,1},{1,0},{2,3},{3,2},{4,5},{5,4},{6,7},{7,6},{8,9},{9,8},{10,11... | collective-permute-start | bytes 6152 | tf_op jit(solution)/shard_map/ppermute | solution.py:84
  37.4 14.0 %all-to-all-start.2 = ((f32[16,32,128]{2,1,0:T(8,128)}), f32[16,32,128]{2,1,0:T(8,128)S(1)}, u32[]{:S(2)}, u32[]{:S(2)}) async-start(f32[16,32,128]{2,1,0:T(8,128)} %bitcast.12), calls=%async_computation.2 | async-start | bytes 524288 | tf_op jit(solution)/shard_map/all_to_all | solution.py:33
  52.8 13.0 %all-to-all-start.3 = ((f32[16,32,128]{2,1,0:T(8,128)}), f32[16,32,128]{2,1,0:T(8,128)S(1)}, u32[]{:S(2)}, u32[]{:S(2)}) async-start(f32[16,32,128]{2,1,0:T(8,128)} %broadcast_subtract_fusion), calls=%async_computation.3 | async-start | bytes 524288 | tf_op jit(solution)/shard_map/all_to_all | solution.py:43

commit v20 on v16

--- a/solution.py
+++ b/solution.py
@@ -60,7 +60,7 @@
     key_act = jax.nn.silu(key_raw.astype(jnp.float32)).astype(jnp.bfloat16).reshape(blocked)
     value_blk = value_raw.reshape(blocked)
     mask = causal_mask(GROUP)[None, None]
-    block_kv = jnp.einsum("cshd,cshe->chde", key_act, value_blk, preferred_element_type=jnp.float32)
+    block_kv = jnp.einsum("cshe,cshd->ched", value_blk, key_act, preferred_element_type=jnp.float32)
     own_total = jnp.sum(block_kv, axis=0)
     before = lower_sum(own_total)
     if blocks == 1:
@@ -71,7 +71,7 @@
     attn = jnp.where(mask, scores, 0.0).astype(jnp.bfloat16)
     mixed = jnp.einsum("chts,cshe->cthe", attn, value_blk, preferred_element_type=jnp.float32)
     mixed = mixed + jnp.einsum(
-        "cthd,chde->cthe", query_act, state_b, preferred_element_type=jnp.float32
+        "cthd,ched->cthe", query_act, state_b, preferred_element_type=jnp.float32
     )
     mixed = mixed.reshape(tok_rows, head_count, width)
     grad_in = out_grad.astype(jnp.float32) * out_gain
@@ -101,7 +101,7 @@
     bscore = jnp.where(mask, bscore, 0.0).astype(jnp.bfloat16)
     dquery = jnp.einsum("chts,cshd->cthd", bscore, key_act, preferred_element_type=jnp.float32)
     dquery = dquery + jnp.einsum(
-        "cthe,chde->cthd", delta_blk, state_b, preferred_element_type=jnp.float32
+        "cthe,ched->cthd", delta_blk, state_b, preferred_element_type=jnp.float32
     )
     dkey = jnp.einsum("chts,cthd->cshd", bscore, query_act, preferred_element_type=jnp.float32)
     dkey = dkey + jnp.einsum(

time: 68.1 us -> 68.2 us (level)
  no operation moved by 1% of the time
where the time goes in v20:
time: 68.2 us; the launch traced here: 67.6 us
  waiting for transfers between devices  34.7 us (51%)
  starting transfers between devices  19.1 us (28%)
  local copies, waits for them, and re-layouts  5.75 us (8%)
  matrix products  5.33 us (8%)
  other arithmetic  1.8 us (3%)
  between operations  0.84 us (1%)
    all_to_all x2, waiting for transfers between devices, exclusive_scan(): lax.all_to_all(rows.reshape(count, chunk, width), 'seq', 0, 0, tiled=True)  18 us
    all_to_all x2, waiting for transfers between devices, exclusive_scan(): spread = lax.all_to_all(prefix, 'seq', 0, 0, tiled=True)  15.6 us
    all_to_all x2, starting transfers between devices, exclusive_scan(): lax.all_to_all(rows.reshape(count, chunk, width), 'seq', 0, 0, tiled=True)  12 us
    all_to_all x2, starting transfers between devices, exclusive_scan(): spread = lax.all_to_all(prefix, 'seq', 0, 0, tiled=True)  7.08 us
    unnamed x15, local copies, waits for them, and re-layouts  5.75 us
    another operation x2, other arithmetic, exclusive_scan(): inclusive = lax.cumsum(gathered, axis=0, reverse=reverse)  1.51 us
  transfers between devices with their start and end apart: 5, of which 5 were waited for; matrix products, arithmetic and copies ran while one was open for 7% of the time, Pallas kernels for 0%

profile of v20, /device:TPU:0, one launch (start us, length us, event | category | flops | bytes accessed | tf_op | source)
XLA Modules:
  0.0 67.6 jit_solution(12498617513309581137)
XLA Ops:
  0.6 1.1 %copy.10 = bf16[256,4,128]{0,2,1:T(8,128)(2,1)S(1)} copy(bf16[256,4,128]{2,1,0:T(4,128)(2,1)} %param.6) | data formatting | bytes 524288 | tf_op args[1]
  1.8 1.0 %fusion.24 = f32[4,128,128]{1,2,0:T(8,128)} fusion(bf16[256,4,128]{2,1,0:T(4,128)(2,1)S(1)} %copy-done, bf16[256,4,128]{0,2,1:T(8,128)(2,1)S(1)} %copy.10), kind=kOutput, calls=%fused_computation.47 | convolution fusion | flops 34340864 | bytes 786432 | tf_op jit(solution)/shard_map/cshe,cshd->ched/dot_general | solution.py:63
  2.8 8.4 %all-to-all-start = ((f32[16,32,128]{2,1,0:T(8,128)}), f32[16,32,128]{2,1,0:T(8,128)S(1)}, u32[]{:S(2)}, u32[]{:S(2)}) async-start(f32[16,32,128]{2,1,0:T(8,128)} %bitcast.2), calls=%async_computation | async-start | bytes 524288 | tf_op jit(solution)/shard_map/all_to_all | solution.py:33
  11.5 0.8 %copy-done.2 = bf16[256,4,128]{2,1,0:T(4,128)(2,1)S(1)} copy-done((bf16[256,4,128]{2,1,0:T(4,128)(2,1)S(1)}, bf16[256,4,128]{2,1,0:T(4,128)(2,1)}, u32[]{:S(2)}) %copy-start.2) | copy-done | bytes 262168
  12.5 8.7 %all-to-all-done = f32[16,32,128]{2,1,0:T(8,128)S(1)} async-done(((f32[16,32,128]{2,1,0:T(8,128)}), f32[16,32,128]{2,1,0:T(8,128)S(1)}, u32[]{:S(2)}, u32[]{:S(2)}) %all-to-all-start) | async-done | bytes 262176 | tf_op jit(solution)/shard_map/all_to_all | solution.py:33
  21.2 0.7 %reduce-window_subtract_fusion.1 = f32[16,32,128]{2,1,0:T(8,128)} fusion(f32[16,32,128]{2,1,0:T(8,128)S(1)} %all-to-all-done), kind=kOutput, calls=%fused_computation.18 | output fusion | flops 1048576 | bytes 524288 | tf_op jit(solution)/shard_map/exclusive_scan/reduce_window_sum | solution.py:36
  21.9 3.5 %all-to-all-start.1 = ((f32[16,32,128]{2,1,0:T(8,128)}), f32[16,32,128]{2,1,0:T(8,128)S(1)}, u32[]{:S(2)}, u32[]{:S(2)}) async-start(f32[16,32,128]{2,1,0:T(8,128)} %reduce-window_subtract_fusion.1), calls=%async_computation.1 | async-start | bytes 524288 | tf_op jit(solution)/shard_map/all_to_all | solution.py:40
  25.5 0.5 fusion
  26.3 8.4 %all-to-all-done.1 = f32[16,32,128]{2,1,0:T(8,128)S(1)} async-done(((f32[16,32,128]{2,1,0:T(8,128)}), f32[16,32,128]{2,1,0:T(8,128)S(1)}, u32[]{:S(2)}, u32[]{:S(2)}) %all-to-all-start.1) | async-done | bytes 262176 | tf_op jit(solution)/shard_map/all_to_all | solution.py:40
  34.7 0.3 multiply_reduce_fusion.1
  35.1 1.1 %collective-permute-done = f32[2,256]{1,0:T(2,128)S(1)} collective-permute-done((f32[2,256]{1,0:T(2,128)S(1)}, f32[2,256]{1,0:T(2,128)S(1)}, u32[]{:S(2)}, u32[]{:S(2)}) %collective-permute-start) | collective-permute-done | bytes 2080 | tf_op jit(solution)/shard_map/ppermute | solution.py:81
  36.5 1.0 %fusion.41 = f32[4,128,128]{2,1,0:T(8,128)} fusion(bf16[256,4,128]{0,2,1:T(8,128)(2,1)S(1)} %get-tuple-element.14, bf16[256,4,128]{0,2,1:T(8,128)(2,1)S(1)} %copy.9), kind=kOutput, calls=%fused_computation.62 | convolution fusion | flops 34340864 | bytes 786432 | tf_op jit(solution)/shard_map/cthd,cthe->chde/dot_general | solution.py:90
  37.5 3.5 %all-to-all-start.2 = ((f32[16,32,128]{2,1,0:T(8,128)}), f32[16,32,128]{2,1,0:T(8,128)S(1)}, u32[]{:S(2)}, u32[]{:S(2)}) async-start(f32[16,32,128]{2,1,0:T(8,128)} %bitcast.13), calls=%async_computation.2 | async-start | bytes 524288 | tf_op jit(solution)/shard_map/all_to_all | solution.py:33
  41.0 0.9 %copy.26 = bf16[256,4,128]{2,1,0:T(4,128)(2,1)} copy(bf16[256,4,128]{0,2,1:T(8,128)(2,1)S(1)} %get-tuple-element.15) | data formatting | bytes 524288
  42.1 9.3 %all-to-all-done.2 = f32[16,32,128]{2,1,0:T(8,128)S(1)} async-done(((f32[16,32,128]{2,1,0:T(8,128)}), f32[16,32,128]{2,1,0:T(8,128)S(1)}, u32[]{:S(2)}, u32[]{:S(2)}) %all-to-all-start.2) | async-done | bytes 262176 | tf_op jit(solution)/shard_map/all_to_all | solution.py:33
  51.4 0.8 %reduce-window_subtract_fusion = f32[16,32,128]{2,1,0:T(8,128)} fusion(f32[16,32,128]{2,1,0:T(8,128)S(1)} %all-to-all-done.2), kind=kOutput, calls=%fused_computation.17 | output fusion | flops 1048576 | bytes 524288 | tf_op jit(solution)/shard_map/exclusive_scan/reduce_window_sum | solution.py:36
  52.2 3.5 %all-to-all-start.3 = ((f32[16,32,128]{2,1,0:T(8,128)}), f32[16,32,128]{2,1,0:T(8,128)S(1)}, u32[]{:S(2)}, u32[]{:S(2)}) async-start(f32[16,32,128]{2,1,0:T(8,128)} %reduce-window_subtract_fusion), calls=%async_computation.3 | async-start | bytes 524288 | tf_op jit(solution)/shard_map/all_to_all | solution.py:40
  55.8 0.3 fusion.1
  56.4 0.4 fusion.7
  56.8 0.9 %copy.27 = bf16[256,4,128]{2,1,0:T(4,128)(2,1)} copy(bf16[256,4,128]{0,2,1:T(8,128)(2,1)S(1)} %fusion.7) | data formatting | bytes 524288
  58.0 7.2 %all-to-all-done.3 = f32[16,32,128]{2,1,0:T(8,128)S(1)} async-done(((f32[16,32,128]{2,1,0:T(8,128)}), f32[16,32,128]{2,1,0:T(8,128)S(1)}, u32[]{:S(2)}, u32[]{:S(2)}) %all-to-all-start.3) | async-done | bytes 262176 | tf_op jit(solution)/shard_map/all_to_all | solution.py:40
  65.2 0.3 fusion.10
  65.5 0.9 %copy.29 = bf16[256,4,128]{2,1,0:T(4,128)(2,1)} copy(bf16[256,4,128]{0,2,1:T(8,128)(2,1)S(1)} %fusion.10) | data formatting | bytes 524288
  66.7 0.9 %copy.28 = bf16[256,4,128]{2,1,0:T(4,128)(2,1)} copy(bf16[256,4,128]{0,2,1:T(8,128)(2,1)S(1)} %fusion.8) | data formatting | bytes 524288
  (23 shorter events, 2.2 us)
Async XLA Ops:
  0.6 1.2 %copy-start = (bf16[256,4,128]{2,1,0:T(4,128)(2,1)S(1)}, bf16[256,4,128]{2,1,0:T(4,128)(2,1)}, u32[]{:S(2)}) copy-start(bf16[256,4,128]{2,1,0:T(4,128)(2,1)} %param.7) | copy-start | bytes 786436
  2.8 8.5 %copy-start.1 = (bf16[256,4,128]{2,1,0:T(4,128)(2,1)S(1)}, bf16[256,4,128]{2,1,0:T(4,128)(2,1)}, u32[]{:S(2)}) copy-start(bf16[256,4,128]{2,1,0:T(4,128)(2,1)} %param.5) | copy-start | bytes 786436
  2.8 18.3 %all-to-all-start = ((f32[16,32,128]{2,1,0:T(8,128)}), f32[16,32,128]{2,1,0:T(8,128)S(1)}, u32[]{:S(2)}, u32[]{:S(2)}) async-start(f32[16,32,128]{2,1,0:T(8,128)} %bitcast.2), calls=%async_computation | async-start | bytes 524288 | tf_op jit(solution)/shard_map/all_to_all | solution.py:33
  11.3 1.0 %copy-start.2 = (bf16[256,4,128]{2,1,0:T(4,128)(2,1)S(1)}, bf16[256,4,128]{2,1,0:T(4,128)(2,1)}, u32[]{:S(2)}) copy-start(bf16[256,4,128]{2,1,0:T(4,128)(2,1)} %param.9) | copy-start | bytes 786436
  21.9 12.8 %all-to-all-start.1 = ((f32[16,32,128]{2,1,0:T(8,128)}), f32[16,32,128]{2,1,0:T(8,128)S(1)}, u32[]{:S(2)}, u32[]{:S(2)}) async-start(f32[16,32,128]{2,1,0:T(8,128)} %reduce-window_subtract_fusion.1), calls=%async_computation.1 | async-start | bytes 524288 | tf_op jit(solution)/shard_map/all_to_all | solution.py:40
  26.3 8.4 %copy-start.3 = (f32[4,128]{1,0:T(4,128)S(1)}, f32[4,128]{1,0:T(4,128)}, u32[]{:S(2)}) copy-start(f32[4,128]{1,0:T(4,128)} %param.8) | copy-start | bytes 6148
  35.0 1.2 %collective-permute-start = (f32[2,256]{1,0:T(2,128)S(1)}, f32[2,256]{1,0:T(2,128)S(1)}, u32[]{:S(2)}, u32[]{:S(2)}) collective-permute-start(f32[2,256]{1,0:T(2,128)S(1)} %pad_maximum_fusion), channel_id=1, source_target_pairs={{0,1},{1,0},{2,3},{3,2},{4,5},{5,4},{6,7},{7,6},{8,9},{9,8},{10,11... | collective-permute-start | bytes 6152 | tf_op jit(solution)/shard_map/ppermute | solution.py:81
  37.5 14.0 %all-to-all-start.2 = ((f32[16,32,128]{2,1,0:T(8,128)}), f32[16,32,128]{2,1,0:T(8,128)S(1)}, u32[]{:S(2)}, u32[]{:S(2)}) async-start(f32[16,32,128]{2,1,0:T(8,128)} %bitcast.13), calls=%async_computation.2 | async-start | bytes 524288 | tf_op jit(solution)/shard_map/all_to_all | solution.py:33
  52.2 13.0 %all-to-all-start.3 = ((f32[16,32,128]{2,1,0:T(8,128)}), f32[16,32,128]{2,1,0:T(8,128)S(1)}, u32[]{:S(2)}, u32[]{:S(2)}) async-start(f32[16,32,128]{2,1,0:T(8,128)} %reduce-window_subtract_fusion), calls=%async_computation.3 | async-start | bytes 524288 | tf_op jit(solution)/shard_map/all_to_all | solution.py:40

commit v21 on v18

--- a/solution.py
+++ b/solution.py
@@ -60,7 +60,7 @@
     key_act = jax.nn.silu(key_raw.astype(jnp.float32)).astype(jnp.bfloat16).reshape(blocked)
     value_blk = value_raw.reshape(blocked)
     mask = causal_mask(GROUP)[None, None]
-    block_kv = jnp.einsum("cshd,cshe->chde", key_act, value_blk, preferred_element_type=jnp.float32)
+    block_kv = jnp.einsum("cshe,cshd->ched", value_blk, key_act, preferred_element_type=jnp.float32)
     own_total = jnp.sum(block_kv, axis=0)
     before = lower_sum(own_total)
     if blocks == 1:
@@ -71,7 +71,7 @@
     attn = jnp.where(mask, scores, 0.0).astype(jnp.bfloat16)
     mixed = jnp.einsum("chts,cshe->cthe", attn, value_blk, preferred_element_type=jnp.float32)
     mixed = mixed + jnp.einsum(
-        "cthd,chde->cthe", query_act, state_b, preferred_element_type=jnp.float32
+        "cthd,ched->cthe", query_act, state_b, preferred_element_type=jnp.float32
     )
     mixed = mixed.reshape(tok_rows, head_count, width)
     grad_in = out_grad.astype(jnp.float32) * out_gain
@@ -103,7 +103,7 @@
     bscore = jnp.where(mask, bscore, 0.0).astype(jnp.bfloat16)
     dquery = jnp.einsum("chts,cshd->cthd", bscore, key_act, preferred_element_type=jnp.float32)
     dquery = dquery + jnp.einsum(
-        "cthe,chde->cthd", delta_blk, state_b, preferred_element_type=jnp.float32
+        "cthe,ched->cthd", delta_blk, state_b, preferred_element_type=jnp.float32
     )
     dkey = jnp.einsum("chts,cthd->cshd", bscore, query_act, preferred_element_type=jnp.float32)
     dkey = dkey + jnp.einsum(

time: 68.2 us -> 68.3 us (level)
  no operation moved by 1% of the time
where the time goes in v21:
time: 68.3 us; the launch traced here: 67.6 us
  waiting for transfers between devices  34.5 us (51%)
  starting transfers between devices  19.3 us (28%)
  local copies, waits for them, and re-layouts  5.76 us (8%)
  matrix products  5.43 us (8%)
  other arithmetic  1.8 us (3%)
  between operations  0.86 us (1%)
    all_to_all x2, waiting for transfers between devices, exclusive_scan(): lax.all_to_all(rows.reshape(count, chunk, width), 'seq', 0, 0, tiled=True)  17.8 us
    all_to_all x2, waiting for transfers between devices, exclusive_scan(): spread = lax.all_to_all(prefix, 'seq', 0, 0, tiled=True)  15.6 us
    all_to_all x2, starting transfers between devices, exclusive_scan(): lax.all_to_all(rows.reshape(count, chunk, width), 'seq', 0, 0, tiled=True)  12 us
    all_to_all x2, starting transfers between devices, exclusive_scan(): spread = lax.all_to_all(prefix, 'seq', 0, 0, tiled=True)  7.21 us
    unnamed x19, local copies, waits for them, and re-layouts  5.76 us
    another operation x2, other arithmetic, exclusive_scan(): inclusive = lax.cumsum(gathered, axis=0, reverse=reverse)  1.51 us
  transfers between devices with their start and end apart: 5, of which 5 were waited for; matrix products, arithmetic and copies ran while one was open for 7% of the time, Pallas kernels for 0%

profile of v21, /device:TPU:0, one launch (start us, length us, event | category | flops | bytes accessed | tf_op | source)
XLA Modules:
  0.0 67.6 jit_solution(5754563372534074897)
XLA Ops:
  0.6 1.1 %copy.10 = bf16[256,4,128]{0,2,1:T(8,128)(2,1)S(1)} copy(bf16[256,4,128]{2,1,0:T(4,128)(2,1)} %param.6) | data formatting | bytes 524288 | tf_op args[1]
  1.8 1.0 %fusion.29 = f32[4,128,128]{1,2,0:T(8,128)} fusion(bf16[256,4,128]{2,1,0:T(4,128)(2,1)S(1)} %copy-done, bf16[256,4,128]{0,2,1:T(8,128)(2,1)S(1)} %copy.10), kind=kOutput, calls=%fused_computation.52 | convolution fusion | flops 34340864 | bytes 786432 | tf_op jit(solution)/shard_map/cshe,cshd->ched/dot_general | solution.py:63
  2.8 8.4 %all-to-all-start = ((f32[16,32,128]{2,1,0:T(8,128)}), f32[16,32,128]{2,1,0:T(8,128)S(1)}, u32[]{:S(2)}, u32[]{:S(2)}) async-start(f32[16,32,128]{2,1,0:T(8,128)} %bitcast.2), calls=%async_computation | async-start | bytes 524288 | tf_op jit(solution)/shard_map/all_to_all | solution.py:33
  11.5 0.8 %copy-done.2 = bf16[256,4,128]{2,1,0:T(4,128)(2,1)S(1)} copy-done((bf16[256,4,128]{2,1,0:T(4,128)(2,1)S(1)}, bf16[256,4,128]{2,1,0:T(4,128)(2,1)}, u32[]{:S(2)}) %copy-start.2) | copy-done | bytes 262168
  12.5 8.7 %all-to-all-done = f32[16,32,128]{2,1,0:T(8,128)S(1)} async-done(((f32[16,32,128]{2,1,0:T(8,128)}), f32[16,32,128]{2,1,0:T(8,128)S(1)}, u32[]{:S(2)}, u32[]{:S(2)}) %all-to-all-start) | async-done | bytes 262176 | tf_op jit(solution)/shard_map/all_to_all | solution.py:33
  21.2 0.7 %reduce-window_subtract_fusion.1 = f32[16,32,128]{2,1,0:T(8,128)} fusion(f32[16,32,128]{2,1,0:T(8,128)S(1)} %all-to-all-done), kind=kOutput, calls=%fused_computation.18 | output fusion | flops 1048576 | bytes 524288 | tf_op jit(solution)/shard_map/exclusive_scan/reduce_window_sum | solution.py:36
  21.9 3.5 %all-to-all-start.1 = ((f32[16,32,128]{2,1,0:T(8,128)}), f32[16,32,128]{2,1,0:T(8,128)S(1)}, u32[]{:S(2)}, u32[]{:S(2)}) async-start(f32[16,32,128]{2,1,0:T(8,128)} %reduce-window_subtract_fusion.1), calls=%async_computation.1 | async-start | bytes 524288 | tf_op jit(solution)/shard_map/all_to_all | solution.py:40
  25.5 0.5 fusion
  26.3 8.4 %all-to-all-done.1 = f32[16,32,128]{2,1,0:T(8,128)S(1)} async-done(((f32[16,32,128]{2,1,0:T(8,128)}), f32[16,32,128]{2,1,0:T(8,128)S(1)}, u32[]{:S(2)}, u32[]{:S(2)}) %all-to-all-start.1) | async-done | bytes 262176 | tf_op jit(solution)/shard_map/all_to_all | solution.py:40
  34.7 0.3 multiply_reduce_fusion.1
  35.1 1.1 %collective-permute-done = f32[2,256]{1,0:T(2,128)S(1)} collective-permute-done((f32[2,256]{1,0:T(2,128)S(1)}, f32[2,256]{1,0:T(2,128)S(1)}, u32[]{:S(2)}, u32[]{:S(2)}) %collective-permute-start) | collective-permute-done | bytes 2080 | tf_op jit(solution)/shard_map/ppermute | solution.py:81
  36.3 1.1 %fusion.24 = f32[4,128,128]{2,1,0:T(8,128)} fusion(f32[256,4,128]{0,2,1:T(8,128)S(1)} %get-tuple-element.18, bf16[256,4,128]{0,2,1:T(8,128)(2,1)S(1)} %copy.17, f32[256]{0:T(256)S(1)} %fusion.35, f32[256]{0:T(256)S(1)} %bitcast.66, f32[4,128]{1,0:T(4,128)S(1)} %copy-done.5, bf16[256,4,128]{0,2,1:T(8,128)(2,1)S(1)} %copy.9), kind=kOutput, calls=%fused_computation.44 | convolution fusion | flops 34996224 | bytes 1314816 | tf_op jit(solution)/shard_map/cthd,cthe->chde/dot_general | solution.py:91
  37.4 3.5 %all-to-all-start.2 = ((f32[16,32,128]{2,1,0:T(8,128)}), f32[16,32,128]{2,1,0:T(8,128)S(1)}, u32[]{:S(2)}, u32[]{:S(2)}) async-start(f32[16,32,128]{2,1,0:T(8,128)} %bitcast.13), calls=%async_computation.2 | async-start | bytes 524288 | tf_op jit(solution)/shard_map/all_to_all | solution.py:33
  41.1 0.9 %copy.26 = bf16[256,4,128]{2,1,0:T(4,128)(2,1)} copy(bf16[256,4,128]{0,2,1:T(8,128)(2,1)S(1)} %get-tuple-element.15) | data formatting | bytes 524288
  42.2 9.1 %all-to-all-done.2 = f32[16,32,128]{2,1,0:T(8,128)S(1)} async-done(((f32[16,32,128]{2,1,0:T(8,128)}), f32[16,32,128]{2,1,0:T(8,128)S(1)}, u32[]{:S(2)}, u32[]{:S(2)}) %all-to-all-start.2) | async-done | bytes 262176 | tf_op jit(solution)/shard_map/all_to_all | solution.py:33
  51.4 0.8 %reduce-window_subtract_fusion = f32[16,32,128]{2,1,0:T(8,128)} fusion(f32[16,32,128]{2,1,0:T(8,128)S(1)} %all-to-all-done.2), kind=kOutput, calls=%fused_computation.17 | output fusion | flops 1048576 | bytes 524288 | tf_op jit(solution)/shard_map/exclusive_scan/reduce_window_sum | solution.py:36
  52.1 3.7 %all-to-all-start.3 = ((f32[16,32,128]{2,1,0:T(8,128)}), f32[16,32,128]{2,1,0:T(8,128)S(1)}, u32[]{:S(2)}, u32[]{:S(2)}) async-start(f32[16,32,128]{2,1,0:T(8,128)} %reduce-window_subtract_fusion), calls=%async_computation.3 | async-start | bytes 524288 | tf_op jit(solution)/shard_map/all_to_all | solution.py:40
  55.8 0.3 fusion.1
  56.5 0.4 fusion.7
  56.9 0.9 %copy.27 = bf16[256,4,128]{2,1,0:T(4,128)(2,1)} copy(bf16[256,4,128]{0,2,1:T(8,128)(2,1)S(1)} %fusion.7) | data formatting | bytes 524288
  58.0 7.2 %all-to-all-done.3 = f32[16,32,128]{2,1,0:T(8,128)S(1)} async-done(((f32[16,32,128]{2,1,0:T(8,128)}), f32[16,32,128]{2,1,0:T(8,128)S(1)}, u32[]{:S(2)}, u32[]{:S(2)}) %all-to-all-start.3) | async-done | bytes 262176 | tf_op jit(solution)/shard_map/all_to_all | solution.py:40
  65.3 0.3 fusion.10
  65.6 0.9 %copy.29 = bf16[256,4,128]{2,1,0:T(4,128)(2,1)} copy(bf16[256,4,128]{0,2,1:T(8,128)(2,1)S(1)} %fusion.10) | data formatting | bytes 524288
  66.8 0.9 %copy.28 = bf16[256,4,128]{2,1,0:T(4,128)(2,1)} copy(bf16[256,4,128]{0,2,1:T(8,128)(2,1)S(1)} %fusion.8) | data formatting | bytes 524288
  (27 shorter events, 2.2 us)
Async XLA Ops:
  0.6 1.2 %copy-start = (bf16[256,4,128]{2,1,0:T(4,128)(2,1)S(1)}, bf16[256,4,128]{2,1,0:T(4,128)(2,1)}, u32[]{:S(2)}) copy-start(bf16[256,4,128]{2,1,0:T(4,128)(2,1)} %param.7) | copy-start | bytes 786436
  2.8 8.5 %copy-start.1 = (bf16[256,4,128]{2,1,0:T(4,128)(2,1)S(1)}, bf16[256,4,128]{2,1,0:T(4,128)(2,1)}, u32[]{:S(2)}) copy-start(bf16[256,4,128]{2,1,0:T(4,128)(2,1)} %param.5) | copy-start | bytes 786436
  2.8 18.3 %all-to-all-start = ((f32[16,32,128]{2,1,0:T(8,128)}), f32[16,32,128]{2,1,0:T(8,128)S(1)}, u32[]{:S(2)}, u32[]{:S(2)}) async-start(f32[16,32,128]{2,1,0:T(8,128)} %bitcast.2), calls=%async_computation | async-start | bytes 524288 | tf_op jit(solution)/shard_map/all_to_all | solution.py:33
  11.3 1.0 %copy-start.2 = (bf16[256,4,128]{2,1,0:T(4,128)(2,1)S(1)}, bf16[256,4,128]{2,1,0:T(4,128)(2,1)}, u32[]{:S(2)}) copy-start(bf16[256,4,128]{2,1,0:T(4,128)(2,1)} %param.9) | copy-start | bytes 786436
  12.5 13.0 %copy-start.3 = (pred[256,256]{1,0:T(8,128)(4,1)}, pred[256,256]{1,0:T(8,128)(4,1)S(1)}, u32[]{:S(2)}) copy-start(pred[256,256]{1,0:T(8,128)(4,1)S(1)} %iota_compare_fusion) | copy-start | bytes 196612
  21.9 12.8 %all-to-all-start.1 = ((f32[16,32,128]{2,1,0:T(8,128)}), f32[16,32,128]{2,1,0:T(8,128)S(1)}, u32[]{:S(2)}, u32[]{:S(2)}) async-start(f32[16,32,128]{2,1,0:T(8,128)} %reduce-window_subtract_fusion.1), calls=%async_computation.1 | async-start | bytes 524288 | tf_op jit(solution)/shard_map/all_to_all | solution.py:40
  26.3 8.4 %copy-start.5 = (f32[4,128]{1,0:T(4,128)S(1)}, f32[4,128]{1,0:T(4,128)}, u32[]{:S(2)}) copy-start(f32[4,128]{1,0:T(4,128)} %param.8) | copy-start | bytes 6148
  35.0 1.2 %collective-permute-start = (f32[2,256]{1,0:T(2,128)S(1)}, f32[2,256]{1,0:T(2,128)S(1)}, u32[]{:S(2)}, u32[]{:S(2)}) collective-permute-start(f32[2,256]{1,0:T(2,128)S(1)} %pad_maximum_fusion), channel_id=1, source_target_pairs={{0,1},{1,0},{2,3},{3,2},{4,5},{5,4},{6,7},{7,6},{8,9},{9,8},{10,11... | collective-permute-start | bytes 6152 | tf_op jit(solution)/shard_map/ppermute | solution.py:81
  37.4 14.0 %all-to-all-start.2 = ((f32[16,32,128]{2,1,0:T(8,128)}), f32[16,32,128]{2,1,0:T(8,128)S(1)}, u32[]{:S(2)}, u32[]{:S(2)}) async-start(f32[16,32,128]{2,1,0:T(8,128)} %bitcast.13), calls=%async_computation.2 | async-start | bytes 524288 | tf_op jit(solution)/shard_map/all_to_all | solution.py:33
  52.1 3.7 %copy-start.4 = (pred[256,256]{1,0:T(8,128)(4,1)S(1)}, pred[256,256]{1,0:T(8,128)(4,1)}, u32[]{:S(2)}) copy-start(pred[256,256]{1,0:T(8,128)(4,1)} %copy-done.3) | copy-start | bytes 196612
  52.1 13.1 %all-to-all-start.3 = ((f32[16,32,128]{2,1,0:T(8,128)}), f32[16,32,128]{2,1,0:T(8,128)S(1)}, u32[]{:S(2)}, u32[]{:S(2)}) async-start(f32[16,32,128]{2,1,0:T(8,128)} %reduce-window_subtract_fusion), calls=%async_computation.3 | async-start | bytes 524288 | tf_op jit(solution)/shard_map/all_to_all | solution.py:40
